TPU v7x, 256 devices: a whole 4x4x8 slice. The times are simulated.
256 devices in a mesh: req: 32 (over z, x), head: 4 (over y), blk: 2 (over core).
Axes of the slice: x: 4, y: 4, z: 8, core: 2. Of those that a mesh axis runs over, the one named last changes fastest.
Arguments:
- x_tokens: bfloat16 [32, 512, 1024], P('req', ('head', 'blk')), may hold values from -40 to 40
- query: bfloat16 [32, 512, 1024], P('req', None, ('head', 'blk')), may hold values from -200 to 200
- key_new: bfloat16 [32, 512, 1024], P('req', None, ('head', 'blk')), may hold values from -4 to 4
- value_new: bfloat16 [32, 512, 1024], P('req', None, ('head', 'blk')), may hold values from -4 to 4
- cache_keys: bfloat16 [32, 2048, 1024], P('req', None, ('head', 'blk')), may hold values from -4 to 4
- cache_values: bfloat16 [32, 2048, 1024], P('req', None, ('head', 'blk')), may hold values from -4 to 4
- prefix_keys: bfloat16 [4, 512, 1024], P(None, None, ('head', 'blk')), may hold values from -4 to 4
- prefix_values: bfloat16 [4, 512, 1024], P(None, None, ('head', 'blk')), may hold values from -4 to 4
- history_len: int32 [32], P('req'), may hold values from 512 to 2048, as said below
- group_ids: int32 [32], P('req'), may hold values from 0 to 3
- out_weight: bfloat16 [1024, 1024], P(('head', 'blk')), may hold values from -0.1875 to 0.1875
- norm_gain: float32 [1024], replicated, may hold values from 0.5 to 1.5
- router_weight: bfloat16 [1024, 16], replicated, may hold values from -0.1875 to 0.1875
- expert_gate: bfloat16 [1024, 45056], P(None, ('req', 'head')), may hold values from -0.1875 to 0.1875
- expert_up: bfloat16 [1024, 45056], P(None, ('req', 'head')), may hold values from -0.1875 to 0.1875
- expert_down: bfloat16 [45056, 1024], P(('req', 'head')), may hold values from -0.109375 to 0.109375
- expert_ids: int32 [32, 512, 2], P('req', ('head', 'blk')), may hold values from 0 to 15, all different within a row; in each aligned block of 64 rows (0 to 63, 64 to 127, ..., all dimensions but the last counted through in order) at most 16 rows name the same one
- keep_mask: int32 [32, 512, 2], P('req', ('head', 'blk')), may hold values 0 or 1
Outputs:
- y_out: bfloat16 [32, 512, 1024], P('req', ('head', 'blk'))
- new_keys: bfloat16 [32, 2560, 1024], P('req', ('head', 'blk'))
- new_values: bfloat16 [32, 2560, 1024], P('req', ('head', 'blk'))
Inputs may be any that keep to these rules, and one draw needn't show every extreme that they name: `history_len`: one request has exactly 2048 used slots. `expert_ids`: the two experts of a token differ; within each aligned block of 64 tokens (one request, positions b * 64 onward) no expert is named by more than 16 choices, dropped ones included.
All inputs are finite; a program needn't handle non-finite values. No bound on the sum of `keep_mask` on one device may be relied on, other than what follows from the above.
Results may differ from a plain program's by a relative error of at most 0.0036.
Values may be sent and summed in bfloat16 or wider, within the bound.
No kernel may reach another device: no remote copies, remote signals or barrier semaphores. Data moves between devices by JAX's collectives and lax.ppermute only.
A program may use at most 64 MiB of HBM per device.

v0:
```python
import jax
import jax.numpy as jnp
from jax import lax
from jax.sharding import PartitionSpec as P

HD = 64
SLOT = 16


EPSILON = 1e-06


def attend_request(operands):
    (
        queries,
        keys_stretch,
        values_stretch,
        keys_cache,
        values_cache,
        keys_prefix,
        values_prefix,
        length,
    ) = operands
    heads_here = queries.shape[1] // HD
    prefix_rows = keys_prefix.shape[0]
    history_rows = keys_cache.shape[0]
    stretch_rows = queries.shape[0]
    keys_all = jnp.concatenate([keys_prefix, keys_cache, keys_stretch], 0).reshape(
        -1, heads_here, HD
    )
    values_all = jnp.concatenate([values_prefix, values_cache, values_stretch], 0).reshape(
        -1, heads_here, HD
    )
    key_pos = jnp.arange(keys_all.shape[0])
    query_pos = jnp.arange(stretch_rows)
    in_prefix = key_pos < prefix_rows
    in_history = (
        (key_pos >= prefix_rows)
        & (key_pos < prefix_rows + history_rows)
        & (key_pos - prefix_rows < length)
    )
    in_stretch = (key_pos[None, :] >= prefix_rows + history_rows) & (
        key_pos[None, :] - prefix_rows - history_rows <= query_pos[:, None]
    )
    visible = (in_prefix | in_history)[None, :] | in_stretch
    scores = jnp.einsum(
        "qhd,khd->hqk",
        queries.reshape(stretch_rows, heads_here, HD),
        keys_all,
        preferred_element_type=jnp.float32,
    ) * HD ** (-0.5)
    highest = jnp.max(jnp.where(visible[None], scores, -jnp.inf), axis=-1, keepdims=True)
    weights = jnp.where(visible[None], jnp.exp(scores - highest), 0.0)
    total = jnp.sum(weights, axis=-1, keepdims=True)
    rounded = weights.astype(jnp.bfloat16)
    mixed = jnp.einsum(
        "hqk,khd->qhd", rounded, values_all, preferred_element_type=jnp.float32
    ) / jnp.transpose(total, (1, 0, 2))
    return mixed.reshape(stretch_rows, -1).astype(jnp.bfloat16)


def extend(cache, stretch, length):
    hist = cache.shape[0]
    rows = stretch.shape[0]
    width = cache.shape[1]
    span = jnp.arange(hist + rows)
    padded_cache = jnp.concatenate([cache, jnp.zeros((rows, width), cache.dtype)], 0)
    framed = jnp.concatenate(
        [jnp.zeros((hist, width), stretch.dtype), stretch, jnp.zeros((hist, width), stretch.dtype)], 0
    )
    shifted = lax.dynamic_slice(framed, (hist - length, jnp.int32(0)), (hist + rows, width))
    return jnp.where((span < length)[:, None], padded_cache, shifted)


def to_positions(grown):
    groups = lax.axis_size(("head", "blk"))
    lead, rows, width = grown.shape
    parts = grown.reshape(lead, groups, rows // groups, width)
    got = lax.all_to_all(parts, ("head", "blk"), split_axis=1, concat_axis=1, tiled=True)
    return jnp.transpose(got, (0, 2, 1, 3)).reshape(lead, rows // groups, groups * width)


def body(
    x_tokens,
    query,
    key_new,
    value_new,
    cache_keys,
    cache_values,
    prefix_keys,
    prefix_values,
    history_len,
    group_ids,
    out_weight,
    norm_gain,
    router_weight,
    expert_gate,
    expert_up,
    expert_down,
    expert_ids,
    keep_mask,
):
    grown_keys = jax.vmap(extend)(cache_keys, key_new, history_len)
    grown_values = jax.vmap(extend)(cache_values, value_new, history_len)
    new_keys = to_positions(grown_keys)
    new_values = to_positions(grown_values)
    chosen_keys = jnp.take(prefix_keys, group_ids, axis=0)
    chosen_values = jnp.take(prefix_values, group_ids, axis=0)
    attended = lax.map(
        attend_request,
        (
            query,
            key_new,
            value_new,
            cache_keys,
            cache_values,
            chosen_keys,
            chosen_values,
            history_len,
        ),
    )
    requests_here = x_tokens.shape[0]
    rows_here = x_tokens.shape[1]
    width = x_tokens.shape[2]
    full_weight = lax.all_gather(out_weight, ("head", "blk"), axis=0, tiled=True)
    by_token = lax.all_to_all(attended, ("head", "blk"), split_axis=1, concat_axis=2, tiled=True)
    projected = jnp.einsum(
        "rqf,fd->rqd", by_token, full_weight, preferred_element_type=jnp.float32
    )
    resid = x_tokens.astype(jnp.float32) + projected
    mean_square = jnp.mean(resid * resid, axis=-1, keepdims=True)
    normed = (resid * lax.rsqrt(mean_square + EPSILON) * norm_gain).astype(jnp.bfloat16)
    logits = jnp.dot(normed.reshape(-1, width), router_weight, preferred_element_type=jnp.float32)
    picks = expert_ids.reshape(-1, 2)
    chosen = jnp.take_along_axis(logits, picks, axis=1)
    keep = keep_mask.reshape(-1, 2)
    gate_weights = jax.nn.sigmoid(chosen - chosen[:, ::-1]) * keep.astype(jnp.float32)
    experts = router_weight.shape[1]
    slots_here = requests_here * SLOT
    block_picks = expert_ids.reshape(requests_here, rows_here * 2)
    onehot = (block_picks[:, :, None] == jnp.arange(experts)[None, None, :]).astype(jnp.int32)
    ranks = jnp.sum((jnp.cumsum(onehot, axis=1) - 1) * onehot, axis=-1)
    places = (block_picks * slots_here + jnp.arange(requests_here)[:, None] * SLOT + ranks).reshape(
        -1
    )
    sent_rows = (normed[:, :, None, :] * keep_mask[:, :, :, None].astype(jnp.bfloat16)).reshape(
        -1, width
    )
    buffer = jnp.zeros((experts * slots_here, width), jnp.bfloat16).at[places].set(sent_rows)
    holders = lax.axis_size("req") // experts
    outgoing = jnp.repeat(buffer.reshape(experts, slots_here, width), holders, axis=0)
    arrived = lax.all_to_all(outgoing, "req", split_axis=0, concat_axis=0, tiled=True)
    gathered = lax.all_gather(arrived, "head", axis=0, tiled=False)
    flat_rows = gathered.reshape(-1, width)
    gate_val = jnp.dot(flat_rows, expert_gate, preferred_element_type=jnp.float32)
    up_val = jnp.dot(flat_rows, expert_up, preferred_element_type=jnp.float32)
    hidden = (jax.nn.gelu(gate_val, approximate=True) * up_val).astype(jnp.bfloat16)
    partial = (
        jnp.dot(hidden, expert_down, preferred_element_type=jnp.float32)
        .astype(jnp.bfloat16)
        .reshape(gathered.shape)
    )
    shard_parts = lax.all_to_all(partial, "head", split_axis=0, concat_axis=0, tiled=True)
    half_sum = jnp.sum(shard_parts.astype(jnp.float32), axis=0).astype(jnp.bfloat16)
    returned = lax.all_to_all(half_sum, "req", split_axis=0, concat_axis=0, tiled=True)
    combined = jnp.sum(
        returned.reshape(experts, holders, slots_here, width), axis=1, dtype=jnp.float32
    ).reshape(experts * slots_here, width)
    picked = jnp.take(combined, places, axis=0).reshape(-1, 2, width)
    mixture = jnp.sum(picked * gate_weights[:, :, None], axis=1)
    y_out = (
        (resid.reshape(-1, width) + mixture)
        .astype(jnp.bfloat16)
        .reshape(requests_here, rows_here, width)
    )
    return (y_out, new_keys, new_values)


def solution(mesh):
    return jax.shard_map(
        body,
        mesh=mesh,
        in_specs=(
            P("req", ("head", "blk"), None),
            P("req", None, ("head", "blk")),
            P("req", None, ("head", "blk")),
            P("req", None, ("head", "blk")),
            P("req", None, ("head", "blk")),
            P("req", None, ("head", "blk")),
            P(None, None, ("head", "blk")),
            P(None, None, ("head", "blk")),
            P("req"),
            P("req"),
            P(("head", "blk"), None),
            P(),
            P(),
            P(None, ("req", "head")),
            P(None, ("req", "head")),
            P(("req", "head"), None),
            P("req", ("head", "blk"), None),
            P("req", ("head", "blk"), None),
        ),
        out_specs=(
            P("req", ("head", "blk"), None),
            P("req", ("head", "blk"), None),
            P("req", ("head", "blk"), None),
        ),
        check_vma=False,
    )
```

profile of v0, /device:TPU:4, one launch (start us, length us, event | category | flops | bytes accessed | tf_op | source)
XLA Modules:
  0.0 273.6 jit_solution(18118193608281846395)
XLA Ops:
  8.6 1.0 dynamic-slice_select_fusion
  10.4 1.2 copy.101
  11.6 1.0 copy.102
  12.6 1.0 copy.103
  14.2 4.3 %fusion.10 = pred[512,3072]{0,1:T(8,128)(4,1)} fusion(s32[3072]{0:T(1024)S(1)} %iota_add_fusion, pred[3072]{0:T(1024)(128)(4,1)S(1)} %get-tuple-element.73, pred[3072]{0:T(1024)(128)(4,1)S(1)} %get-tuple-element.74), kind=kLoop, calls=%fused_computation.16 | loop fusion | flops 4718592 | bytes 1591296 | tf_op jit(solution)/shard_map/while/body/eval_jaxpr/or | solution.py:45
  18.5 9.0 %fusion.72 = (f32[2,512]{1,0:T(2,128)S(1)}, bf16[2,512,3072]{1,2,0:T(8,128)(2,1)}) fusion(pred[512,3072]{0,1:T(8,128)(4,1)} %fusion.10, bf16[512,2,64]{0,2,1:T(8,128)(2,1)S(1)} %bitcast.130, bf16[512,2,64]{0,2,1:T(8,128)(2,1)S(1)} %bitcast.129, bf16[2048,2,64]{0,2,1:T(8,128)(2,1)S(1)} %bitcast.124, bf16[512,2,64]{0,2,1:T(8,128)(2,1)S(1)} %bitcast.126), kind=kOutput, calls=%fused_computation.108 | convolution fusion | flops 832048128 | bytes 8785920 | tf_op jit(solution)/shard_map/while/body/eval_jaxpr/sub | solution.py:53
  27.5 4.0 %fusion.29 = bf16[512,2,64]{0,2,1:T(8,128)(2,1)S(1)} fusion(bf16[2,512,3072]{1,2,0:T(8,128)(2,1)} %get-tuple-element.70, bf16[512,2,64]{0,2,1:T(8,128)(2,1)S(1)} %bitcast.128, bf16[2048,2,64]{0,2,1:T(8,128)(2,1)S(1)} %bitcast.123, bf16[512,2,64]{0,2,1:T(8,128)(2,1)S(1)} %bitcast.127, f32[512,2]{0,1:T(2,128)S(1)} %bitcast.133), kind=kOutput, calls=%fused_computation.39 | convolution fusion | flops 405143552 | bytes 7213056 | tf_op jit(solution)/shard_map/while/body/eval_jaxpr/hqk,khd->qhd/dot_general | solution.py:56
  32.2 1.4 reduce.3
  33.6 0.7 reshape.530
  34.3 4.5 %all-to-all-start = ((bf16[8,2,4096]{2,1,0:T(2,128)(2,1)}), bf16[8,2,4096]{2,1,0:T(2,128)(2,1)S(1)}, u32[]{:S(2)}, u32[]{:S(2)}) async-start(bf16[8,2,4096]{2,1,0:T(2,128)(2,1)} %reshape.530), calls=%async_computation | async-start | bytes 262144 | tf_op jit(solution)/shard_map/all_to_all | solution.py:126
  40.2 4.8 %all-to-all-done = bf16[8,2,4096]{2,1,0:T(2,128)(2,1)S(1)} async-done(((bf16[8,2,4096]{2,1,0:T(2,128)(2,1)}), bf16[8,2,4096]{2,1,0:T(2,128)(2,1)S(1)}, u32[]{:S(2)}, u32[]{:S(2)}) %all-to-all-start) | async-done | bytes 131104 | tf_op jit(solution)/shard_map/all_to_all | solution.py:126
  45.3 2.2 multiply_reduce_fusion.1
  47.5 0.7 copy-done.1
  49.2 1.4 scatter_custom_fusion
  50.7 39.4 %all_to_all.40 = bf16[32,16,1024]{2,1,0:T(8,128)(2,1)} all-to-all(bf16[32,16,1024]{2,1,0:T(8,128)(2,1)S(1)} %bitcast.117), channel_id=1, replica_groups=mesh['req'=32,'head'=4,'blk'=2] {'req'}, dimensions={0} | all-to-all | bytes 2097152 | tf_op jit(solution)/shard_map/all_to_all | solution.py:152
  90.3 6.3 %fusion.42 = (bf16[1,2560,128]{2,1,0:T(8,128)(2,1)}, bf16[1,2560,128]{2,1,0:T(8,128)(2,1)}) fusion(s32[]{:T(128)} %bitcast.33, bf16[1,2048,128]{2,1,0:T(8,128)(2,1)S(1)} %broadcast.289, bf16[1,512,128]{2,1,0:T(8,128)(2,1)S(1)} %copy-done.8, bf16[1,2048,128]{2,1,0:T(8,128)(2,1)S(1)} %copy-done.4, pred[2560]{0:T(1024)(128)(4,1)S(1)} %iota_compare_fusion.4, ...), kind=kLoop, calls=%fused_computation.51 | loop fusion | flops 4587520 | bytes 3148292 | tf_op jit(solution)/shard_map/vmap(jit(_where))/select_n | solution.py:72
  96.6 3.5 %all-to-all-start.5 = ((bf16[1,8,320,128]{3,2,0,1:T(8,128)(2,1)}), bf16[1,8,320,128]{3,2,0,1:T(8,128)(2,1)S(1)}, u32[]{:S(2)}, u32[]{:S(2)}) async-start(bf16[1,8,320,128]{3,2,0,1:T(8,128)(2,1)} %bitcast.36), calls=%async_computation.5 | async-start | bytes 1310720 | tf_op jit(solution)/shard_map/all_to_all | solution.py:79
  100.2 42.8 %all-gather.6.cloned.1.call-done = bf16[128,16,1024]{2,1,0:T(8,128)(2,1)} async-done(((bf16[32,16,1024]{2,1,0:T(8,128)(2,1)}), bf16[128,16,1024]{2,1,0:T(8,128)(2,1)}) %all-gather.6.cloned.1.call-update) | async-done | bytes 4194320 | tf_op jit(solution)/shard_map/all_gather | solution.py:153
  143.0 5.6 %fusion.73 = f32[2048,352]{0,1:T(8,128)} fusion(bf16[2048,1024]{1,0:T(8,128)(2,1)} %bitcast.131, bf16[1024,352]{0,1:T(8,128)(2,1)S(1)} %copy-done.14), kind=kOutput, calls=%fused_computation.109 | convolution fusion | flops 1476395008 | bytes 7798784 | tf_op jit(solution)/shard_map/dot_general | solution.py:155
  148.6 9.2 %convolution_convert_fusion = bf16[2048,1024]{1,0:T(8,128)(2,1)} fusion(bf16[352,1024]{1,0:T(8,128)(2,1)S(1)} %copy-done, bf16[2048,1024]{1,0:T(8,128)(2,1)} %bitcast.132, bf16[1024,352]{0,1:T(8,128)(2,1)S(1)} %copy-done.15, f32[2048,352]{0,1:T(8,128)} %fusion.73), kind=kOutput, calls=%fused_computation.19 | convolution fusion | flops 2962096128 | bytes 12713984 | tf_op jit(solution)/shard_map/dot_general | solution.py:159
  157.8 54.6 %all_to_all.41 = bf16[4,32,16,1024]{3,2,1,0:T(8,128)(2,1)} all-to-all(bf16[4,32,16,1024]{3,2,1,0:T(8,128)(2,1)} %bitcast.116), channel_id=1, replica_groups=mesh['req'=32,'head'=4,'blk'=2] {'head'}, dimensions={0} | all-to-all | bytes 8388608 | tf_op jit(solution)/shard_map/all_to_all | solution.py:163
  212.4 3.5 %all-to-all-start.4 = ((bf16[1,8,320,128]{3,2,0,1:T(8,128)(2,1)}), bf16[1,8,320,128]{3,2,0,1:T(8,128)(2,1)S(1)}, u32[]{:S(2)}, u32[]{:S(2)}) async-start(bf16[1,8,320,128]{3,2,0,1:T(8,128)(2,1)} %bitcast.34), calls=%async_computation.4 | async-start | bytes 1310720 | tf_op jit(solution)/shard_map/all_to_all | solution.py:79
  216.0 4.4 %reduce_sum.69 = bf16[32,16,1024]{2,1,0:T(8,128)(2,1)} reduce(bf16[4,32,16,1024]{3,2,1,0:T(8,128)(2,1)} %all_to_all.41, bf16[]{:T(256)} %constant.108.clone.1), dimensions={0}, to_apply=%region_6.8 | reduce | flops 1572864 | bytes 5242882 | tf_op jit(solution)/shard_map/reduce_sum | solution.py:164
  220.4 7.2 %all-to-all-done.4 = bf16[1,8,320,128]{3,2,0,1:T(8,128)(2,1)S(1)} async-done(((bf16[1,8,320,128]{3,2,0,1:T(8,128)(2,1)}), bf16[1,8,320,128]{3,2,0,1:T(8,128)(2,1)S(1)}, u32[]{:S(2)}, u32[]{:S(2)}) %all-to-all-start.4) | async-done | bytes 655392 | tf_op jit(solution)/shard_map/all_to_all | solution.py:79
  227.6 8.5 %all-to-all-start.3 = ((bf16[32,16,1024]{2,1,0:T(8,128)(2,1)}), bf16[32,16,1024]{2,1,0:T(8,128)(2,1)S(1)}, u32[]{:S(2)}, u32[]{:S(2)}) async-start(bf16[32,16,1024]{2,1,0:T(8,128)(2,1)} %reduce_sum.69), calls=%async_computation.3 | async-start | bytes 2097152 | tf_op jit(solution)/shard_map/all_to_all | solution.py:165
  236.7 0.9 copy_bitcast_fusion
  237.6 0.9 copy_bitcast_fusion.1
  238.7 1.3 gather_fusion.1
  240.4 23.4 %all-to-all-done.3 = bf16[32,16,1024]{2,1,0:T(8,128)(2,1)S(1)} async-done(((bf16[32,16,1024]{2,1,0:T(8,128)(2,1)}), bf16[32,16,1024]{2,1,0:T(8,128)(2,1)S(1)}, u32[]{:S(2)}, u32[]{:S(2)}) %all-to-all-start.3) | async-done | bytes 1048608 | tf_op jit(solution)/shard_map/all_to_all | solution.py:165
  264.1 0.8 gather_fusion
  265.2 0.8 multiply_reduce_fusion
  266.1 0.7 fusion.44
  (84 shorter events, 6.3 us)
Async XLA Ops:
  7.2 141.4 %copy-start = (bf16[352,1024]{1,0:T(8,128)(2,1)S(1)}, bf16[352,1024]{1,0:T(8,128)(2,1)}, u32[]{:S(2)}) copy-start(bf16[352,1024]{1,0:T(8,128)(2,1)} %param.35) | copy-start | bytes 2162692
  7.2 6.6 %copy-start.4 = (bf16[1,2048,128]{2,1,0:T(8,128)(2,1)S(1)}, bf16[1,2048,128]{2,1,0:T(8,128)(2,1)}, u32[]{:S(2)}) copy-start(bf16[1,2048,128]{2,1,0:T(8,128)(2,1)} %param.25) | copy-start | bytes 1572868
  7.2 6.8 %copy-start.8 = (bf16[1,512,128]{2,1,0:T(8,128)(2,1)S(1)}, bf16[1,512,128]{2,1,0:T(8,128)(2,1)}, u32[]{:S(2)}) copy-start(bf16[1,512,128]{2,1,0:T(8,128)(2,1)} %param.23) | copy-start | bytes 393220
  7.2 38.1 %all-gather.4.cloned.1.call-start = ((), (), s32[]{:S(2)}) async-start(), calls=%async_computation.6 | async-start | bytes 2359296 | tf_op jit(solution)/shard_map/all_gather | solution.py:125
  27.5 11.4 %copy-start.11 = (s32[1,64,2]{1,2,0:T(2,128)S(1)}, s32[1,64,2]{1,2,0:T(2,128)}, u32[]{:S(2)}) copy-start(s32[1,64,2]{1,2,0:T(2,128)} %param.36) | copy-start | bytes 1540
  27.5 11.9 %copy-start.13 = (s32[1,64,2]{1,2,0:T(2,128)S(1)}, s32[1,64,2]{1,2,0:T(2,128)}, u32[]{:S(2)}) copy-start(s32[1,64,2]{1,2,0:T(2,128)} %param.37) | copy-start | bytes 1540
  31.5 13.8 %copy-start.9 = (bf16[1,64,1024]{2,1,0:T(8,128)(2,1)S(1)}, bf16[1,64,1024]{2,1,0:T(8,128)(2,1)}, u32[]{:S(2)}) copy-start(bf16[1,64,1024]{2,1,0:T(8,128)(2,1)} %param.20) | copy-start | bytes 393220
  31.5 16.7 %copy-start.12 = (f32[1024]{0:T(1024)S(1)}, f32[1024]{0:T(1024)}, u32[]{:S(2)}) copy-start(f32[1024]{0:T(1024)} %param.31) | copy-start | bytes 12292
  34.3 10.7 %all-to-all-start = ((bf16[8,2,4096]{2,1,0:T(2,128)(2,1)}), bf16[8,2,4096]{2,1,0:T(2,128)(2,1)S(1)}, u32[]{:S(2)}, u32[]{:S(2)}) async-start(bf16[8,2,4096]{2,1,0:T(2,128)(2,1)} %reshape.530), calls=%async_computation | async-start | bytes 262144 | tf_op jit(solution)/shard_map/all_to_all | solution.py:126
  38.9 104.1 %all-gather.6.cloned.1.call-start = ((), (), s32[]{:S(2)}) async-start(), calls=%async_computation.7 | async-start | bytes 5242880 | tf_op jit(solution)/shard_map/all_gather | solution.py:153
  47.5 0.7 copy-start.1
  48.3 0.7 copy-start.5
  49.2 41.1 %copy-start.3 = (bf16[1,2048,128]{2,1,0:T(8,128)(2,1)S(1)}, bf16[1,2048,128]{2,1,0:T(8,128)(2,1)}, u32[]{:S(2)}) copy-start(bf16[1,2048,128]{2,1,0:T(8,128)(2,1)} %param.24) | copy-start | bytes 1572868
  49.2 41.1 %copy-start.7 = (bf16[1,512,128]{2,1,0:T(8,128)(2,1)S(1)}, bf16[1,512,128]{2,1,0:T(8,128)(2,1)}, u32[]{:S(2)}) copy-start(bf16[1,512,128]{2,1,0:T(8,128)(2,1)} %param.22) | copy-start | bytes 393220
  90.1 52.9 %copy-start.14 = (bf16[1024,352]{0,1:T(8,128)(2,1)S(1)}, bf16[1024,352]{0,1:T(8,128)(2,1)}, u32[]{:S(2)}) copy-start(bf16[1024,352]{0,1:T(8,128)(2,1)} %param.33) | copy-start | bytes 2162692
  96.6 61.2 %all-to-all-start.5 = ((bf16[1,8,320,128]{3,2,0,1:T(8,128)(2,1)}), bf16[1,8,320,128]{3,2,0,1:T(8,128)(2,1)S(1)}, u32[]{:S(2)}, u32[]{:S(2)}) async-start(bf16[1,8,320,128]{3,2,0,1:T(8,128)(2,1)} %bitcast.36), calls=%async_computation.5 | async-start | bytes 1310720 | tf_op jit(solution)/shard_map/all_to_all | solution.py:79
  143.0 5.6 %copy-start.15 = (bf16[1024,352]{0,1:T(8,128)(2,1)S(1)}, bf16[1024,352]{0,1:T(8,128)(2,1)}, u32[]{:S(2)}) copy-start(bf16[1024,352]{0,1:T(8,128)(2,1)} %param.34) | copy-start | bytes 2162692
  212.4 15.2 %all-to-all-start.4 = ((bf16[1,8,320,128]{3,2,0,1:T(8,128)(2,1)}), bf16[1,8,320,128]{3,2,0,1:T(8,128)(2,1)S(1)}, u32[]{:S(2)}, u32[]{:S(2)}) async-start(bf16[1,8,320,128]{3,2,0,1:T(8,128)(2,1)} %bitcast.34), calls=%async_computation.4 | async-start | bytes 1310720 | tf_op jit(solution)/shard_map/all_to_all | solution.py:79
  220.4 18.2 %copy-start.6 = (bf16[64,1024]{1,0:T(8,128)(2,1)S(1)}, bf16[64,1024]{1,0:T(8,128)(2,1)}, u32[]{:S(2)}) copy-start(bf16[64,1024]{1,0:T(8,128)(2,1)} %copy-done.5) | copy-start | bytes 393220
  220.4 18.2 %copy-start.10 = (bf16[1024,16]{0,1:T(8,128)(2,1)S(1)}, bf16[1024,16]{0,1:T(8,128)(2,1)}, u32[]{:S(2)}) copy-start(bf16[1024,16]{0,1:T(8,128)(2,1)} %param.32) | copy-start | bytes 98308
  227.6 36.2 %all-to-all-start.3 = ((bf16[32,16,1024]{2,1,0:T(8,128)(2,1)}), bf16[32,16,1024]{2,1,0:T(8,128)(2,1)S(1)}, u32[]{:S(2)}, u32[]{:S(2)}) async-start(bf16[32,16,1024]{2,1,0:T(8,128)(2,1)} %reduce_sum.69), calls=%async_computation.3 | async-start | bytes 2097152 | tf_op jit(solution)/shard_map/all_to_all | solution.py:165
  264.1 2.0 copy-start.2
Sparse Core Ops, SparseCore 0:
  9.9 30.7 all-gather.3
  90.3 52.6 all-gather.5
where the time goes:
time: 274 us
  blocking collectives  94 us (34%)
  waiting for transfers between devices  79 us (29%)
  matrix products  30.2 us (11%)
  other arithmetic  21.2 us (8%)
  starting transfers between devices  20.2 us (7%)
  between operations  15.8 us (6%)
  local copies, waits for them, and re-layouts  13.2 us (5%)
    all_to_all x1, blocking collectives, body(): lax.all_to_all(partial, 'head', split_axis=0, concat_axis=0, tiled=True)  54.6 us
    all_gather x1, waiting for transfers between devices, body(): gathered = lax.all_gather(arrived, 'head', axis=0, tiled=False)  42.8 us
    all_to_all x1, blocking collectives, body(): lax.all_to_all(outgoing, 'req', split_axis=0, concat_axis=0, tiled=True)  39.4 us
    all_to_all x1, waiting for transfers between devices, body(): lax.all_to_all(half_sum, 'req', split_axis=0, concat_axis=0, tiled=True)  23.4 us
    dot_general x1, matrix products, body(): jnp.dot(hidden, expert_down, preferred_element_type=jnp.float32)  9.24 us
    sub x1, matrix products, attend_request(): weights = jnp.where(visible[None], jnp.exp(scores - highest), 0.0)  9.03 us
    all_to_all x1, starting transfers between devices, body(): lax.all_to_all(half_sum, 'req', split_axis=0, concat_axis=0, tiled=True)  8.47 us
    all_to_all x2, waiting for transfers between devices, to_positions(): lax.all_to_all(parts, ('head', 'blk'), split_axis=1, concat_axis=1, tiled...  7.23 us
  transfers between devices with their start and end apart: 6, of which 4 were waited for; matrix products, arithmetic and copies ran while one was open for 21% of the time, Pallas kernels for 0%

commit v1 on v0

--- a/solution.py
+++ b/solution.py
@@ -148,24 +148,32 @@
     )
     buffer = jnp.zeros((experts * slots_here, width), jnp.bfloat16).at[places].set(sent_rows)
     holders = lax.axis_size("req") // experts
-    outgoing = jnp.repeat(buffer.reshape(experts, slots_here, width), holders, axis=0)
-    arrived = lax.all_to_all(outgoing, "req", split_axis=0, concat_axis=0, tiled=True)
-    gathered = lax.all_gather(arrived, "head", axis=0, tiled=False)
-    flat_rows = gathered.reshape(-1, width)
-    gate_val = jnp.dot(flat_rows, expert_gate, preferred_element_type=jnp.float32)
-    up_val = jnp.dot(flat_rows, expert_up, preferred_element_type=jnp.float32)
-    hidden = (jax.nn.gelu(gate_val, approximate=True) * up_val).astype(jnp.bfloat16)
-    partial = (
-        jnp.dot(hidden, expert_down, preferred_element_type=jnp.float32)
-        .astype(jnp.bfloat16)
-        .reshape(gathered.shape)
-    )
-    shard_parts = lax.all_to_all(partial, "head", split_axis=0, concat_axis=0, tiled=True)
-    half_sum = jnp.sum(shard_parts.astype(jnp.float32), axis=0).astype(jnp.bfloat16)
-    returned = lax.all_to_all(half_sum, "req", split_axis=0, concat_axis=0, tiled=True)
-    combined = jnp.sum(
-        returned.reshape(experts, holders, slots_here, width), axis=1, dtype=jnp.float32
-    ).reshape(experts * slots_here, width)
+    new_keys, new_values, buffer = lax.optimization_barrier((new_keys, new_values, buffer))
+    slabs = buffer.reshape(experts, slots_here, width)
+    chunks = 2
+    step = slots_here // chunks
+    pieces = []
+    for c in range(chunks):
+        piece = slabs[:, c * step:(c + 1) * step]
+        outgoing = jnp.repeat(piece, holders, axis=0)
+        arrived = lax.all_to_all(outgoing, "req", split_axis=0, concat_axis=0, tiled=True)
+        gathered = lax.all_gather(arrived, "head", axis=0, tiled=False)
+        flat_rows = gathered.reshape(-1, width)
+        gate_val = jnp.dot(flat_rows, expert_gate, preferred_element_type=jnp.float32)
+        up_val = jnp.dot(flat_rows, expert_up, preferred_element_type=jnp.float32)
+        hidden = (jax.nn.gelu(gate_val, approximate=True) * up_val).astype(jnp.bfloat16)
+        partial = (
+            jnp.dot(hidden, expert_down, preferred_element_type=jnp.float32)
+            .astype(jnp.bfloat16)
+            .reshape(gathered.shape)
+        )
+        shard_parts = lax.all_to_all(partial, "head", split_axis=0, concat_axis=0, tiled=True)
+        half_sum = jnp.sum(shard_parts.astype(jnp.float32), axis=0).astype(jnp.bfloat16)
+        returned = lax.all_to_all(half_sum, "req", split_axis=0, concat_axis=0, tiled=True)
+        pieces.append(
+            jnp.sum(returned.reshape(experts, holders, step, width), axis=1, dtype=jnp.float32)
+        )
+    combined = jnp.concatenate(pieces, axis=1).reshape(experts * slots_here, width)
     picked = jnp.take(combined, places, axis=0).reshape(-1, 2, width)
     mixture = jnp.sum(picked * gate_weights[:, :, None], axis=1)
     y_out = (

time: 274 us -> 292 us (1.066)
  blocking collectives: 94 us -> 49.5 us
  waiting for transfers between devices: 79 us -> 118 us
  starting transfers between devices: 20.2 us -> 38.9 us
  matrix products: 30.2 us -> 34.5 us
    all_to_all x1 -> x0, blocking collectives: 54.6 us -> none  [body(): lax.all_to_all(partial, 'head', split_axis=0, concat_axis=0, tiled=True)]
    all_to_all x0 -> x2, waiting for transfers between devices: none -> 23.5 us  [body(): lax.all_to_all(partial, 'head', split_axis=0, concat_axis=0, tiled=True)]
    all_to_all x2, waiting for transfers between devices: 7.23 us -> 20.7 us  [to_positions(): lax.all_to_all(parts, ('head', 'blk'), split_axis=1, concat_axis=1, tiled...]
    all_to_all x1 -> x2, blocking collectives: 39.4 us -> 49.5 us  [body(): lax.all_to_all(outgoing, 'req', split_axis=0, concat_axis=0, tiled=True)]
    all_to_all x0 -> x2, starting transfers between devices: none -> 9.97 us  [body(): lax.all_to_all(partial, 'head', split_axis=0, concat_axis=0, tiled=True)]
    all_to_all x1 -> x2, starting transfers between devices: 8.47 us -> 15.8 us  [body(): lax.all_to_all(half_sum, 'req', split_axis=0, concat_axis=0, tiled=True)]
    all_to_all x1, waiting for transfers between devices: 4.82 us -> 0.01 us  [body(): lax.all_to_all(attended, ('head', 'blk'), split_axis=1, concat_axis=2, ti...]
    all_to_all x1 -> x2, waiting for transfers between devices: 23.4 us -> 26.7 us  [body(): lax.all_to_all(half_sum, 'req', split_axis=0, concat_axis=0, tiled=True)]
  transfers between devices with their start and end apart: 6 -> 10, of which waited for: 4 -> 7; matrix products, arithmetic and copies ran while one was open for 21% -> 21% of each run, Pallas kernels for 0% -> 0%
where the time goes in v1:
time: 292 us; the launch traced here: 291 us
  waiting for transfers between devices  118 us (40%)
  blocking collectives  49.5 us (17%)
  starting transfers between devices  38.9 us (13%)
  matrix products  34.5 us (12%)
  other arithmetic  20.6 us (7%)
  between operations  15.5 us (5%)
  local copies, waits for them, and re-layouts  14.3 us (5%)
    all_to_all x2, blocking collectives, body(): lax.all_to_all(outgoing, 'req', split_axis=0, concat_axis=0, tiled=True)  49.5 us
    all_gather x2, waiting for transfers between devices, body(): gathered = lax.all_gather(arrived, 'head', axis=0, tiled=False)  45.9 us
    all_to_all x2, waiting for transfers between devices, body(): lax.all_to_all(half_sum, 'req', split_axis=0, concat_axis=0, tiled=True)  26.7 us
    all_to_all x2, waiting for transfers between devices, body(): lax.all_to_all(partial, 'head', split_axis=0, concat_axis=0, tiled=True)  23.5 us
    all_to_all x2, waiting for transfers between devices, to_positions(): lax.all_to_all(parts, ('head', 'blk'), split_axis=1, concat_axis=1, tiled...  20.7 us
    all_to_all x2, starting transfers between devices, body(): lax.all_to_all(half_sum, 'req', split_axis=0, concat_axis=0, tiled=True)  15.8 us
    dot_general x2, matrix products, body(): jnp.dot(hidden, expert_down, preferred_element_type=jnp.float32)  10.9 us
    all_to_all x2, starting transfers between devices, body(): lax.all_to_all(partial, 'head', split_axis=0, concat_axis=0, tiled=True)  9.97 us
  transfers between devices with their start and end apart: 10, of which 7 were waited for; matrix products, arithmetic and copies ran while one was open for 21% of the time, Pallas kernels for 0%

profile of v1, /device:TPU:4, one launch (start us, length us, event | category | flops | bytes accessed | tf_op | source)
XLA Modules:
  0.0 290.9 jit_solution(8523068845138822945)
XLA Ops:
  10.4 2.0 copy.101
  15.2 2.8 fusion.10
  18.0 9.4 %fusion.115 = (f32[2,512]{1,0:T(2,128)S(1)}, bf16[2,512,3072]{1,2,0:T(8,128)(2,1)}) fusion(pred[512,3072]{0,1:T(8,128)(4,1)S(1)} %fusion.10, bf16[512,2,64]{0,2,1:T(8,128)(2,1)} %bitcast.159, bf16[512,2,64]{0,2,1:T(8,128)(2,1)} %bitcast.158, bf16[2048,2,64]{0,2,1:T(8,128)(2,1)} %bitcast.153, bf16[512,2,64]{0,2,1:T(8,128)(2,1)S(1)} %bitcast.155), kind=kOutput, calls=%fused_computation.142 | convolution fusion | flops 832048128 | bytes 8785920 | tf_op jit(solution)/shard_map/while/body/eval_jaxpr/sub | solution.py:53
  27.5 4.1 %fusion.55 = bf16[512,2,64]{0,2,1:T(8,128)(2,1)S(1)} fusion(bf16[2,512,3072]{1,2,0:T(8,128)(2,1)} %get-tuple-element.78, bf16[512,2,64]{0,2,1:T(8,128)(2,1)S(1)} %bitcast.157, bf16[2048,2,64]{0,2,1:T(8,128)(2,1)} %bitcast.152, bf16[512,2,64]{0,2,1:T(8,128)(2,1)S(1)} %bitcast.156, f32[512,2]{0,1:T(2,128)S(1)} %bitcast.160), kind=kOutput, calls=%fused_computation.57 | convolution fusion | flops 405143552 | bytes 7213056 | tf_op jit(solution)/shard_map/while/body/eval_jaxpr/hqk,khd->qhd/dot_general | solution.py:56
  32.3 1.4 reduce.4
  34.4 4.6 %all-to-all-start = ((bf16[8,2,4096]{2,1,0:T(2,128)(2,1)}), bf16[8,2,4096]{2,1,0:T(2,128)(2,1)S(1)}, u32[]{:S(2)}, u32[]{:S(2)}) async-start(bf16[8,2,4096]{2,1,0:T(2,128)(2,1)} %reshape.548), calls=%async_computation | async-start | bytes 262144 | tf_op jit(solution)/shard_map/all_to_all | solution.py:126
  39.1 6.3 %fusion.80 = (bf16[1,2560,128]{2,1,0:T(8,128)(2,1)}, bf16[1,2560,128]{2,1,0:T(8,128)(2,1)}) fusion(s32[]{:T(128)} %bitcast.21, bf16[1,2048,128]{2,1,0:T(8,128)(2,1)S(1)} %broadcast.300, bf16[1,512,128]{2,1,0:T(8,128)(2,1)S(1)} %copy-done.5, bf16[1,2048,128]{2,1,0:T(8,128)(2,1)S(1)} %copy-done.3, pred[2560]{0:T(1024)(128)(4,1)S(1)} %iota_compare_fusion.4, ...), kind=kLoop, calls=%fused_computation.80 | loop fusion | flops 4587520 | bytes 3148292 | tf_op jit(solution)/shard_map/vmap(jit(_where))/select_n | solution.py:72
  45.4 4.8 %all-to-all-start.2 = ((bf16[1,8,320,128]{3,2,0,1:T(8,128)(2,1)}), bf16[1,8,320,128]{3,2,0,1:T(8,128)(2,1)S(1)}, u32[]{:S(2)}, u32[]{:S(2)}) async-start(bf16[1,8,320,128]{3,2,0,1:T(8,128)(2,1)} %bitcast.24), calls=%async_computation.2 | async-start | bytes 1310720 | tf_op jit(solution)/shard_map/all_to_all | solution.py:79
  51.3 10.7 %all-to-all-done.2 = bf16[1,8,320,128]{3,2,0,1:T(8,128)(2,1)S(1)} async-done(((bf16[1,8,320,128]{3,2,0,1:T(8,128)(2,1)}), bf16[1,8,320,128]{3,2,0,1:T(8,128)(2,1)S(1)}, u32[]{:S(2)}, u32[]{:S(2)}) %all-to-all-start.2) | async-done | bytes 655392 | tf_op jit(solution)/shard_map/all_to_all | solution.py:79
  62.0 3.5 %all-to-all-start.1 = ((bf16[1,8,320,128]{3,2,0,1:T(8,128)(2,1)}), bf16[1,8,320,128]{3,2,0,1:T(8,128)(2,1)S(1)}, u32[]{:S(2)}, u32[]{:S(2)}) async-start(bf16[1,8,320,128]{3,2,0,1:T(8,128)(2,1)} %bitcast.22), calls=%async_computation.1 | async-start | bytes 1310720 | tf_op jit(solution)/shard_map/all_to_all | solution.py:79
  67.1 10.0 %all-to-all-done.1 = bf16[1,8,320,128]{3,2,0,1:T(8,128)(2,1)S(1)} async-done(((bf16[1,8,320,128]{3,2,0,1:T(8,128)(2,1)}), bf16[1,8,320,128]{3,2,0,1:T(8,128)(2,1)S(1)}, u32[]{:S(2)}, u32[]{:S(2)}) %all-to-all-start.1) | async-done | bytes 655392 | tf_op jit(solution)/shard_map/all_to_all | solution.py:79
  78.1 2.2 multiply_reduce_fusion.1
  80.7 1.4 scatter_custom_fusion
  82.2 28.1 %all_to_all.55 = bf16[32,8,1024]{2,1,0:T(8,128)(2,1)} all-to-all(bf16[32,8,1024]{2,1,0:T(8,128)(2,1)S(1)} %bitcast.146), channel_id=1, replica_groups=mesh['req'=32,'head'=4,'blk'=2] {'req'}, dimensions={0} | all-to-all | bytes 1048576 | tf_op jit(solution)/shard_map/all_to_all | solution.py:159
  110.4 21.4 %all_to_all.56 = bf16[32,8,1024]{2,1,0:T(8,128)(2,1)} all-to-all(bf16[32,8,1024]{2,1,0:T(8,128)(2,1)S(1)} %bitcast.147), channel_id=1, replica_groups=mesh['req'=32,'head'=4,'blk'=2] {'req'}, dimensions={0} | all-to-all | bytes 1048576 | tf_op jit(solution)/shard_map/all_to_all | solution.py:159
  131.8 6.8 %all-gather.8.cloned.1.call-done = bf16[128,8,1024]{2,1,0:T(8,128)(2,1)} async-done(((bf16[32,8,1024]{2,1,0:T(8,128)(2,1)}), bf16[128,8,1024]{2,1,0:T(8,128)(2,1)}) %all-gather.8.cloned.1.call-update) | async-done | bytes 2097168 | tf_op jit(solution)/shard_map/all_gather | solution.py:160
  138.6 3.9 %fusion.18 = f32[1024,352]{0,1:T(8,128)} fusion(bf16[1024,352]{0,1:T(8,128)(2,1)} %param.33, bf16[128,8,1024]{2,1,0:T(8,128)(2,1)} %all-gather.8.cloned.1.call-done), kind=kOutput, calls=%fused_computation.26 | convolution fusion | flops 738197504 | bytes 4259840 | tf_op jit(solution)/shard_map/dot_general | solution.py:162
  142.6 5.2 %convolution_convert_fusion.1 = bf16[1024,1024]{1,0:T(8,128)(2,1)} fusion(bf16[352,1024]{1,0:T(8,128)(2,1)S(1)} %copy-done, bf16[1024,352]{0,1:T(8,128)(2,1)} %param.34, bf16[128,8,1024]{2,1,0:T(8,128)(2,1)S(1)} %copy-done.12, f32[1024,352]{0,1:T(8,128)} %fusion.18), kind=kOutput, calls=%fused_computation.29 | convolution fusion | flops 1481048064 | bytes 7077888 | tf_op jit(solution)/shard_map/dot_general | solution.py:166
  147.7 3.6 %all-to-all-start.4 = ((bf16[4,32,8,1024]{3,2,1,0:T(8,128)(2,1)}), bf16[4,32,8,1024]{3,2,1,0:T(8,128)(2,1)S(1)}, u32[]{:S(2)}, u32[]{:S(2)}) async-start(bf16[4,32,8,1024]{3,2,1,0:T(8,128)(2,1)} %bitcast.143), calls=%async_computation.4 | async-start | bytes 4194304 | tf_op jit(solution)/shard_map/all_to_all | solution.py:170
  151.3 39.1 %all-gather.10.cloned.1.call-done = bf16[128,8,1024]{2,1,0:T(8,128)(2,1)} async-done(((bf16[32,8,1024]{2,1,0:T(8,128)(2,1)}), bf16[128,8,1024]{2,1,0:T(8,128)(2,1)}) %all-gather.10.cloned.1.call-update) | async-done | bytes 2097168 | tf_op jit(solution)/shard_map/all_gather | solution.py:160
  190.4 3.8 %fusion.14 = f32[1024,352]{0,1:T(8,128)} fusion(bf16[1024,352]{0,1:T(8,128)(2,1)} %param.33, bf16[128,8,1024]{2,1,0:T(8,128)(2,1)} %all-gather.10.cloned.1.call-done), kind=kOutput, calls=%fused_computation.22 | convolution fusion | flops 738197504 | bytes 4259840 | tf_op jit(solution)/shard_map/dot_general | solution.py:162
  194.2 5.8 %convolution_convert_fusion = bf16[1024,1024]{1,0:T(8,128)(2,1)} fusion(bf16[352,1024]{1,0:T(8,128)(2,1)S(1)} %copy-done, bf16[1024,352]{0,1:T(8,128)(2,1)} %param.34, bf16[128,8,1024]{2,1,0:T(8,128)(2,1)} %all-gather.10.cloned.1.call-done, f32[1024,352]{0,1:T(8,128)} %fusion.14), kind=kOutput, calls=%fused_computation.28 | convolution fusion | flops 1481048064 | bytes 7077888 | tf_op jit(solution)/shard_map/dot_general | solution.py:166
  200.0 1.3 copy-done.1
  201.3 6.4 %all-to-all-start.7 = ((bf16[4,32,8,1024]{3,2,1,0:T(8,128)(2,1)}), bf16[4,32,8,1024]{3,2,1,0:T(8,128)(2,1)S(1)}, u32[]{:S(2)}, u32[]{:S(2)}) async-start(bf16[4,32,8,1024]{3,2,1,0:T(8,128)(2,1)} %bitcast.144), calls=%async_computation.7 | async-start | bytes 4194304 | tf_op jit(solution)/shard_map/all_to_all | solution.py:170
  207.7 2.9 %reduce_sum.90 = bf16[32,8,1024]{2,1,0:T(8,128)(2,1)} reduce(bf16[4,32,8,1024]{3,2,1,0:T(8,128)(2,1)} %copy-done.1, bf16[]{:T(256)} %constant.109.clone.1), dimensions={0}, to_apply=%region_6.8 | reduce | flops 786432 | bytes 2621442 | tf_op jit(solution)/shard_map/reduce_sum | solution.py:171
  210.6 23.5 %all-to-all-done.7 = bf16[4,32,8,1024]{3,2,1,0:T(8,128)(2,1)S(1)} async-done(((bf16[4,32,8,1024]{3,2,1,0:T(8,128)(2,1)}), bf16[4,32,8,1024]{3,2,1,0:T(8,128)(2,1)S(1)}, u32[]{:S(2)}, u32[]{:S(2)}) %all-to-all-start.7) | async-done | bytes 2097184 | tf_op jit(solution)/shard_map/all_to_all | solution.py:170
  234.1 10.2 %all-to-all-start.5 = ((bf16[32,8,1024]{2,1,0:T(8,128)(2,1)}), bf16[32,8,1024]{2,1,0:T(8,128)(2,1)}, u32[]{:S(2)}, u32[]{:S(2)}) async-start(bf16[32,8,1024]{2,1,0:T(8,128)(2,1)} %reduce_sum.90), calls=%async_computation.5 | async-start | bytes 1048576 | tf_op jit(solution)/shard_map/all_to_all | solution.py:172
  244.6 1.3 reduce_sum.92
  245.9 14.3 %all-to-all-done.5 = bf16[32,8,1024]{2,1,0:T(8,128)(2,1)} async-done(((bf16[32,8,1024]{2,1,0:T(8,128)(2,1)}), bf16[32,8,1024]{2,1,0:T(8,128)(2,1)}, u32[]{:S(2)}, u32[]{:S(2)}) %all-to-all-start.5) | async-done | bytes 524320 | tf_op jit(solution)/shard_map/all_to_all | solution.py:172
  260.2 5.6 %all-to-all-start.8 = ((bf16[32,8,1024]{2,1,0:T(8,128)(2,1)}), bf16[32,8,1024]{2,1,0:T(8,128)(2,1)S(1)}, u32[]{:S(2)}, u32[]{:S(2)}) async-start(bf16[32,8,1024]{2,1,0:T(8,128)(2,1)} %reduce_sum.92), calls=%async_computation.8 | async-start | bytes 1048576 | tf_op jit(solution)/shard_map/all_to_all | solution.py:172
  266.3 1.3 gather_fusion.1
  269.2 12.4 %all-to-all-done.8 = bf16[32,8,1024]{2,1,0:T(8,128)(2,1)S(1)} async-done(((bf16[32,8,1024]{2,1,0:T(8,128)(2,1)}), bf16[32,8,1024]{2,1,0:T(8,128)(2,1)S(1)}, u32[]{:S(2)}, u32[]{:S(2)}) %all-to-all-start.8) | async-done | bytes 524320 | tf_op jit(solution)/shard_map/all_to_all | solution.py:172
  (94 shorter events, 15.2 us)
Async XLA Ops:
  7.2 135.4 %copy-start = (bf16[352,1024]{1,0:T(8,128)(2,1)S(1)}, bf16[352,1024]{1,0:T(8,128)(2,1)}, u32[]{:S(2)}) copy-start(bf16[352,1024]{1,0:T(8,128)(2,1)} %param.35) | copy-start | bytes 2162692
  7.2 5.3 %copy-start.4 = (bf16[1,512,128]{2,1,0:T(8,128)(2,1)S(1)}, bf16[1,512,128]{2,1,0:T(8,128)(2,1)}, u32[]{:S(2)}) copy-start(bf16[1,512,128]{2,1,0:T(8,128)(2,1)} %param.22) | copy-start | bytes 393220
  7.2 6.0 %copy-start.7 = (bf16[1,512,128]{2,1,0:T(8,128)(2,1)S(1)}, bf16[1,512,128]{2,1,0:T(8,128)(2,1)}, u32[]{:S(2)}) copy-start(bf16[1,512,128]{2,1,0:T(8,128)(2,1)} %param.21) | copy-start | bytes 393220
  7.2 6.9 %copy-start.3 = (bf16[1,2048,128]{2,1,0:T(8,128)(2,1)S(1)}, bf16[1,2048,128]{2,1,0:T(8,128)(2,1)}, u32[]{:S(2)}) copy-start(bf16[1,2048,128]{2,1,0:T(8,128)(2,1)} %param.25) | copy-start | bytes 1572868
  7.2 70.9 %all-gather.6.cloned.1.call-start = ((), (), s32[]{:S(2)}) async-start(), calls=%async_computation.9 | async-start | bytes 2359296 | tf_op jit(solution)/shard_map/all_gather | solution.py:125
  9.6 5.5 %copy-start.5 = (bf16[1,512,128]{2,1,0:T(8,128)(2,1)S(1)}, bf16[1,512,128]{2,1,0:T(8,128)(2,1)}, u32[]{:S(2)}) copy-start(bf16[1,512,128]{2,1,0:T(8,128)(2,1)} %param.23) | copy-start | bytes 393220
  31.6 7.5 %copy-start.2 = (bf16[1,2048,128]{2,1,0:T(8,128)(2,1)S(1)}, bf16[1,2048,128]{2,1,0:T(8,128)(2,1)}, u32[]{:S(2)}) copy-start(bf16[1,2048,128]{2,1,0:T(8,128)(2,1)} %param.24) | copy-start | bytes 1572868
  34.4 11.0 %all-to-all-start = ((bf16[8,2,4096]{2,1,0:T(2,128)(2,1)}), bf16[8,2,4096]{2,1,0:T(2,128)(2,1)S(1)}, u32[]{:S(2)}, u32[]{:S(2)}) async-start(bf16[8,2,4096]{2,1,0:T(2,128)(2,1)} %reshape.548), calls=%async_computation | async-start | bytes 262144 | tf_op jit(solution)/shard_map/all_to_all | solution.py:126
  39.1 11.2 %copy-start.9 = (s32[1,64,2]{1,2,0:T(2,128)S(1)}, s32[1,64,2]{1,2,0:T(2,128)}, u32[]{:S(2)}) copy-start(s32[1,64,2]{1,2,0:T(2,128)} %param.36) | copy-start | bytes 1540
  39.1 11.7 %copy-start.11 = (s32[1,64,2]{1,2,0:T(2,128)S(1)}, s32[1,64,2]{1,2,0:T(2,128)}, u32[]{:S(2)}) copy-start(s32[1,64,2]{1,2,0:T(2,128)} %param.37) | copy-start | bytes 1540
  45.4 16.5 %all-to-all-start.2 = ((bf16[1,8,320,128]{3,2,0,1:T(8,128)(2,1)}), bf16[1,8,320,128]{3,2,0,1:T(8,128)(2,1)S(1)}, u32[]{:S(2)}, u32[]{:S(2)}) async-start(bf16[1,8,320,128]{3,2,0,1:T(8,128)(2,1)} %bitcast.24), calls=%async_computation.2 | async-start | bytes 1310720 | tf_op jit(solution)/shard_map/all_to_all | solution.py:79
  62.0 15.2 %all-to-all-start.1 = ((bf16[1,8,320,128]{3,2,0,1:T(8,128)(2,1)}), bf16[1,8,320,128]{3,2,0,1:T(8,128)(2,1)S(1)}, u32[]{:S(2)}, u32[]{:S(2)}) async-start(bf16[1,8,320,128]{3,2,0,1:T(8,128)(2,1)} %bitcast.22), calls=%async_computation.1 | async-start | bytes 1310720 | tf_op jit(solution)/shard_map/all_to_all | solution.py:79
  65.5 73.1 %all-gather.8.cloned.1.call-start = ((), (), s32[]{:S(2)}) async-start(), calls=%async_computation.10 | async-start | bytes 2621440 | tf_op jit(solution)/shard_map/all_gather | solution.py:160
  66.1 12.0 %copy-start.6 = (bf16[1,64,1024]{2,1,0:T(8,128)(2,1)S(1)}, bf16[1,64,1024]{2,1,0:T(8,128)(2,1)}, u32[]{:S(2)}) copy-start(bf16[1,64,1024]{2,1,0:T(8,128)(2,1)} %param.20) | copy-start | bytes 393220
  78.1 2.2 copy-start.10
  110.2 80.2 %all-gather.10.cloned.1.call-start = ((), (), s32[]{:S(2)}) async-start(), calls=%async_computation.11 | async-start | bytes 2621440 | tf_op jit(solution)/shard_map/all_gather | solution.py:160
  138.6 3.9 %copy-start.12 = (bf16[128,8,1024]{2,1,0:T(8,128)(2,1)S(1)}, bf16[128,8,1024]{2,1,0:T(8,128)(2,1)}, u32[]{:S(2)}) copy-start(bf16[128,8,1024]{2,1,0:T(8,128)(2,1)} %all-gather.8.cloned.1.call-done) | copy-start | bytes 6291460
  147.7 52.3 %all-to-all-start.4 = ((bf16[4,32,8,1024]{3,2,1,0:T(8,128)(2,1)}), bf16[4,32,8,1024]{3,2,1,0:T(8,128)(2,1)S(1)}, u32[]{:S(2)}, u32[]{:S(2)}) async-start(bf16[4,32,8,1024]{3,2,1,0:T(8,128)(2,1)} %bitcast.143), calls=%async_computation.4 | async-start | bytes 4194304 | tf_op jit(solution)/shard_map/all_to_all | solution.py:170
  200.0 1.3 copy-start.1
  201.3 32.8 %all-to-all-start.7 = ((bf16[4,32,8,1024]{3,2,1,0:T(8,128)(2,1)}), bf16[4,32,8,1024]{3,2,1,0:T(8,128)(2,1)S(1)}, u32[]{:S(2)}, u32[]{:S(2)}) async-start(bf16[4,32,8,1024]{3,2,1,0:T(8,128)(2,1)} %bitcast.144), calls=%async_computation.7 | async-start | bytes 4194304 | tf_op jit(solution)/shard_map/all_to_all | solution.py:170
  234.1 26.0 %all-to-all-start.5 = ((bf16[32,8,1024]{2,1,0:T(8,128)(2,1)}), bf16[32,8,1024]{2,1,0:T(8,128)(2,1)}, u32[]{:S(2)}, u32[]{:S(2)}) async-start(bf16[32,8,1024]{2,1,0:T(8,128)(2,1)} %reduce_sum.90), calls=%async_computation.5 | async-start | bytes 1048576 | tf_op jit(solution)/shard_map/all_to_all | solution.py:172
  244.6 21.6 %copy-start.8 = (bf16[1024,16]{0,1:T(8,128)(2,1)S(1)}, bf16[1024,16]{0,1:T(8,128)(2,1)}, u32[]{:S(2)}) copy-start(bf16[1024,16]{0,1:T(8,128)(2,1)} %param.32) | copy-start | bytes 98308
  260.2 21.4 %all-to-all-start.8 = ((bf16[32,8,1024]{2,1,0:T(8,128)(2,1)}), bf16[32,8,1024]{2,1,0:T(8,128)(2,1)S(1)}, u32[]{:S(2)}, u32[]{:S(2)}) async-start(bf16[32,8,1024]{2,1,0:T(8,128)(2,1)} %reduce_sum.92), calls=%async_computation.8 | async-start | bytes 1048576 | tf_op jit(solution)/shard_map/all_to_all | solution.py:172
Sparse Core Ops, SparseCore 0:
  9.9 30.7 all-gather.5
  110.4 28.2 all-gather.7
  140.4 49.9 all-gather.9

commit v2 on v0

--- a/solution.py
+++ b/solution.py
@@ -80,7 +80,7 @@
     return jnp.transpose(got, (0, 2, 1, 3)).reshape(lead, rows // groups, groups * width)
 
 
-def body(
+def layer(
     x_tokens,
     query,
     key_new,
@@ -106,19 +106,18 @@
     new_values = to_positions(grown_values)
     chosen_keys = jnp.take(prefix_keys, group_ids, axis=0)
     chosen_values = jnp.take(prefix_values, group_ids, axis=0)
-    attended = lax.map(
-        attend_request,
+    attended = attend_request(
         (
-            query,
-            key_new,
-            value_new,
-            cache_keys,
-            cache_values,
-            chosen_keys,
-            chosen_values,
-            history_len,
-        ),
-    )
+            query[0],
+            key_new[0],
+            value_new[0],
+            cache_keys[0],
+            cache_values[0],
+            chosen_keys[0],
+            chosen_values[0],
+            history_len[0],
+        )
+    )[None]
     requests_here = x_tokens.shape[0]
     rows_here = x_tokens.shape[1]
     width = x_tokens.shape[2]
@@ -148,24 +147,31 @@
     )
     buffer = jnp.zeros((experts * slots_here, width), jnp.bfloat16).at[places].set(sent_rows)
     holders = lax.axis_size("req") // experts
-    outgoing = jnp.repeat(buffer.reshape(experts, slots_here, width), holders, axis=0)
+    pair = [(r, r ^ 1) for r in range(lax.axis_size("req"))]
+    other_gate = lax.ppermute(expert_gate, "req", pair)
+    other_up = lax.ppermute(expert_up, "req", pair)
+    other_down = lax.ppermute(expert_down, "req", pair)
+    both_gate = jnp.stack([expert_gate, other_gate])
+    both_up = jnp.stack([expert_up, other_up])
+    both_down = jnp.stack([expert_down, other_down])
+    step = slots_here // holders
+    outgoing = buffer.reshape(experts * holders, step, width)
     arrived = lax.all_to_all(outgoing, "req", split_axis=0, concat_axis=0, tiled=True)
     gathered = lax.all_gather(arrived, "head", axis=0, tiled=False)
     flat_rows = gathered.reshape(-1, width)
-    gate_val = jnp.dot(flat_rows, expert_gate, preferred_element_type=jnp.float32)
-    up_val = jnp.dot(flat_rows, expert_up, preferred_element_type=jnp.float32)
+    gate_val = jnp.einsum("nd,sdf->snf", flat_rows, both_gate, preferred_element_type=jnp.float32)
+    up_val = jnp.einsum("nd,sdf->snf", flat_rows, both_up, preferred_element_type=jnp.float32)
     hidden = (jax.nn.gelu(gate_val, approximate=True) * up_val).astype(jnp.bfloat16)
-    partial = (
-        jnp.dot(hidden, expert_down, preferred_element_type=jnp.float32)
-        .astype(jnp.bfloat16)
-        .reshape(gathered.shape)
-    )
-    shard_parts = lax.all_to_all(partial, "head", split_axis=0, concat_axis=0, tiled=True)
-    half_sum = jnp.sum(shard_parts.astype(jnp.float32), axis=0).astype(jnp.bfloat16)
-    returned = lax.all_to_all(half_sum, "req", split_axis=0, concat_axis=0, tiled=True)
-    combined = jnp.sum(
-        returned.reshape(experts, holders, slots_here, width), axis=1, dtype=jnp.float32
-    ).reshape(experts * slots_here, width)
+    blocks_out = jnp.einsum(
+        "snf,sfd->snd", hidden, both_down, preferred_element_type=jnp.float32
+    ).astype(jnp.bfloat16)
+    pair_sum = jnp.sum(blocks_out.astype(jnp.float32), axis=0).astype(jnp.bfloat16)
+    shard_parts = lax.all_to_all(
+        pair_sum.reshape(gathered.shape), "head", split_axis=0, concat_axis=0, tiled=True
+    )
+    full_sum = jnp.sum(shard_parts.astype(jnp.float32), axis=0).astype(jnp.bfloat16)
+    returned = lax.all_to_all(full_sum, "req", split_axis=0, concat_axis=0, tiled=True)
+    combined = returned.astype(jnp.float32).reshape(experts * slots_here, width)
     picked = jnp.take(combined, places, axis=0).reshape(-1, 2, width)
     mixture = jnp.sum(picked * gate_weights[:, :, None], axis=1)
     y_out = (
@@ -178,7 +184,7 @@
 
 def solution(mesh):
     return jax.shard_map(
-        body,
+        layer,
         mesh=mesh,
         in_specs=(
             P("req", ("head", "blk"), None),

time: 274 us -> 212 us (0.77)
  blocking collectives: 94 us -> 56.1 us
  waiting for transfers between devices: 79 us -> 56.9 us
  other arithmetic: 21.2 us -> 16.4 us
    all_to_all x2, blocking collectives: 94 us -> 56.1 us  [the longest x1 28.2 us: layer(): lax.all_to_all(outgoing, 'req', split_axis=0, concat_axis=0, tiled=True)]
    all_gather x2, waiting for transfers between devices: 42.9 us -> 16.2 us  [the longest x1 16.2 us: layer(): gathered = lax.all_gather(arrived, 'head', axis=0, tiled=False)]
    ppermute x0 -> x3, waiting for transfers between devices: none -> 12.7 us  [the longest x1 6.72 us: layer(): other_down = lax.ppermute(expert_down, 'req', pair)]
    all_to_all x2, waiting for transfers between devices: 28.3 us -> 17.6 us  [the longest x1 12.8 us: layer(): lax.all_to_all(full_sum, 'req', split_axis=0, concat_axis=0, tiled=True)]
    reduce_sum x4 -> x3, other arithmetic: 5.63 us -> 2.3 us  [the longest x1 1.31 us: layer(): jnp.sum(shard_parts.astype(jnp.float32), axis=0).astype(jnp.bfloat16)]
    ppermute x0 -> x3, starting transfers between devices: none -> 3.28 us  [the longest x1 1.26 us: layer(): other_gate = lax.ppermute(expert_gate, 'req', pair)]
  transfers between devices with their start and end apart: 6 -> 9, of which waited for: 4 -> 6; matrix products, arithmetic and copies ran while one was open for 21% -> 25% of each run, Pallas kernels for 0% -> 0%
where the time goes in v2:
time: 212 us
  waiting for transfers between devices  56.9 us (27%)
  blocking collectives  56.1 us (26%)
  matrix products  29.5 us (14%)
  starting transfers between devices  22.3 us (11%)
  other arithmetic  16.4 us (8%)
  between operations  15.8 us (7%)
  local copies, waits for them, and re-layouts  14.5 us (7%)
    all_to_all x1, blocking collectives, layer(): lax.all_to_all(outgoing, 'req', split_axis=0, concat_axis=0, tiled=True)  28.2 us
    all_to_all x1, blocking collectives, layer(): lax.all_to_all(pair_sum.reshape(gathered.shape), 'head', split_axis=0, co...  27.9 us
    all_gather x1, waiting for transfers between devices, layer(): gathered = lax.all_gather(arrived, 'head', axis=0, tiled=False)  16.2 us
    all_to_all x1, waiting for transfers between devices, layer(): lax.all_to_all(full_sum, 'req', split_axis=0, concat_axis=0, tiled=True)  12.8 us
    all_to_all x2, waiting for transfers between devices, to_positions(): lax.all_to_all(parts, ('head', 'blk'), split_axis=1, concat_axis=1, tiled...  9.72 us
    sub x1, matrix products, attend_request(): weights = jnp.where(visible[None], jnp.exp(scores - highest), 0.0)  8.82 us
    dot_general x1, matrix products, layer(): jnp.einsum('snf,sfd->snd', hidden, both_down, preferred_element_type=jnp....  8.72 us
    all_to_all x1, starting transfers between devices, layer(): lax.all_to_all(full_sum, 'req', split_axis=0, concat_axis=0, tiled=True)  7.27 us
  transfers between devices with their start and end apart: 9, of which 6 were waited for; matrix products, arithmetic and copies ran while one was open for 25% of the time, Pallas kernels for 0%

profile of v2, /device:TPU:4, one launch (start us, length us, event | category | flops | bytes accessed | tf_op | source)
XLA Modules:
  0.0 211.5 jit_solution(5736043149874825518)
XLA Ops:
  8.6 1.0 dynamic-slice_select_fusion
  11.0 1.2 copy.101
  15.6 2.8 %fusion.10 = pred[512,3072]{0,1:T(8,128)(4,1)S(1)} fusion(s32[3072]{0:T(1024)S(1)} %iota_add_fusion, pred[3072]{0:T(1024)(128)(4,1)S(1)} %get-tuple-element.43, pred[3072]{0:T(1024)(128)(4,1)S(1)} %get-tuple-element.44), kind=kLoop, calls=%fused_computation.16 | loop fusion | flops 4718592 | bytes 1591296 | tf_op jit(solution)/shard_map/or | solution.py:45
  18.4 8.8 %fusion.101 = (f32[2,512]{1,0:T(2,128)S(1)}, bf16[2,512,3072]{1,2,0:T(8,128)(2,1)}) fusion(pred[512,3072]{0,1:T(8,128)(4,1)S(1)} %fusion.10, bf16[512,2,64]{0,2,1:T(8,128)(2,1)} %bitcast.146, bf16[512,2,64]{0,2,1:T(8,128)(2,1)} %bitcast.145, bf16[2048,2,64]{0,2,1:T(8,128)(2,1)S(1)} %bitcast.140, bf16[512,2,64]{0,2,1:T(8,128)(2,1)} %bitcast.142), kind=kOutput, calls=%fused_computation.127 | convolution fusion | flops 832048128 | bytes 8785920 | tf_op jit(solution)/shard_map/sub | solution.py:53
  27.3 4.1 %fusion.55 = bf16[512,2,64]{0,2,1:T(8,128)(2,1)S(1)} fusion(bf16[2,512,3072]{1,2,0:T(8,128)(2,1)} %get-tuple-element.40, bf16[512,2,64]{0,2,1:T(8,128)(2,1)} %bitcast.144, bf16[2048,2,64]{0,2,1:T(8,128)(2,1)S(1)} %bitcast.139, bf16[512,2,64]{0,2,1:T(8,128)(2,1)} %bitcast.143, f32[512,2]{0,1:T(2,128)S(1)} %bitcast.150), kind=kOutput, calls=%fused_computation.55 | convolution fusion | flops 405143552 | bytes 7213056 | tf_op jit(solution)/shard_map/hqk,khd->qhd/dot_general | solution.py:56
  32.1 1.4 reduce.4
  34.2 4.5 %all-to-all-start = ((bf16[8,2,4096]{2,1,0:T(2,128)(2,1)}), bf16[8,2,4096]{2,1,0:T(2,128)(2,1)S(1)}, u32[]{:S(2)}, u32[]{:S(2)}) async-start(bf16[8,2,4096]{2,1,0:T(2,128)(2,1)} %reshape.520), calls=%async_computation | async-start | bytes 262144 | tf_op jit(solution)/shard_map/all_to_all | solution.py:125
  40.1 4.8 %all-to-all-done = bf16[8,2,4096]{2,1,0:T(2,128)(2,1)S(1)} async-done(((bf16[8,2,4096]{2,1,0:T(2,128)(2,1)}), bf16[8,2,4096]{2,1,0:T(2,128)(2,1)S(1)}, u32[]{:S(2)}, u32[]{:S(2)}) %all-to-all-start) | async-done | bytes 131104 | tf_op jit(solution)/shard_map/all_to_all | solution.py:125
  45.2 2.2 %multiply_reduce_fusion.1 = (f32[64]{0:T(128)S(1)}, f32[1,64,1024]{2,1,0:T(8,128)S(1)}) fusion(bf16[1024,1024]{1,0:T(8,128)(2,1)} %all-gather.4.cloned.1.call-done, bf16[8,8,8,128]{3,2,1,0:T(8,128)(2,1)S(1)} %bitcast.137, bf16[1,64,1024]{2,1,0:T(8,128)(2,1)S(1)} %copy-done.9), kind=kOutput, calls=%fused_computation.78 | convolution fusion | flops 134479808 | bytes 2621696 | tf_op jit(solution)/shard_map/rqf,fd->rqd/dot_general | solution.py:126
  49.1 1.4 scatter_custom_fusion
  50.5 28.2 %all_to_all.40 = bf16[32,8,1024]{2,1,0:T(8,128)(2,1)} all-to-all(bf16[32,8,1024]{2,1,0:T(8,128)(2,1)S(1)} %bitcast.134), channel_id=1, replica_groups=mesh['req'=32,'head'=4,'blk'=2] {'req'}, dimensions={0} | all-to-all | bytes 1048576 | tf_op jit(solution)/shard_map/all_to_all | solution.py:159
  78.7 1.3 collective-permute-start
  79.9 0.9 collective-permute-start.1
  80.8 1.2 collective-permute-start.2
  82.1 6.3 %fusion.68 = (bf16[1,2560,128]{2,1,0:T(8,128)(2,1)}, bf16[1,2560,128]{2,1,0:T(8,128)(2,1)}) fusion(s32[]{:T(128)} %bitcast.41, bf16[1,2048,128]{2,1,0:T(8,128)(2,1)S(1)} %broadcast.272, bf16[1,512,128]{2,1,0:T(8,128)(2,1)S(1)} %copy-done.8, bf16[1,2048,128]{2,1,0:T(8,128)(2,1)S(1)} %copy-done.4, pred[2560]{0:T(1024)(128)(4,1)S(1)} %iota_compare_fusion.4, ...), kind=kLoop, calls=%fused_computation.67 | loop fusion | flops 4587520 | bytes 3148292 | tf_op jit(solution)/shard_map/vmap(jit(_where))/select_n | solution.py:72
  88.4 3.5 %all-to-all-start.5 = ((bf16[1,8,320,128]{3,2,0,1:T(8,128)(2,1)}), bf16[1,8,320,128]{3,2,0,1:T(8,128)(2,1)S(1)}, u32[]{:S(2)}, u32[]{:S(2)}) async-start(bf16[1,8,320,128]{3,2,0,1:T(8,128)(2,1)} %bitcast.44), calls=%async_computation.5 | async-start | bytes 1310720 | tf_op jit(solution)/shard_map/all_to_all | solution.py:79
  91.9 5.9 %collective-permute-done = bf16[1024,352]{0,1:T(8,128)(2,1)} collective-permute-done((bf16[1024,352]{0,1:T(8,128)(2,1)S(1)}, bf16[1024,352]{0,1:T(8,128)(2,1)}, u32[]{:S(2)}, u32[]{:S(2)}) %collective-permute-start) | collective-permute-done | bytes 720928 | tf_op jit(solution)/shard_map/ppermute | solution.py:151
  97.9 16.2 %all-gather.6.cloned.1.call-done = bf16[128,8,1024]{2,1,0:T(8,128)(2,1)} async-done(((bf16[32,8,1024]{2,1,0:T(8,128)(2,1)}), bf16[128,8,1024]{2,1,0:T(8,128)(2,1)}) %all-gather.6.cloned.1.call-update) | async-done | bytes 2097168 | tf_op jit(solution)/shard_map/all_gather | solution.py:160
  114.1 5.4 %fusion.23 = f32[2,352,1024]{2,1,0:T(8,128)} fusion(bf16[128,8,1024]{2,1,0:T(8,128)(2,1)} %all-gather.6.cloned.1.call-done, bf16[1,1024,352]{1,2,0:T(8,128)(2,1)} %bitcast.22, bf16[1,1024,352]{1,2,0:T(8,128)(2,1)} %bitcast.147), kind=kOutput, calls=%fused_computation.31 | convolution fusion | flops 1477115904 | bytes 6422528 | tf_op jit(solution)/shard_map/nd,sdf->snf/dot_general | solution.py:162
  119.5 6.7 %collective-permute-done.2 = bf16[352,1024]{1,0:T(8,128)(2,1)} collective-permute-done((bf16[352,1024]{1,0:T(8,128)(2,1)}, bf16[352,1024]{1,0:T(8,128)(2,1)}, u32[]{:S(2)}, u32[]{:S(2)}) %collective-permute-start.2) | collective-permute-done | bytes 720928 | tf_op jit(solution)/shard_map/ppermute | solution.py:153
  126.2 8.7 %convert_reduce_fusion = bf16[1024,1024]{1,0:T(8,128)(2,1)} fusion(f32[2,352,1024]{2,1,0:T(8,128)} %fusion.23, bf16[128,8,1024]{2,1,0:T(8,128)(2,1)S(1)} %copy-done.14, bf16[1,1024,352]{1,2,0:T(8,128)(2,1)} %bitcast.31, bf16[1,1024,352]{1,2,0:T(8,128)(2,1)} %bitcast.148, bf16[1,352,1024]{2,1,0:T(8,128)(2,1)} %bitcast.35, bf16[1,352,1024]{2,1,0:T(8,128)(2,1)} %bitcast.149), kind=kOutput, calls=%fused_computation.19 | convolution fusion | flops 2964586496 | bytes 9961472 | tf_op jit(solution)/shard_map/snf,sfd->snd/dot_general | solution.py:165
  135.0 27.9 %all_to_all.41 = bf16[4,32,8,1024]{3,2,1,0:T(8,128)(2,1)S(1)} all-to-all(bf16[4,32,8,1024]{3,2,1,0:T(8,128)(2,1)} %bitcast.133), channel_id=1, replica_groups=mesh['req'=32,'head'=4,'blk'=2] {'head'}, dimensions={0} | all-to-all | bytes 4194304 | tf_op jit(solution)/shard_map/all_to_all | solution.py:169
  162.9 3.5 %all-to-all-start.4 = ((bf16[1,8,320,128]{3,2,0,1:T(8,128)(2,1)}), bf16[1,8,320,128]{3,2,0,1:T(8,128)(2,1)S(1)}, u32[]{:S(2)}, u32[]{:S(2)}) async-start(bf16[1,8,320,128]{3,2,0,1:T(8,128)(2,1)} %bitcast.132), calls=%async_computation.4 | async-start | bytes 1310720 | tf_op jit(solution)/shard_map/all_to_all | solution.py:79
  167.1 1.3 reduce_sum.72
  168.4 9.7 %all-to-all-done.4 = bf16[1,8,320,128]{3,2,0,1:T(8,128)(2,1)S(1)} async-done(((bf16[1,8,320,128]{3,2,0,1:T(8,128)(2,1)}), bf16[1,8,320,128]{3,2,0,1:T(8,128)(2,1)S(1)}, u32[]{:S(2)}, u32[]{:S(2)}) %all-to-all-start.4) | async-done | bytes 655392 | tf_op jit(solution)/shard_map/all_to_all | solution.py:79
  178.1 7.3 %all-to-all-start.3 = ((bf16[32,8,1024]{2,1,0:T(8,128)(2,1)}), bf16[32,8,1024]{2,1,0:T(8,128)(2,1)S(1)}, u32[]{:S(2)}, u32[]{:S(2)}) async-start(bf16[32,8,1024]{2,1,0:T(8,128)(2,1)} %reduce_sum.72), calls=%async_computation.3 | async-start | bytes 1048576 | tf_op jit(solution)/shard_map/all_to_all | solution.py:173
  185.4 0.9 copy_bitcast_fusion
  186.3 0.9 copy_bitcast_fusion.1
  187.4 1.3 gather_fusion.1
  189.1 12.8 %all-to-all-done.3 = bf16[32,8,1024]{2,1,0:T(8,128)(2,1)S(1)} async-done(((bf16[32,8,1024]{2,1,0:T(8,128)(2,1)}), bf16[32,8,1024]{2,1,0:T(8,128)(2,1)S(1)}, u32[]{:S(2)}, u32[]{:S(2)}) %all-to-all-start.3) | async-done | bytes 524320 | tf_op jit(solution)/shard_map/all_to_all | solution.py:173
  202.0 0.8 gather_fusion
  203.2 0.8 multiply_reduce_fusion
  (89 shorter events, 11.6 us)
Async XLA Ops:
  7.2 180.1 %copy-start = (bf16[1024,16]{0,1:T(8,128)(2,1)S(1)}, bf16[1024,16]{0,1:T(8,128)(2,1)}, u32[]{:S(2)}) copy-start(bf16[1024,16]{0,1:T(8,128)(2,1)} %param.32) | copy-start | bytes 98308
  7.2 5.1 %copy-start.7 = (bf16[1,512,128]{2,1,0:T(8,128)(2,1)S(1)}, bf16[1,512,128]{2,1,0:T(8,128)(2,1)}, u32[]{:S(2)}) copy-start(bf16[1,512,128]{2,1,0:T(8,128)(2,1)} %param.22) | copy-start | bytes 393220
  7.2 5.9 %copy-start.10 = (bf16[1,512,128]{2,1,0:T(8,128)(2,1)S(1)}, bf16[1,512,128]{2,1,0:T(8,128)(2,1)}, u32[]{:S(2)}) copy-start(bf16[1,512,128]{2,1,0:T(8,128)(2,1)} %param.21) | copy-start | bytes 393220
  7.2 7.4 %copy-start.4 = (bf16[1,2048,128]{2,1,0:T(8,128)(2,1)S(1)}, bf16[1,2048,128]{2,1,0:T(8,128)(2,1)}, u32[]{:S(2)}) copy-start(bf16[1,2048,128]{2,1,0:T(8,128)(2,1)} %param.25) | copy-start | bytes 1572868
  7.2 7.6 %copy-start.8 = (bf16[1,512,128]{2,1,0:T(8,128)(2,1)S(1)}, bf16[1,512,128]{2,1,0:T(8,128)(2,1)}, u32[]{:S(2)}) copy-start(bf16[1,512,128]{2,1,0:T(8,128)(2,1)} %param.23) | copy-start | bytes 393220
  7.2 37.9 %all-gather.4.cloned.1.call-start = ((), (), s32[]{:S(2)}) async-start(), calls=%async_computation.6 | async-start | bytes 2359296 | tf_op jit(solution)/shard_map/all_gather | solution.py:124
  27.3 11.6 %copy-start.11 = (s32[1,64,2]{1,2,0:T(2,128)S(1)}, s32[1,64,2]{1,2,0:T(2,128)}, u32[]{:S(2)}) copy-start(s32[1,64,2]{1,2,0:T(2,128)} %param.36) | copy-start | bytes 1540
  27.3 12.1 %copy-start.13 = (s32[1,64,2]{1,2,0:T(2,128)S(1)}, s32[1,64,2]{1,2,0:T(2,128)}, u32[]{:S(2)}) copy-start(s32[1,64,2]{1,2,0:T(2,128)} %param.37) | copy-start | bytes 1540
  31.4 13.7 %copy-start.9 = (bf16[1,64,1024]{2,1,0:T(8,128)(2,1)S(1)}, bf16[1,64,1024]{2,1,0:T(8,128)(2,1)}, u32[]{:S(2)}) copy-start(bf16[1,64,1024]{2,1,0:T(8,128)(2,1)} %param.20) | copy-start | bytes 393220
  34.2 10.7 %all-to-all-start = ((bf16[8,2,4096]{2,1,0:T(2,128)(2,1)}), bf16[8,2,4096]{2,1,0:T(2,128)(2,1)S(1)}, u32[]{:S(2)}, u32[]{:S(2)}) async-start(bf16[8,2,4096]{2,1,0:T(2,128)(2,1)} %reshape.520), calls=%async_computation | async-start | bytes 262144 | tf_op jit(solution)/shard_map/all_to_all | solution.py:125
  38.8 9.3 %copy-start.12 = (f32[1024]{0:T(1024)S(1)}, f32[1024]{0:T(1024)}, u32[]{:S(2)}) copy-start(f32[1024]{0:T(1024)} %param.31) | copy-start | bytes 12292
  38.8 75.3 %all-gather.6.cloned.1.call-start = ((), (), s32[]{:S(2)}) async-start(), calls=%async_computation.7 | async-start | bytes 2621440 | tf_op jit(solution)/shard_map/all_gather | solution.py:160
  47.4 0.7 copy-start.1
  47.4 31.3 %copy-start.15 = (bf16[1024,352]{0,1:T(8,128)(2,1)S(1)}, bf16[1024,352]{0,1:T(8,128)(2,1)}, u32[]{:S(2)}) copy-start(bf16[1024,352]{0,1:T(8,128)(2,1)} %param.33) | copy-start | bytes 2162692
  48.1 34.0 %copy-start.3 = (bf16[1,2048,128]{2,1,0:T(8,128)(2,1)S(1)}, bf16[1,2048,128]{2,1,0:T(8,128)(2,1)}, u32[]{:S(2)}) copy-start(bf16[1,2048,128]{2,1,0:T(8,128)(2,1)} %param.24) | copy-start | bytes 1572868
  48.2 0.7 copy-start.5
  78.7 19.2 %collective-permute-start = (bf16[1024,352]{0,1:T(8,128)(2,1)S(1)}, bf16[1024,352]{0,1:T(8,128)(2,1)}, u32[]{:S(2)}, u32[]{:S(2)}) collective-permute-start(bf16[1024,352]{0,1:T(8,128)(2,1)S(1)} %copy-done.15), channel_id=1, source_target_pairs={{0,8},{8,0},{16,24},{24,16},{32,40},{40,32},{48,56},{56,48},{64,72... | collective-permute-start | bytes 2162696 | tf_op jit(solution)/shard_map/ppermute | solution.py:151
  79.9 39.6 %collective-permute-start.1 = (bf16[1024,352]{0,1:T(8,128)(2,1)}, bf16[1024,352]{0,1:T(8,128)(2,1)}, u32[]{:S(2)}, u32[]{:S(2)}) collective-permute-start(bf16[1024,352]{0,1:T(8,128)(2,1)} %param.34), channel_id=1, source_target_pairs={{0,8},{8,0},{16,24},{24,16},{32,40},{40,32},{48,56},{56,48},{64,72... | collective-permute-start | bytes 2162696 | tf_op jit(solution)/shard_map/ppermute | solution.py:152
  80.8 45.5 %collective-permute-start.2 = (bf16[352,1024]{1,0:T(8,128)(2,1)}, bf16[352,1024]{1,0:T(8,128)(2,1)}, u32[]{:S(2)}, u32[]{:S(2)}) collective-permute-start(bf16[352,1024]{1,0:T(8,128)(2,1)} %param.35), channel_id=1, source_target_pairs={{0,8},{8,0},{16,24},{24,16},{32,40},{40,32},{48,56},{56,48},{64,72... | collective-permute-start | bytes 2162696 | tf_op jit(solution)/shard_map/ppermute | solution.py:153
  88.4 46.6 %all-to-all-start.5 = ((bf16[1,8,320,128]{3,2,0,1:T(8,128)(2,1)}), bf16[1,8,320,128]{3,2,0,1:T(8,128)(2,1)S(1)}, u32[]{:S(2)}, u32[]{:S(2)}) async-start(bf16[1,8,320,128]{3,2,0,1:T(8,128)(2,1)} %bitcast.44), calls=%async_computation.5 | async-start | bytes 1310720 | tf_op jit(solution)/shard_map/all_to_all | solution.py:79
  114.1 12.2 %copy-start.14 = (bf16[128,8,1024]{2,1,0:T(8,128)(2,1)S(1)}, bf16[128,8,1024]{2,1,0:T(8,128)(2,1)}, u32[]{:S(2)}) copy-start(bf16[128,8,1024]{2,1,0:T(8,128)(2,1)} %all-gather.6.cloned.1.call-done) | copy-start | bytes 6291460
  162.9 15.2 %all-to-all-start.4 = ((bf16[1,8,320,128]{3,2,0,1:T(8,128)(2,1)}), bf16[1,8,320,128]{3,2,0,1:T(8,128)(2,1)S(1)}, u32[]{:S(2)}, u32[]{:S(2)}) async-start(bf16[1,8,320,128]{3,2,0,1:T(8,128)(2,1)} %bitcast.132), calls=%async_computation.4 | async-start | bytes 1310720 | tf_op jit(solution)/shard_map/all_to_all | solution.py:79
  168.4 18.9 %copy-start.6 = (bf16[64,1024]{1,0:T(8,128)(2,1)S(1)}, bf16[64,1024]{1,0:T(8,128)(2,1)}, u32[]{:S(2)}) copy-start(bf16[64,1024]{1,0:T(8,128)(2,1)} %copy-done.5) | copy-start | bytes 393220
  178.1 23.8 %all-to-all-start.3 = ((bf16[32,8,1024]{2,1,0:T(8,128)(2,1)}), bf16[32,8,1024]{2,1,0:T(8,128)(2,1)S(1)}, u32[]{:S(2)}, u32[]{:S(2)}) async-start(bf16[32,8,1024]{2,1,0:T(8,128)(2,1)} %reduce_sum.72), calls=%async_computation.3 | async-start | bytes 1048576 | tf_op jit(solution)/shard_map/all_to_all | solution.py:173
  202.0 2.0 copy-start.2
Sparse Core Ops, SparseCore 0:
  9.9 30.8 all-gather.3
  78.8 35.2 all-gather.5

commit v3 on v2

--- a/solution.py
+++ b/solution.py
@@ -72,12 +72,22 @@
     return jnp.where((span < length)[:, None], padded_cache, shifted)
 
 
-def to_positions(grown):
+def to_positions(grown_keys, grown_values):
     groups = lax.axis_size(("head", "blk"))
-    lead, rows, width = grown.shape
-    parts = grown.reshape(lead, groups, rows // groups, width)
-    got = lax.all_to_all(parts, ("head", "blk"), split_axis=1, concat_axis=1, tiled=True)
-    return jnp.transpose(got, (0, 2, 1, 3)).reshape(lead, rows // groups, groups * width)
+    me = lax.axis_index(("head", "blk"))
+    lead, rows, width = grown_keys.shape
+    span = rows // groups
+    parts = jnp.stack([grown_keys[0], grown_values[0]]).reshape(2, groups, span, width)
+    blocks = [lax.dynamic_index_in_dim(parts, me, axis=1, keepdims=False)]
+    for k in range(1, groups):
+        block = lax.dynamic_index_in_dim(parts, (me + k) % groups, axis=1, keepdims=False)
+        perm = [(i, (i + k) % groups) for i in range(groups)]
+        blocks.append(lax.ppermute(block, ("head", "blk"), perm))
+    stacked = jnp.stack(blocks, axis=1)
+    order = (me - jnp.arange(groups)) % groups
+    by_source = jnp.take(stacked, order, axis=1)
+    joined = jnp.transpose(by_source, (0, 2, 1, 3)).reshape(2, lead, span, groups * width)
+    return joined[0], joined[1]
 
 
 def layer(
@@ -102,8 +112,7 @@
 ):
     grown_keys = jax.vmap(extend)(cache_keys, key_new, history_len)
     grown_values = jax.vmap(extend)(cache_values, value_new, history_len)
-    new_keys = to_positions(grown_keys)
-    new_values = to_positions(grown_values)
+    new_keys, new_values = to_positions(grown_keys, grown_values)
     chosen_keys = jnp.take(prefix_keys, group_ids, axis=0)
     chosen_values = jnp.take(prefix_values, group_ids, axis=0)
     attended = attend_request(

time: 212 us -> 215 us (1.014)
  blocking collectives: 56.1 us -> 28.2 us
  waiting for transfers between devices: 56.9 us -> 76.8 us
  local copies, waits for them, and re-layouts: 14.5 us -> 21.5 us
    all_to_all x1 -> x0, blocking collectives: 27.9 us -> none  [layer(): lax.all_to_all(pair_sum.reshape(gathered.shape), 'head', split_axis=0, co...]
    ppermute x0 -> x7, waiting for transfers between devices: none -> 24.1 us  [to_positions(): blocks.append(lax.ppermute(block, ('head', 'blk'), perm))]
    all_to_all x2 -> x1, waiting for transfers between devices: 9.72 us -> 0.01 us  [layer(): lax.all_to_all(pair_sum.reshape(gathered.shape), 'head', split_axis=0, co...]
    ppermute x0 -> x7, starting transfers between devices: none -> 6.12 us  [to_positions(): blocks.append(lax.ppermute(block, ('head', 'blk'), perm))]
    unnamed x42 -> x51, local copies, waits for them, and re-layouts: 6.62 us -> 11.4 us
    ppermute x1, waiting for transfers between devices: 6.72 us -> 11 us  [layer(): other_down = lax.ppermute(expert_down, 'req', pair)]
    all_gather x1, waiting for transfers between devices: 16.2 us -> 12.6 us  [layer(): gathered = lax.all_gather(arrived, 'head', axis=0, tiled=False)]
    all_to_all x2 -> x1, starting transfers between devices: 7.08 us -> 3.83 us  [layer(): lax.all_to_all(pair_sum.reshape(gathered.shape), 'head', split_axis=0, co...]
  transfers between devices with their start and end apart: 9 -> 15, of which waited for: 6 -> 7; matrix products, arithmetic and copies ran while one was open for 25% -> 28% of each run, Pallas kernels for 0% -> 0%
where the time goes in v3:
time: 215 us; the launch traced here: 213 us
  waiting for transfers between devices  76.8 us (36%)
  matrix products  29.5 us (14%)
  blocking collectives  28.2 us (13%)
  starting transfers between devices  23.3 us (11%)
  local copies, waits for them, and re-layouts  21.5 us (10%)
  other arithmetic  17.6 us (8%)
  between operations  16 us (7%)
    all_to_all x1, blocking collectives, layer(): lax.all_to_all(outgoing, 'req', split_axis=0, concat_axis=0, tiled=True)  28.2 us
    ppermute x7, waiting for transfers between devices, to_positions(): blocks.append(lax.ppermute(block, ('head', 'blk'), perm))  24.1 us
    all_to_all x1, waiting for transfers between devices, layer(): lax.all_to_all(full_sum, 'req', split_axis=0, concat_axis=0, tiled=True)  14.7 us
    all_gather x1, waiting for transfers between devices, layer(): gathered = lax.all_gather(arrived, 'head', axis=0, tiled=False)  12.6 us
    unnamed x51, local copies, waits for them, and re-layouts  11.4 us
    ppermute x1, waiting for transfers between devices, layer(): other_down = lax.ppermute(expert_down, 'req', pair)  11 us
    ppermute x1, waiting for transfers between devices, layer(): other_gate = lax.ppermute(expert_gate, 'req', pair)  8.96 us
    sub x1, matrix products, attend_request(): weights = jnp.where(visible[None], jnp.exp(scores - highest), 0.0)  8.81 us
  transfers between devices with their start and end apart: 15, of which 7 were waited for; matrix products, arithmetic and copies ran while one was open for 28% of the time, Pallas kernels for 0%

profile of v3, /device:TPU:4, one launch (start us, length us, event | category | flops | bytes accessed | tf_op | source)
XLA Modules:
  0.0 213.0 jit_solution(12628346555352052562)
XLA Ops:
  9.2 1.0 dynamic-slice_select_fusion
  11.0 1.2 copy.99
  15.6 2.8 %fusion.10 = pred[512,3072]{0,1:T(8,128)(4,1)S(1)} fusion(s32[3072]{0:T(1024)S(1)} %iota_add_fusion, pred[3072]{0:T(1024)(128)(4,1)S(1)} %get-tuple-element.53, pred[3072]{0:T(1024)(128)(4,1)S(1)} %get-tuple-element.54), kind=kLoop, calls=%fused_computation.17 | loop fusion | flops 4718592 | bytes 1591296 | tf_op jit(solution)/shard_map/or | solution.py:45
  18.4 8.8 %fusion.104 = (f32[2,512]{1,0:T(2,128)S(1)}, bf16[2,512,3072]{1,2,0:T(8,128)(2,1)}) fusion(pred[512,3072]{0,1:T(8,128)(4,1)S(1)} %fusion.10, bf16[512,2,64]{0,2,1:T(8,128)(2,1)} %bitcast.173, bf16[512,2,64]{0,2,1:T(8,128)(2,1)} %bitcast.172, bf16[2048,2,64]{0,2,1:T(8,128)(2,1)S(1)} %bitcast.167, bf16[512,2,64]{0,2,1:T(8,128)(2,1)} %bitcast.170), kind=kOutput, calls=%fused_computation.160 | convolution fusion | flops 832048128 | bytes 8785920 | tf_op jit(solution)/shard_map/sub | solution.py:53
  27.3 4.1 %fusion.55 = bf16[512,2,64]{0,2,1:T(8,128)(2,1)S(1)} fusion(bf16[2,512,3072]{1,2,0:T(8,128)(2,1)} %get-tuple-element.50, bf16[512,2,64]{0,2,1:T(8,128)(2,1)} %bitcast.171, bf16[2048,2,64]{0,2,1:T(8,128)(2,1)S(1)} %bitcast.166, bf16[512,2,64]{0,2,1:T(8,128)(2,1)} %bitcast.169, f32[512,2]{0,1:T(2,128)S(1)} %bitcast.176), kind=kOutput, calls=%fused_computation.58 | convolution fusion | flops 405143552 | bytes 7213056 | tf_op jit(solution)/shard_map/hqk,khd->qhd/dot_general | solution.py:56
  32.1 1.4 reduce.4
  34.2 4.5 %all-to-all-start = ((bf16[8,2,4096]{2,1,0:T(2,128)(2,1)}), bf16[8,2,4096]{2,1,0:T(2,128)(2,1)S(1)}, u32[]{:S(2)}, u32[]{:S(2)}) async-start(bf16[8,2,4096]{2,1,0:T(2,128)(2,1)} %reshape.575), calls=%async_computation | async-start | bytes 262144 | tf_op jit(solution)/shard_map/all_to_all | solution.py:134
  40.0 4.8 %all-to-all-done = bf16[8,2,4096]{2,1,0:T(2,128)(2,1)S(1)} async-done(((bf16[8,2,4096]{2,1,0:T(2,128)(2,1)}), bf16[8,2,4096]{2,1,0:T(2,128)(2,1)S(1)}, u32[]{:S(2)}, u32[]{:S(2)}) %all-to-all-start) | async-done | bytes 131104 | tf_op jit(solution)/shard_map/all_to_all | solution.py:134
  45.2 2.2 %multiply_reduce_fusion.1 = (f32[64]{0:T(128)S(1)}, f32[1,64,1024]{2,1,0:T(8,128)S(1)}) fusion(bf16[1024,1024]{1,0:T(8,128)(2,1)} %all-gather.4.cloned.1.call-done, bf16[8,8,8,128]{3,2,1,0:T(8,128)(2,1)S(1)} %bitcast.164, bf16[1,64,1024]{2,1,0:T(8,128)(2,1)S(1)} %copy-done.9), kind=kOutput, calls=%fused_computation.83 | convolution fusion | flops 134479808 | bytes 2621696 | tf_op jit(solution)/shard_map/rqf,fd->rqd/dot_general | solution.py:135
  49.1 1.4 scatter_custom_fusion
  50.4 28.2 %all_to_all.30 = bf16[32,8,1024]{2,1,0:T(8,128)(2,1)} all-to-all(bf16[32,8,1024]{2,1,0:T(8,128)(2,1)S(1)} %bitcast.161), channel_id=1, replica_groups=mesh['req'=32,'head'=4,'blk'=2] {'req'}, dimensions={0} | all-to-all | bytes 1048576 | tf_op jit(solution)/shard_map/all_to_all | solution.py:168
  78.9 5.8 %fusion.67 = (bf16[1,2560,128]{2,1,0:T(8,128)(2,1)S(1)}, bf16[1,2560,128]{2,1,0:T(8,128)(2,1)S(1)}) fusion(s32[]{:T(128)} %bitcast.41, bf16[1,2048,128]{2,1,0:T(8,128)(2,1)S(1)} %broadcast.378, bf16[1,512,128]{2,1,0:T(8,128)(2,1)S(1)} %copy-done.7, bf16[1,2048,128]{2,1,0:T(8,128)(2,1)S(1)} %copy-done.3, pred[2560]{0:T(1024)(128)(4,1)S(1)} %iota_compare_fusion.4, ...), kind=kLoop, calls=%fused_computation.69 | loop fusion | flops 4587520 | bytes 3148292 | tf_op jit(solution)/shard_map/vmap(jit(_where))/select_n | solution.py:72
  86.5 1.2 collective-permute-start
  88.5 1.2 collective-permute-start.2
  90.4 6.2 %collective-permute-done.3 = bf16[2,320,128]{2,1,0:T(8,128)(2,1)S(1)} collective-permute-done((bf16[2,320,128]{2,1,0:T(8,128)(2,1)S(1)}, bf16[2,320,128]{2,1,0:T(8,128)(2,1)S(1)}, u32[]{:S(2)}, u32[]{:S(2)}) %collective-permute-start.3) | collective-permute-done | bytes 163872 | tf_op jit(solution)/shard_map/ppermute | solution.py:85
  96.6 9.0 %collective-permute-done = bf16[1024,352]{0,1:T(8,128)(2,1)S(1)} collective-permute-done((bf16[1024,352]{0,1:T(8,128)(2,1)S(1)}, bf16[1024,352]{0,1:T(8,128)(2,1)S(1)}, u32[]{:S(2)}, u32[]{:S(2)}) %collective-permute-start) | collective-permute-done | bytes 720928 | tf_op jit(solution)/shard_map/ppermute | solution.py:160
  105.5 1.2 collective-permute-start.6
  106.7 12.6 %all-gather.6.cloned.1.call-done = bf16[128,8,1024]{2,1,0:T(8,128)(2,1)} async-done(((bf16[32,8,1024]{2,1,0:T(8,128)(2,1)}), bf16[128,8,1024]{2,1,0:T(8,128)(2,1)}) %all-gather.6.cloned.1.call-update) | async-done | bytes 2097168 | tf_op jit(solution)/shard_map/all_gather | solution.py:169
  119.4 5.4 %fusion.23 = f32[2,352,1024]{2,1,0:T(8,128)} fusion(bf16[128,8,1024]{2,1,0:T(8,128)(2,1)} %all-gather.6.cloned.1.call-done, bf16[1,1024,352]{1,2,0:T(8,128)(2,1)} %bitcast.175, bf16[1,1024,352]{1,2,0:T(8,128)(2,1)} %bitcast.174), kind=kOutput, calls=%fused_computation.32 | convolution fusion | flops 1477115904 | bytes 6422528 | tf_op jit(solution)/shard_map/nd,sdf->snf/dot_general | solution.py:171
  124.8 11.0 %collective-permute-done.2 = bf16[352,1024]{1,0:T(8,128)(2,1)} collective-permute-done((bf16[352,1024]{1,0:T(8,128)(2,1)}, bf16[352,1024]{1,0:T(8,128)(2,1)}, u32[]{:S(2)}, u32[]{:S(2)}) %collective-permute-start.2) | collective-permute-done | bytes 720928 | tf_op jit(solution)/shard_map/ppermute | solution.py:162
  135.8 2.8 %collective-permute-start.8 = (bf16[2,320,128]{2,1,0:T(8,128)(2,1)}, bf16[2,320,128]{2,1,0:T(8,128)(2,1)}, u32[]{:S(2)}, u32[]{:S(2)}) collective-permute-start(bf16[2,320,128]{2,1,0:T(8,128)(2,1)} %get-tuple-element.40), channel_id=1, source_target_pairs={{0,6},{1,7},{2,0},{3,1},{4,2},{5,3},{6,4},{7,5},{8,14},{9,15},{10,... | collective-permute-start | bytes 491528 | tf_op jit(solution)/shard_map/ppermute | solution.py:85
  138.5 8.7 %convert_reduce_fusion = bf16[1024,1024]{1,0:T(8,128)(2,1)} fusion(f32[2,352,1024]{2,1,0:T(8,128)} %fusion.23, bf16[128,8,1024]{2,1,0:T(8,128)(2,1)S(1)} %copy-done.14, bf16[1,1024,352]{1,2,0:T(8,128)(2,1)} %bitcast.31, bf16[1,1024,352]{1,2,0:T(8,128)(2,1)} %bitcast.30, bf16[1,352,1024]{2,1,0:T(8,128)(2,1)} %bitcast.35, bf16[1,352,1024]{2,1,0:T(8,128)(2,1)} %bitcast.34), kind=kOutput, calls=%fused_computation.20 | convolution fusion | flops 2964586496 | bytes 9961472 | tf_op jit(solution)/shard_map/snf,sfd->snd/dot_general | solution.py:174
  147.3 3.8 %all-to-all-start.2 = ((bf16[4,32,8,1024]{3,2,1,0:T(8,128)(2,1)}), bf16[4,32,8,1024]{3,2,1,0:T(8,128)(2,1)S(1)}, u32[]{:S(2)}, u32[]{:S(2)}) async-start(bf16[4,32,8,1024]{3,2,1,0:T(8,128)(2,1)} %bitcast.160), calls=%async_computation.2 | async-start | bytes 4194304 | tf_op jit(solution)/shard_map/all_to_all | solution.py:178
  151.1 1.5 collective-permute-start.9
  157.3 17.9 %collective-permute-done.9 = bf16[2,320,128]{2,1,0:T(8,128)(2,1)S(1)} collective-permute-done((bf16[2,320,128]{2,1,0:T(8,128)(2,1)}, bf16[2,320,128]{2,1,0:T(8,128)(2,1)S(1)}, u32[]{:S(2)}, u32[]{:S(2)}) %collective-permute-start.9) | collective-permute-done | bytes 163872 | tf_op jit(solution)/shard_map/ppermute | solution.py:85
  175.2 1.8 gather_fusion.1
  177.0 1.5 select_bitcast_fusion
  178.6 1.3 reduce_sum.72
  179.9 5.6 %all-to-all-start.3 = ((bf16[32,8,1024]{2,1,0:T(8,128)(2,1)}), bf16[32,8,1024]{2,1,0:T(8,128)(2,1)S(1)}, u32[]{:S(2)}, u32[]{:S(2)}) async-start(bf16[32,8,1024]{2,1,0:T(8,128)(2,1)} %reduce_sum.72), calls=%async_computation.3 | async-start | bytes 1048576 | tf_op jit(solution)/shard_map/all_to_all | solution.py:182
  185.6 1.3 copy_bitcast_fusion
  187.0 1.3 gather_fusion.2
  188.7 14.7 %all-to-all-done.3 = bf16[32,8,1024]{2,1,0:T(8,128)(2,1)S(1)} async-done(((bf16[32,8,1024]{2,1,0:T(8,128)(2,1)}), bf16[32,8,1024]{2,1,0:T(8,128)(2,1)S(1)}, u32[]{:S(2)}, u32[]{:S(2)}) %all-to-all-start.3) | async-done | bytes 524320 | tf_op jit(solution)/shard_map/all_to_all | solution.py:182
  (116 shorter events, 20.8 us)
Async XLA Ops:
  7.2 179.7 %copy-start = (bf16[1024,16]{0,1:T(8,128)(2,1)S(1)}, bf16[1024,16]{0,1:T(8,128)(2,1)}, u32[]{:S(2)}) copy-start(bf16[1024,16]{0,1:T(8,128)(2,1)} %param.32) | copy-start | bytes 98308
  7.2 5.1 %copy-start.7 = (bf16[1,512,128]{2,1,0:T(8,128)(2,1)S(1)}, bf16[1,512,128]{2,1,0:T(8,128)(2,1)}, u32[]{:S(2)}) copy-start(bf16[1,512,128]{2,1,0:T(8,128)(2,1)} %param.22) | copy-start | bytes 393220
  7.2 5.9 %copy-start.10 = (bf16[1,512,128]{2,1,0:T(8,128)(2,1)S(1)}, bf16[1,512,128]{2,1,0:T(8,128)(2,1)}, u32[]{:S(2)}) copy-start(bf16[1,512,128]{2,1,0:T(8,128)(2,1)} %param.21) | copy-start | bytes 393220
  7.2 7.4 %copy-start.4 = (bf16[1,2048,128]{2,1,0:T(8,128)(2,1)S(1)}, bf16[1,2048,128]{2,1,0:T(8,128)(2,1)}, u32[]{:S(2)}) copy-start(bf16[1,2048,128]{2,1,0:T(8,128)(2,1)} %param.25) | copy-start | bytes 1572868
  7.2 37.9 %all-gather.4.cloned.1.call-start = ((), (), s32[]{:S(2)}) async-start(), calls=%async_computation.4 | async-start | bytes 2359296 | tf_op jit(solution)/shard_map/all_gather | solution.py:133
  10.2 4.6 %copy-start.8 = (bf16[1,512,128]{2,1,0:T(8,128)(2,1)S(1)}, bf16[1,512,128]{2,1,0:T(8,128)(2,1)}, u32[]{:S(2)}) copy-start(bf16[1,512,128]{2,1,0:T(8,128)(2,1)} %param.23) | copy-start | bytes 393220
  27.2 11.6 %copy-start.11 = (s32[1,64,2]{1,2,0:T(2,128)S(1)}, s32[1,64,2]{1,2,0:T(2,128)}, u32[]{:S(2)}) copy-start(s32[1,64,2]{1,2,0:T(2,128)} %param.36) | copy-start | bytes 1540
  27.2 12.0 %copy-start.13 = (s32[1,64,2]{1,2,0:T(2,128)S(1)}, s32[1,64,2]{1,2,0:T(2,128)}, u32[]{:S(2)}) copy-start(s32[1,64,2]{1,2,0:T(2,128)} %param.37) | copy-start | bytes 1540
  31.4 13.7 %copy-start.9 = (bf16[1,64,1024]{2,1,0:T(8,128)(2,1)S(1)}, bf16[1,64,1024]{2,1,0:T(8,128)(2,1)}, u32[]{:S(2)}) copy-start(bf16[1,64,1024]{2,1,0:T(8,128)(2,1)} %param.20) | copy-start | bytes 393220
  34.2 10.6 %all-to-all-start = ((bf16[8,2,4096]{2,1,0:T(2,128)(2,1)}), bf16[8,2,4096]{2,1,0:T(2,128)(2,1)S(1)}, u32[]{:S(2)}, u32[]{:S(2)}) async-start(bf16[8,2,4096]{2,1,0:T(2,128)(2,1)} %reshape.575), calls=%async_computation | async-start | bytes 262144 | tf_op jit(solution)/shard_map/all_to_all | solution.py:134
  38.7 80.6 %all-gather.6.cloned.1.call-start = ((), (), s32[]{:S(2)}) async-start(), calls=%async_computation.5 | async-start | bytes 2621440 | tf_op jit(solution)/shard_map/all_gather | solution.py:169
  45.0 3.1 %copy-start.12 = (f32[1024]{0:T(1024)S(1)}, f32[1024]{0:T(1024)}, u32[]{:S(2)}) copy-start(f32[1024]{0:T(1024)} %param.31) | copy-start | bytes 12292
  47.3 0.7 copy-start.1
  48.1 0.7 copy-start.5
  49.1 29.8 %copy-start.3 = (bf16[1,2048,128]{2,1,0:T(8,128)(2,1)S(1)}, bf16[1,2048,128]{2,1,0:T(8,128)(2,1)}, u32[]{:S(2)}) copy-start(bf16[1,2048,128]{2,1,0:T(8,128)(2,1)} %param.24) | copy-start | bytes 1572868
  84.8 1.7 copy-start.15
  85.8 10.7 %collective-permute-start.3 = (bf16[2,320,128]{2,1,0:T(8,128)(2,1)S(1)}, bf16[2,320,128]{2,1,0:T(8,128)(2,1)S(1)}, u32[]{:S(2)}, u32[]{:S(2)}) collective-permute-start(bf16[2,320,128]{2,1,0:T(8,128)(2,1)S(1)} %get-tuple-element.45), channel_id=1, source_target_pairs={{0,1},{1,2},{2,3},{3,4},{4,5},{5,6},{6,7},{7,0},{8,9},{9,10},{10,1... | collective-permute-start | bytes 491528 | tf_op jit(solution)/shard_map/ppermute | solution.py:85
  85.8 65.3 %collective-permute-start.4 = (bf16[2,320,128]{2,1,0:T(8,128)(2,1)}, bf16[2,320,128]{2,1,0:T(8,128)(2,1)}, u32[]{:S(2)}, u32[]{:S(2)}) collective-permute-start(bf16[2,320,128]{2,1,0:T(8,128)(2,1)} %get-tuple-element.44), channel_id=1, source_target_pairs={{0,2},{1,3},{2,4},{3,5},{4,6},{5,7},{6,0},{7,1},{8,10},{9,11},{10,... | collective-permute-start | bytes 491528 | tf_op jit(solution)/shard_map/ppermute | solution.py:85
  86.5 19.0 %collective-permute-start = (bf16[1024,352]{0,1:T(8,128)(2,1)S(1)}, bf16[1024,352]{0,1:T(8,128)(2,1)S(1)}, u32[]{:S(2)}, u32[]{:S(2)}) collective-permute-start(bf16[1024,352]{0,1:T(8,128)(2,1)S(1)} %copy-done.15), channel_id=1, source_target_pairs={{0,8},{8,0},{16,24},{24,16},{32,40},{40,32},{48,56},{56,48},{64,72... | collective-permute-start | bytes 2162696 | tf_op jit(solution)/shard_map/ppermute | solution.py:160
  87.7 37.1 %collective-permute-start.1 = (bf16[1024,352]{0,1:T(8,128)(2,1)}, bf16[1024,352]{0,1:T(8,128)(2,1)}, u32[]{:S(2)}, u32[]{:S(2)}) collective-permute-start(bf16[1024,352]{0,1:T(8,128)(2,1)} %param.34), channel_id=1, source_target_pairs={{0,8},{8,0},{16,24},{24,16},{32,40},{40,32},{48,56},{56,48},{64,72... | collective-permute-start | bytes 2162696 | tf_op jit(solution)/shard_map/ppermute | solution.py:161
  88.5 47.2 %collective-permute-start.2 = (bf16[352,1024]{1,0:T(8,128)(2,1)}, bf16[352,1024]{1,0:T(8,128)(2,1)}, u32[]{:S(2)}, u32[]{:S(2)}) collective-permute-start(bf16[352,1024]{1,0:T(8,128)(2,1)} %param.35), channel_id=1, source_target_pairs={{0,8},{8,0},{16,24},{24,16},{32,40},{40,32},{48,56},{56,48},{64,72... | collective-permute-start | bytes 2162696 | tf_op jit(solution)/shard_map/ppermute | solution.py:162
  96.5 57.0 %collective-permute-start.5 = (bf16[2,320,128]{2,1,0:T(8,128)(2,1)}, bf16[2,320,128]{2,1,0:T(8,128)(2,1)}, u32[]{:S(2)}, u32[]{:S(2)}) collective-permute-start(bf16[2,320,128]{2,1,0:T(8,128)(2,1)} %get-tuple-element.43), channel_id=1, source_target_pairs={{0,3},{1,4},{2,5},{3,6},{4,7},{5,0},{6,1},{7,2},{8,11},{9,12},{10,... | collective-permute-start | bytes 491528 | tf_op jit(solution)/shard_map/ppermute | solution.py:85
  105.5 13.8 %copy-start.16 = (bf16[1024,352]{0,1:T(8,128)(2,1)}, bf16[1024,352]{0,1:T(8,128)(2,1)S(1)}, u32[]{:S(2)}) copy-start(bf16[1024,352]{0,1:T(8,128)(2,1)S(1)} %collective-permute-done) | copy-start | bytes 2162692
  105.5 48.9 %collective-permute-start.6 = (bf16[2,320,128]{2,1,0:T(8,128)(2,1)}, bf16[2,320,128]{2,1,0:T(8,128)(2,1)}, u32[]{:S(2)}, u32[]{:S(2)}) collective-permute-start(bf16[2,320,128]{2,1,0:T(8,128)(2,1)} %get-tuple-element.42), channel_id=1, source_target_pairs={{0,4},{1,5},{2,6},{3,7},{4,0},{5,1},{6,2},{7,3},{8,12},{9,13},{10,... | collective-permute-start | bytes 491528 | tf_op jit(solution)/shard_map/ppermute | solution.py:85
  119.4 19.2 %copy-start.14 = (bf16[128,8,1024]{2,1,0:T(8,128)(2,1)S(1)}, bf16[128,8,1024]{2,1,0:T(8,128)(2,1)}, u32[]{:S(2)}) copy-start(bf16[128,8,1024]{2,1,0:T(8,128)(2,1)} %all-gather.6.cloned.1.call-done) | copy-start | bytes 6291460
  124.8 30.6 %collective-permute-start.7 = (bf16[2,320,128]{2,1,0:T(8,128)(2,1)}, bf16[2,320,128]{2,1,0:T(8,128)(2,1)}, u32[]{:S(2)}, u32[]{:S(2)}) collective-permute-start(bf16[2,320,128]{2,1,0:T(8,128)(2,1)} %get-tuple-element.41), channel_id=1, source_target_pairs={{0,5},{1,6},{2,7},{3,0},{4,1},{5,2},{6,3},{7,4},{8,13},{9,14},{10,... | collective-permute-start | bytes 491528 | tf_op jit(solution)/shard_map/ppermute | solution.py:85
  135.8 20.6 %collective-permute-start.8 = (bf16[2,320,128]{2,1,0:T(8,128)(2,1)}, bf16[2,320,128]{2,1,0:T(8,128)(2,1)}, u32[]{:S(2)}, u32[]{:S(2)}) collective-permute-start(bf16[2,320,128]{2,1,0:T(8,128)(2,1)} %get-tuple-element.40), channel_id=1, source_target_pairs={{0,6},{1,7},{2,0},{3,1},{4,2},{5,3},{6,4},{7,5},{8,14},{9,15},{10,... | collective-permute-start | bytes 491528 | tf_op jit(solution)/shard_map/ppermute | solution.py:85
  147.3 31.3 %all-to-all-start.2 = ((bf16[4,32,8,1024]{3,2,1,0:T(8,128)(2,1)}), bf16[4,32,8,1024]{3,2,1,0:T(8,128)(2,1)S(1)}, u32[]{:S(2)}, u32[]{:S(2)}) async-start(bf16[4,32,8,1024]{3,2,1,0:T(8,128)(2,1)} %bitcast.160), calls=%async_computation.2 | async-start | bytes 4194304 | tf_op jit(solution)/shard_map/all_to_all | solution.py:178
  151.1 24.1 %collective-permute-start.9 = (bf16[2,320,128]{2,1,0:T(8,128)(2,1)}, bf16[2,320,128]{2,1,0:T(8,128)(2,1)S(1)}, u32[]{:S(2)}, u32[]{:S(2)}) collective-permute-start(bf16[2,320,128]{2,1,0:T(8,128)(2,1)} %get-tuple-element.39), channel_id=1, source_target_pairs={{0,7},{1,0},{2,1},{3,2},{4,3},{5,4},{6,5},{7,6},{8,15},{9,8},{10,9... | collective-permute-start | bytes 491528 | tf_op jit(solution)/shard_map/ppermute | solution.py:85
  179.9 23.5 %all-to-all-start.3 = ((bf16[32,8,1024]{2,1,0:T(8,128)(2,1)}), bf16[32,8,1024]{2,1,0:T(8,128)(2,1)S(1)}, u32[]{:S(2)}, u32[]{:S(2)}) async-start(bf16[32,8,1024]{2,1,0:T(8,128)(2,1)} %reduce_sum.72), calls=%async_computation.3 | async-start | bytes 1048576 | tf_op jit(solution)/shard_map/all_to_all | solution.py:182
  185.6 1.3 copy-start.6
  204.3 1.2 copy-start.2
Sparse Core Ops, SparseCore 0:
  9.9 30.8 all-gather.3
  78.8 40.5 all-gather.5

commit v4 on v3

--- a/solution.py
+++ b/solution.py
@@ -164,22 +164,28 @@
     both_up = jnp.stack([expert_up, other_up])
     both_down = jnp.stack([expert_down, other_down])
     step = slots_here // holders
-    outgoing = buffer.reshape(experts * holders, step, width)
-    arrived = lax.all_to_all(outgoing, "req", split_axis=0, concat_axis=0, tiled=True)
-    gathered = lax.all_gather(arrived, "head", axis=0, tiled=False)
-    flat_rows = gathered.reshape(-1, width)
-    gate_val = jnp.einsum("nd,sdf->snf", flat_rows, both_gate, preferred_element_type=jnp.float32)
-    up_val = jnp.einsum("nd,sdf->snf", flat_rows, both_up, preferred_element_type=jnp.float32)
-    hidden = (jax.nn.gelu(gate_val, approximate=True) * up_val).astype(jnp.bfloat16)
-    blocks_out = jnp.einsum(
-        "snf,sfd->snd", hidden, both_down, preferred_element_type=jnp.float32
-    ).astype(jnp.bfloat16)
-    pair_sum = jnp.sum(blocks_out.astype(jnp.float32), axis=0).astype(jnp.bfloat16)
-    shard_parts = lax.all_to_all(
-        pair_sum.reshape(gathered.shape), "head", split_axis=0, concat_axis=0, tiled=True
-    )
-    full_sum = jnp.sum(shard_parts.astype(jnp.float32), axis=0).astype(jnp.bfloat16)
-    returned = lax.all_to_all(full_sum, "req", split_axis=0, concat_axis=0, tiled=True)
+    slabs = buffer.reshape(experts * holders, step, width)
+    chunks = 2
+    size = step // chunks
+    pieces = []
+    for c in range(chunks):
+        outgoing = slabs[:, c * size:(c + 1) * size]
+        arrived = lax.all_to_all(outgoing, "req", split_axis=0, concat_axis=0, tiled=True)
+        gathered = lax.all_gather(arrived, "head", axis=0, tiled=False)
+        flat_rows = gathered.reshape(-1, width)
+        gate_val = jnp.einsum("nd,sdf->snf", flat_rows, both_gate, preferred_element_type=jnp.float32)
+        up_val = jnp.einsum("nd,sdf->snf", flat_rows, both_up, preferred_element_type=jnp.float32)
+        hidden = (jax.nn.gelu(gate_val, approximate=True) * up_val).astype(jnp.bfloat16)
+        blocks_out = jnp.einsum(
+            "snf,sfd->snd", hidden, both_down, preferred_element_type=jnp.float32
+        ).astype(jnp.bfloat16)
+        pair_sum = jnp.sum(blocks_out.astype(jnp.float32), axis=0).astype(jnp.bfloat16)
+        shard_parts = lax.all_to_all(
+            pair_sum.reshape(gathered.shape), "head", split_axis=0, concat_axis=0, tiled=True
+        )
+        full_sum = jnp.sum(shard_parts.astype(jnp.float32), axis=0).astype(jnp.bfloat16)
+        pieces.append(lax.all_to_all(full_sum, "req", split_axis=0, concat_axis=0, tiled=True))
+    returned = jnp.concatenate(pieces, axis=1)
     combined = returned.astype(jnp.float32).reshape(experts * slots_here, width)
     picked = jnp.take(combined, places, axis=0).reshape(-1, 2, width)
     mixture = jnp.sum(picked * gate_weights[:, :, None], axis=1)

time: 215 us -> 239 us (1.11)
  blocking collectives: 28.2 us -> 0 us
  starting transfers between devices: 23.3 us -> 51.3 us
  waiting for transfers between devices: 76.8 us -> 87.7 us
  local copies, waits for them, and re-layouts: 21.5 us -> 28.3 us
  other arithmetic: 17.6 us -> 22 us
  matrix products: 29.5 us -> 32.1 us
    all_to_all x1 -> x0, blocking collectives: 28.2 us -> none  [layer(): lax.all_to_all(outgoing, 'req', split_axis=0, concat_axis=0, tiled=True)]
    ppermute x7, waiting for transfers between devices: 24.1 us -> 0.02 us  [to_positions(): blocks.append(lax.ppermute(block, ('head', 'blk'), perm))]
    all_to_all x0 -> x2, waiting for transfers between devices: none -> 21.6 us  [layer(): lax.all_to_all(outgoing, 'req', split_axis=0, concat_axis=0, tiled=True)]
    all_to_all x0 -> x2, starting transfers between devices: none -> 17.2 us  [layer(): lax.all_to_all(outgoing, 'req', split_axis=0, concat_axis=0, tiled=True)]
    all_gather x1 -> x2, waiting for transfers between devices: 12.6 us -> 0.02 us  [layer(): gathered = lax.all_gather(arrived, 'head', axis=0, tiled=False)]
    ppermute x1, waiting for transfers between devices: 0.01 us -> 12.2 us  [layer(): other_up = lax.ppermute(expert_up, 'req', pair)]
    all_to_all x1 -> x2, waiting for transfers between devices: 0.01 us -> 7.81 us  [layer(): lax.all_to_all(pair_sum.reshape(gathered.shape), 'head', split_axis=0, co...]
    all_to_all x1 -> x2, starting transfers between devices: 5.56 us -> 12.5 us  [layer(): lax.all_to_all(full_sum, 'req', split_axis=0, concat_axis=0, tiled=True)]
  transfers between devices with their start and end apart: 15 -> 20, of which waited for: 7 -> 10; matrix products, arithmetic and copies ran while one was open for 28% -> 31% of each run, Pallas kernels for 0% -> 0%
where the time goes in v4:
time: 239 us; the launch traced here: 237 us
  waiting for transfers between devices  87.7 us (37%)
  starting transfers between devices  51.3 us (21%)
  matrix products  32.1 us (13%)
  local copies, waits for them, and re-layouts  28.3 us (12%)
  other arithmetic  22 us (9%)
  between operations  15.8 us (7%)
    all_to_all x2, waiting for transfers between devices, layer(): lax.all_to_all(outgoing, 'req', split_axis=0, concat_axis=0, tiled=True)  21.6 us
    all_to_all x2, starting transfers between devices, layer(): lax.all_to_all(outgoing, 'req', split_axis=0, concat_axis=0, tiled=True)  17.2 us
    ppermute x1, waiting for transfers between devices, layer(): other_down = lax.ppermute(expert_down, 'req', pair)  14.6 us
    all_to_all x2, waiting for transfers between devices, layer(): lax.all_to_all(full_sum, 'req', split_axis=0, concat_axis=0, tiled=True)  14 us
    all_to_all x2, starting transfers between devices, layer(): lax.all_to_all(full_sum, 'req', split_axis=0, concat_axis=0, tiled=True)  12.5 us
    ppermute x1, waiting for transfers between devices, layer(): other_up = lax.ppermute(expert_up, 'req', pair)  12.2 us
    ppermute x1, waiting for transfers between devices, layer(): other_gate = lax.ppermute(expert_gate, 'req', pair)  11.9 us
    unnamed x53, local copies, waits for them, and re-layouts  10.3 us
  transfers between devices with their start and end apart: 20, of which 10 were waited for; matrix products, arithmetic and copies ran while one was open for 31% of the time, Pallas kernels for 0%

profile of v4, /device:TPU:4, one launch (start us, length us, event | category | flops | bytes accessed | tf_op | source)
XLA Modules:
  0.0 237.2 jit_solution(8142258844807176897)
XLA Ops:
  10.4 2.1 copy.143
  13.9 2.8 %fusion.10 = pred[512,3072]{0,1:T(8,128)(4,1)S(1)} fusion(s32[3072]{0:T(1024)S(1)} %iota_add_fusion, pred[3072]{0:T(1024)(128)(4,1)S(1)} %get-tuple-element.55, pred[3072]{0:T(1024)(128)(4,1)S(1)} %get-tuple-element.56), kind=kLoop, calls=%fused_computation.17 | loop fusion | flops 4718592 | bytes 1591296 | tf_op jit(solution)/shard_map/or | solution.py:45
  16.7 8.9 %fusion.97 = (f32[2,512]{1,0:T(2,128)S(1)}, bf16[2,512,3072]{1,2,0:T(8,128)(2,1)}) fusion(pred[512,3072]{0,1:T(8,128)(4,1)S(1)} %fusion.10, bf16[512,2,64]{0,2,1:T(8,128)(2,1)} %bitcast.174, bf16[512,2,64]{0,2,1:T(8,128)(2,1)S(1)} %bitcast.173, bf16[2048,2,64]{0,2,1:T(8,128)(2,1)} %bitcast.168, bf16[512,2,64]{0,2,1:T(8,128)(2,1)S(1)} %bitcast.171), kind=kOutput, calls=%fused_computation.169 | convolution fusion | flops 832048128 | bytes 8785920 | tf_op jit(solution)/shard_map/sub | solution.py:53
  25.6 4.0 %fusion.39 = bf16[512,2,64]{0,2,1:T(8,128)(2,1)S(1)} fusion(bf16[2,512,3072]{1,2,0:T(8,128)(2,1)} %get-tuple-element.52, bf16[512,2,64]{0,2,1:T(8,128)(2,1)S(1)} %bitcast.172, bf16[2048,2,64]{0,2,1:T(8,128)(2,1)S(1)} %bitcast.167, bf16[512,2,64]{0,2,1:T(8,128)(2,1)S(1)} %bitcast.170, f32[512,2]{0,1:T(2,128)S(1)} %bitcast.181), kind=kOutput, calls=%fused_computation.59 | convolution fusion | flops 405143552 | bytes 7213056 | tf_op jit(solution)/shard_map/hqk,khd->qhd/dot_general | solution.py:56
  32.4 4.5 %all-to-all-start = ((bf16[8,2,4096]{2,1,0:T(2,128)(2,1)}), bf16[8,2,4096]{2,1,0:T(2,128)(2,1)S(1)}, u32[]{:S(2)}, u32[]{:S(2)}) async-start(bf16[8,2,4096]{2,1,0:T(2,128)(2,1)} %reshape.583), calls=%async_computation | async-start | bytes 262144 | tf_op jit(solution)/shard_map/all_to_all | solution.py:134
  38.1 4.9 %all-to-all-done = bf16[8,2,4096]{2,1,0:T(2,128)(2,1)S(1)} async-done(((bf16[8,2,4096]{2,1,0:T(2,128)(2,1)}), bf16[8,2,4096]{2,1,0:T(2,128)(2,1)S(1)}, u32[]{:S(2)}, u32[]{:S(2)}) %all-to-all-start) | async-done | bytes 131104 | tf_op jit(solution)/shard_map/all_to_all | solution.py:134
  43.2 2.2 multiply_reduce_fusion.1
  48.2 11.6 %all-to-all-start.1 = ((bf16[32,4,1024]{2,1,0:T(4,128)(2,1)}), bf16[32,4,1024]{2,1,0:T(4,128)(2,1)S(1)}, u32[]{:S(2)}, u32[]{:S(2)}) async-start(bf16[32,4,1024]{2,1,0:T(4,128)(2,1)} %get-tuple-element.49), calls=%async_computation.1 | async-start | bytes 524288 | tf_op jit(solution)/shard_map/all_to_all | solution.py:173
  60.1 10.8 %all-to-all-done.1 = bf16[32,4,1024]{2,1,0:T(4,128)(2,1)S(1)} async-done(((bf16[32,4,1024]{2,1,0:T(4,128)(2,1)}), bf16[32,4,1024]{2,1,0:T(4,128)(2,1)S(1)}, u32[]{:S(2)}, u32[]{:S(2)}) %all-to-all-start.1) | async-done | bytes 262176 | tf_op jit(solution)/shard_map/all_to_all | solution.py:173
  71.7 5.8 %fusion.51 = (bf16[1,2560,128]{2,1,0:T(8,128)(2,1)S(1)}, bf16[1,2560,128]{2,1,0:T(8,128)(2,1)S(1)}) fusion(s32[]{:T(128)} %bitcast.39, bf16[1,2048,128]{2,1,0:T(8,128)(2,1)S(1)} %broadcast.394, bf16[1,512,128]{2,1,0:T(8,128)(2,1)S(1)} %copy-done.6, bf16[1,2048,128]{2,1,0:T(8,128)(2,1)S(1)} %copy-done.2, pred[2560]{0:T(1024)(128)(4,1)S(1)} %iota_compare_fusion.4, ...), kind=kLoop, calls=%fused_computation.70 | loop fusion | flops 4587520 | bytes 3148292 | tf_op jit(solution)/shard_map/vmap(jit(_where))/select_n | solution.py:72
  80.7 2.7 %collective-permute-start.6 = (bf16[2,320,128]{2,1,0:T(8,128)(2,1)S(1)}, bf16[2,320,128]{2,1,0:T(8,128)(2,1)S(1)}, u32[]{:S(2)}, u32[]{:S(2)}) collective-permute-start(bf16[2,320,128]{2,1,0:T(8,128)(2,1)S(1)} %get-tuple-element.42), channel_id=1, source_target_pairs={{0,4},{1,5},{2,6},{3,7},{4,0},{5,1},{6,2},{7,3},{8,12},{9,13},{10,... | collective-permute-start | bytes 491528 | tf_op jit(solution)/shard_map/ppermute | solution.py:85
  85.1 5.6 %all-to-all-start.4 = ((bf16[32,4,1024]{2,1,0:T(4,128)(2,1)}), bf16[32,4,1024]{2,1,0:T(4,128)(2,1)S(1)}, u32[]{:S(2)}, u32[]{:S(2)}) async-start(bf16[32,4,1024]{2,1,0:T(4,128)(2,1)} %get-tuple-element.50), calls=%async_computation.4 | async-start | bytes 524288 | tf_op jit(solution)/shard_map/all_to_all | solution.py:173
  92.3 10.8 %all-to-all-done.4 = bf16[32,4,1024]{2,1,0:T(4,128)(2,1)S(1)} async-done(((bf16[32,4,1024]{2,1,0:T(4,128)(2,1)}), bf16[32,4,1024]{2,1,0:T(4,128)(2,1)S(1)}, u32[]{:S(2)}, u32[]{:S(2)}) %all-to-all-start.4) | async-done | bytes 262176 | tf_op jit(solution)/shard_map/all_to_all | solution.py:173
  111.2 11.9 %collective-permute-done = bf16[1024,352]{0,1:T(8,128)(2,1)} collective-permute-done((bf16[1024,352]{0,1:T(8,128)(2,1)S(1)}, bf16[1024,352]{0,1:T(8,128)(2,1)}, u32[]{:S(2)}, u32[]{:S(2)}) %collective-permute-start) | collective-permute-done | bytes 720928 | tf_op jit(solution)/shard_map/ppermute | solution.py:160
  123.1 3.2 %convolution_bitcast_fusion.3 = f32[2,512,352]{1,2,0:T(8,128)} fusion(bf16[512,1024,1]{1,0,2:T(8,128)(2,1)S(1)} %reshape.577, bf16[1,1024,352]{1,2,0:T(8,128)(2,1)} %bitcast.22, bf16[1,1024,352]{1,2,0:T(8,128)(2,1)S(1)} %bitcast.176), kind=kOutput, calls=%fused_computation.27 | convolution fusion | flops 738918400 | bytes 3932160 | tf_op jit(solution)/shard_map/nd,sdf->snf/dot_general | solution.py:176
  126.3 12.2 %collective-permute-done.1 = bf16[1024,352]{0,1:T(8,128)(2,1)} collective-permute-done((bf16[1024,352]{0,1:T(8,128)(2,1)}, bf16[1024,352]{0,1:T(8,128)(2,1)}, u32[]{:S(2)}, u32[]{:S(2)}) %collective-permute-start.1) | collective-permute-done | bytes 720928 | tf_op jit(solution)/shard_map/ppermute | solution.py:161
  138.5 14.6 %collective-permute-done.2 = bf16[352,1024]{1,0:T(8,128)(2,1)} collective-permute-done((bf16[352,1024]{1,0:T(8,128)(2,1)}, bf16[352,1024]{1,0:T(8,128)(2,1)}, u32[]{:S(2)}, u32[]{:S(2)}) %collective-permute-start.2) | collective-permute-done | bytes 720928 | tf_op jit(solution)/shard_map/ppermute | solution.py:162
  153.1 4.6 %convert_reduce_fusion.1 = bf16[512,1024]{1,0:T(8,128)(2,1)S(1)} fusion(bf16[1,352,1024]{2,1,0:T(8,128)(2,1)} %bitcast.32, bf16[1,352,1024]{2,1,0:T(8,128)(2,1)} %bitcast.177, f32[2,512,352]{1,2,0:T(8,128)} %convolution_bitcast_fusion.3, bf16[512,1024,1]{1,0,2:T(8,128)(2,1)S(1)} %reshape.577, bf16[1,1024,352]{1,2,0:T(8,128)(2,1)} %bitcast.29, ...), kind=kOutput, calls=%fused_computation.22 | convolution fusion | flops 1483014144 | bytes 6422528 | tf_op jit(solution)/shard_map/snf,sfd->snd/dot_general | solution.py:179
  158.9 3.7 %all-to-all-start.2 = ((bf16[4,32,4,1024]{3,2,1,0:T(4,128)(2,1)}), bf16[4,32,4,1024]{3,2,1,0:T(4,128)(2,1)S(1)}, u32[]{:S(2)}, u32[]{:S(2)}) async-start(bf16[4,32,4,1024]{3,2,1,0:T(4,128)(2,1)} %reshape.449), calls=%async_computation.2 | async-start | bytes 2097152 | tf_op jit(solution)/shard_map/all_to_all | solution.py:183
  164.1 3.4 %convolution_bitcast_fusion.1 = f32[2,512,352]{1,2,0:T(8,128)} fusion(bf16[512,1024,1]{1,0,2:T(8,128)(2,1)S(1)} %reshape.578, bf16[1,1024,352]{1,2,0:T(8,128)(2,1)} %bitcast.22, bf16[1,1024,352]{1,2,0:T(8,128)(2,1)} %bitcast.175), kind=kOutput, calls=%fused_computation.25 | convolution fusion | flops 738918400 | bytes 3932160 | tf_op jit(solution)/shard_map/nd,sdf->snf/dot_general | solution.py:176
  167.5 5.7 %convert_reduce_fusion = bf16[512,1024]{1,0:T(8,128)(2,1)} fusion(bf16[1,352,1024]{2,1,0:T(8,128)(2,1)} %bitcast.32, bf16[1,352,1024]{2,1,0:T(8,128)(2,1)} %bitcast.178, f32[2,512,352]{1,2,0:T(8,128)} %convolution_bitcast_fusion.1, bf16[512,1024,1]{1,0,2:T(8,128)(2,1)S(1)} %reshape.578, bf16[1,1024,352]{1,2,0:T(8,128)(2,1)} %bitcast.29, ...), kind=kOutput, calls=%fused_computation.21 | convolution fusion | flops 1483014144 | bytes 6422528 | tf_op jit(solution)/shard_map/snf,sfd->snd/dot_general | solution.py:179
  173.2 2.2 reshape.451
  175.4 1.8 all-to-all-done.2
  177.2 4.2 %all-to-all-start.5 = ((bf16[4,32,4,1024]{3,2,1,0:T(4,128)(2,1)}), bf16[4,32,4,1024]{3,2,1,0:T(4,128)(2,1)}, u32[]{:S(2)}, u32[]{:S(2)}) async-start(bf16[4,32,4,1024]{3,2,1,0:T(4,128)(2,1)} %reshape.451), calls=%async_computation.5 | async-start | bytes 2097152 | tf_op jit(solution)/shard_map/all_to_all | solution.py:183
  184.5 2.2 gather_fusion.1
  186.9 2.5 %reduce_sum.96 = bf16[32,4,1024]{2,1,0:T(4,128)(2,1)} reduce(bf16[4,32,4,1024]{3,2,1,0:T(4,128)(2,1)} %copy-done.1, bf16[]{:T(256)} %constant.176.clone.1), dimensions={0}, to_apply=%region_7.9 | reduce | flops 393216 | bytes 1310722 | tf_op jit(solution)/shard_map/reduce_sum | solution.py:186
  189.5 6.0 %all-to-all-done.5 = bf16[4,32,4,1024]{3,2,1,0:T(4,128)(2,1)} async-done(((bf16[4,32,4,1024]{3,2,1,0:T(4,128)(2,1)}), bf16[4,32,4,1024]{3,2,1,0:T(4,128)(2,1)}, u32[]{:S(2)}, u32[]{:S(2)}) %all-to-all-start.5) | async-done | bytes 1048608 | tf_op jit(solution)/shard_map/all_to_all | solution.py:183
  195.5 6.8 %all-to-all-start.3 = ((bf16[32,4,1024]{2,1,0:T(4,128)(2,1)}), bf16[32,4,1024]{2,1,0:T(4,128)(2,1)S(1)}, u32[]{:S(2)}, u32[]{:S(2)}) async-start(bf16[32,4,1024]{2,1,0:T(4,128)(2,1)} %reduce_sum.96), calls=%async_computation.3 | async-start | bytes 524288 | tf_op jit(solution)/shard_map/all_to_all | solution.py:187
  203.7 2.5 %reduce_sum.98 = bf16[32,4,1024]{2,1,0:T(4,128)(2,1)} reduce(bf16[4,32,4,1024]{3,2,1,0:T(4,128)(2,1)} %all-to-all-done.5, bf16[]{:T(256)} %constant.176.clone.1), dimensions={0}, to_apply=%region_9.11 | reduce | flops 393216 | bytes 1310722 | tf_op jit(solution)/shard_map/reduce_sum | solution.py:186
  206.2 5.9 %all-to-all-done.3 = bf16[32,4,1024]{2,1,0:T(4,128)(2,1)S(1)} async-done(((bf16[32,4,1024]{2,1,0:T(4,128)(2,1)}), bf16[32,4,1024]{2,1,0:T(4,128)(2,1)S(1)}, u32[]{:S(2)}, u32[]{:S(2)}) %all-to-all-start.3) | async-done | bytes 262176 | tf_op jit(solution)/shard_map/all_to_all | solution.py:187
  212.1 5.7 %all-to-all-start.6 = ((bf16[32,4,1024]{2,1,0:T(4,128)(2,1)}), bf16[32,4,1024]{2,1,0:T(4,128)(2,1)S(1)}, u32[]{:S(2)}, u32[]{:S(2)}) async-start(bf16[32,4,1024]{2,1,0:T(4,128)(2,1)} %reduce_sum.98), calls=%async_computation.6 | async-start | bytes 524288 | tf_op jit(solution)/shard_map/all_to_all | solution.py:187
  219.7 8.0 %all-to-all-done.6 = bf16[32,4,1024]{2,1,0:T(4,128)(2,1)S(1)} async-done(((bf16[32,4,1024]{2,1,0:T(4,128)(2,1)}), bf16[32,4,1024]{2,1,0:T(4,128)(2,1)S(1)}, u32[]{:S(2)}, u32[]{:S(2)}) %all-to-all-start.6) | async-done | bytes 262176 | tf_op jit(solution)/shard_map/all_to_all | solution.py:187
  (136 shorter events, 37.5 us)
Async XLA Ops:
  7.2 210.6 %copy-start = (bf16[1024,16]{0,1:T(8,128)(2,1)S(1)}, bf16[1024,16]{0,1:T(8,128)(2,1)}, u32[]{:S(2)}) copy-start(bf16[1024,16]{0,1:T(8,128)(2,1)} %param.32) | copy-start | bytes 98308
  7.2 5.3 %copy-start.6 = (bf16[1,512,128]{2,1,0:T(8,128)(2,1)S(1)}, bf16[1,512,128]{2,1,0:T(8,128)(2,1)}, u32[]{:S(2)}) copy-start(bf16[1,512,128]{2,1,0:T(8,128)(2,1)} %param.22) | copy-start | bytes 393220
  7.2 5.4 %copy-start.9 = (bf16[1,512,128]{2,1,0:T(8,128)(2,1)S(1)}, bf16[1,512,128]{2,1,0:T(8,128)(2,1)}, u32[]{:S(2)}) copy-start(bf16[1,512,128]{2,1,0:T(8,128)(2,1)} %param.21) | copy-start | bytes 393220
  7.2 6.3 %copy-start.3 = (bf16[1,2048,128]{2,1,0:T(8,128)(2,1)S(1)}, bf16[1,2048,128]{2,1,0:T(8,128)(2,1)}, u32[]{:S(2)}) copy-start(bf16[1,2048,128]{2,1,0:T(8,128)(2,1)} %param.25) | copy-start | bytes 1572868
  7.2 36.0 %all-gather.6.cloned.1.call-start = ((), (), s32[]{:S(2)}) async-start(), calls=%async_computation.7 | async-start | bytes 2359296 | tf_op jit(solution)/shard_map/all_gather | solution.py:133
  25.6 11.3 %copy-start.10 = (s32[1,64,2]{1,2,0:T(2,128)S(1)}, s32[1,64,2]{1,2,0:T(2,128)}, u32[]{:S(2)}) copy-start(s32[1,64,2]{1,2,0:T(2,128)} %param.36) | copy-start | bytes 1540
  29.6 7.8 %copy-start.12 = (s32[1,64,2]{1,2,0:T(2,128)S(1)}, s32[1,64,2]{1,2,0:T(2,128)}, u32[]{:S(2)}) copy-start(s32[1,64,2]{1,2,0:T(2,128)} %param.37) | copy-start | bytes 1540
  29.6 13.7 %copy-start.8 = (bf16[1,64,1024]{2,1,0:T(8,128)(2,1)S(1)}, bf16[1,64,1024]{2,1,0:T(8,128)(2,1)}, u32[]{:S(2)}) copy-start(bf16[1,64,1024]{2,1,0:T(8,128)(2,1)} %param.20) | copy-start | bytes 393220
  32.4 10.6 %all-to-all-start = ((bf16[8,2,4096]{2,1,0:T(2,128)(2,1)}), bf16[8,2,4096]{2,1,0:T(2,128)(2,1)S(1)}, u32[]{:S(2)}, u32[]{:S(2)}) async-start(bf16[8,2,4096]{2,1,0:T(2,128)(2,1)} %reshape.583), calls=%async_computation | async-start | bytes 262144 | tf_op jit(solution)/shard_map/all_to_all | solution.py:134
  38.1 7.7 %copy-start.14 = (s32[128]{0:T(128)}, s32[128]{0:T(128)S(1)}, u32[]{:S(2)}) copy-start(s32[128]{0:T(128)S(1)} %fusion.73) | copy-start | bytes 1540
  45.8 25.8 %copy-start.2 = (bf16[1,2048,128]{2,1,0:T(8,128)(2,1)S(1)}, bf16[1,2048,128]{2,1,0:T(8,128)(2,1)}, u32[]{:S(2)}) copy-start(bf16[1,2048,128]{2,1,0:T(8,128)(2,1)} %param.24) | copy-start | bytes 1572868
  48.2 22.7 %all-to-all-start.1 = ((bf16[32,4,1024]{2,1,0:T(4,128)(2,1)}), bf16[32,4,1024]{2,1,0:T(4,128)(2,1)S(1)}, u32[]{:S(2)}, u32[]{:S(2)}) async-start(bf16[32,4,1024]{2,1,0:T(4,128)(2,1)} %get-tuple-element.49), calls=%async_computation.1 | async-start | bytes 524288 | tf_op jit(solution)/shard_map/all_to_all | solution.py:173
  59.8 50.0 %all-gather.8.cloned.1.call-start = ((), (), s32[]{:S(2)}) async-start(), calls=%async_computation.8 | async-start | bytes 1310720 | tf_op jit(solution)/shard_map/all_gather | solution.py:174
  77.7 6.8 %copy-start.15 = (s32[128]{0:T(128)S(1)}, s32[128]{0:T(128)}, u32[]{:S(2)}) copy-start(s32[128]{0:T(128)} %copy-done.14) | copy-start | bytes 1540
  77.7 26.1 %copy-start.17 = (bf16[1024,352]{0,1:T(8,128)(2,1)S(1)}, bf16[1024,352]{0,1:T(8,128)(2,1)}, u32[]{:S(2)}) copy-start(bf16[1024,352]{0,1:T(8,128)(2,1)} %param.33) | copy-start | bytes 2162692
  78.7 25.2 %collective-permute-start.3 = (bf16[2,320,128]{2,1,0:T(8,128)(2,1)S(1)}, bf16[2,320,128]{2,1,0:T(8,128)(2,1)S(1)}, u32[]{:S(2)}, u32[]{:S(2)}) collective-permute-start(bf16[2,320,128]{2,1,0:T(8,128)(2,1)S(1)} %get-tuple-element.45), channel_id=1, source_target_pairs={{0,1},{1,2},{2,3},{3,4},{4,5},{5,6},{6,7},{7,0},{8,9},{9,10},{10,1... | collective-permute-start | bytes 491528 | tf_op jit(solution)/shard_map/ppermute | solution.py:85
  78.7 27.1 %collective-permute-start.4 = (bf16[2,320,128]{2,1,0:T(8,128)(2,1)S(1)}, bf16[2,320,128]{2,1,0:T(8,128)(2,1)S(1)}, u32[]{:S(2)}, u32[]{:S(2)}) collective-permute-start(bf16[2,320,128]{2,1,0:T(8,128)(2,1)S(1)} %get-tuple-element.44), channel_id=1, source_target_pairs={{0,2},{1,3},{2,4},{3,5},{4,6},{5,7},{6,0},{7,1},{8,10},{9,11},{10,... | collective-permute-start | bytes 491528 | tf_op jit(solution)/shard_map/ppermute | solution.py:85
  79.2 28.1 %collective-permute-start.5 = (bf16[2,320,128]{2,1,0:T(8,128)(2,1)S(1)}, bf16[2,320,128]{2,1,0:T(8,128)(2,1)S(1)}, u32[]{:S(2)}, u32[]{:S(2)}) collective-permute-start(bf16[2,320,128]{2,1,0:T(8,128)(2,1)S(1)} %get-tuple-element.43), channel_id=1, source_target_pairs={{0,3},{1,4},{2,5},{3,6},{4,7},{5,0},{6,1},{7,2},{8,11},{9,12},{10,... | collective-permute-start | bytes 491528 | tf_op jit(solution)/shard_map/ppermute | solution.py:85
  80.7 28.5 %collective-permute-start.6 = (bf16[2,320,128]{2,1,0:T(8,128)(2,1)S(1)}, bf16[2,320,128]{2,1,0:T(8,128)(2,1)S(1)}, u32[]{:S(2)}, u32[]{:S(2)}) collective-permute-start(bf16[2,320,128]{2,1,0:T(8,128)(2,1)S(1)} %get-tuple-element.42), channel_id=1, source_target_pairs={{0,4},{1,5},{2,6},{3,7},{4,0},{5,1},{6,2},{7,3},{8,12},{9,13},{10,... | collective-permute-start | bytes 491528 | tf_op jit(solution)/shard_map/ppermute | solution.py:85
  83.4 98.1 %collective-permute-start.7 = (bf16[2,320,128]{2,1,0:T(8,128)(2,1)S(1)}, bf16[2,320,128]{2,1,0:T(8,128)(2,1)S(1)}, u32[]{:S(2)}, u32[]{:S(2)}) collective-permute-start(bf16[2,320,128]{2,1,0:T(8,128)(2,1)S(1)} %get-tuple-element.41), channel_id=1, source_target_pairs={{0,5},{1,6},{2,7},{3,0},{4,1},{5,2},{6,3},{7,4},{8,13},{9,14},{10,... | collective-permute-start | bytes 491528 | tf_op jit(solution)/shard_map/ppermute | solution.py:85
  85.1 18.0 %all-to-all-start.4 = ((bf16[32,4,1024]{2,1,0:T(4,128)(2,1)}), bf16[32,4,1024]{2,1,0:T(4,128)(2,1)S(1)}, u32[]{:S(2)}, u32[]{:S(2)}) async-start(bf16[32,4,1024]{2,1,0:T(4,128)(2,1)} %get-tuple-element.50), calls=%async_computation.4 | async-start | bytes 524288 | tf_op jit(solution)/shard_map/all_to_all | solution.py:173
  90.7 72.0 %all-gather.10.cloned.1.call-start = ((), (), s32[]{:S(2)}) async-start(), calls=%async_computation.9 | async-start | bytes 1310720 | tf_op jit(solution)/shard_map/all_gather | solution.py:174
  103.9 19.2 %collective-permute-start = (bf16[1024,352]{0,1:T(8,128)(2,1)S(1)}, bf16[1024,352]{0,1:T(8,128)(2,1)}, u32[]{:S(2)}, u32[]{:S(2)}) collective-permute-start(bf16[1024,352]{0,1:T(8,128)(2,1)S(1)} %copy-done.17), channel_id=1, source_target_pairs={{0,8},{8,0},{16,24},{24,16},{32,40},{40,32},{48,56},{56,48},{64,72... | collective-permute-start | bytes 2162696 | tf_op jit(solution)/shard_map/ppermute | solution.py:160
  105.8 32.7 %collective-permute-start.1 = (bf16[1024,352]{0,1:T(8,128)(2,1)}, bf16[1024,352]{0,1:T(8,128)(2,1)}, u32[]{:S(2)}, u32[]{:S(2)}) collective-permute-start(bf16[1024,352]{0,1:T(8,128)(2,1)} %param.34), channel_id=1, source_target_pairs={{0,8},{8,0},{16,24},{24,16},{32,40},{40,32},{48,56},{56,48},{64,72... | collective-permute-start | bytes 2162696 | tf_op jit(solution)/shard_map/ppermute | solution.py:161
  107.3 45.8 %collective-permute-start.2 = (bf16[352,1024]{1,0:T(8,128)(2,1)}, bf16[352,1024]{1,0:T(8,128)(2,1)}, u32[]{:S(2)}, u32[]{:S(2)}) collective-permute-start(bf16[352,1024]{1,0:T(8,128)(2,1)} %param.35), channel_id=1, source_target_pairs={{0,8},{8,0},{16,24},{24,16},{32,40},{40,32},{48,56},{56,48},{64,72... | collective-permute-start | bytes 2162696 | tf_op jit(solution)/shard_map/ppermute | solution.py:162
  109.2 73.0 %collective-permute-start.8 = (bf16[2,320,128]{2,1,0:T(8,128)(2,1)S(1)}, bf16[2,320,128]{2,1,0:T(8,128)(2,1)S(1)}, u32[]{:S(2)}, u32[]{:S(2)}) collective-permute-start(bf16[2,320,128]{2,1,0:T(8,128)(2,1)S(1)} %get-tuple-element.40), channel_id=1, source_target_pairs={{0,6},{1,7},{2,0},{3,1},{4,2},{5,3},{6,4},{7,5},{8,14},{9,15},{10,... | collective-permute-start | bytes 491528 | tf_op jit(solution)/shard_map/ppermute | solution.py:85
  123.1 59.8 %collective-permute-start.9 = (bf16[2,320,128]{2,1,0:T(8,128)(2,1)S(1)}, bf16[2,320,128]{2,1,0:T(8,128)(2,1)}, u32[]{:S(2)}, u32[]{:S(2)}) collective-permute-start(bf16[2,320,128]{2,1,0:T(8,128)(2,1)S(1)} %get-tuple-element.39), channel_id=1, source_target_pairs={{0,7},{1,0},{2,1},{3,2},{4,3},{5,4},{6,5},{7,6},{8,15},{9,8},{10,9... | collective-permute-start | bytes 491528 | tf_op jit(solution)/shard_map/ppermute | solution.py:85
  158.9 18.3 %all-to-all-start.2 = ((bf16[4,32,4,1024]{3,2,1,0:T(4,128)(2,1)}), bf16[4,32,4,1024]{3,2,1,0:T(4,128)(2,1)S(1)}, u32[]{:S(2)}, u32[]{:S(2)}) async-start(bf16[4,32,4,1024]{3,2,1,0:T(4,128)(2,1)} %reshape.449), calls=%async_computation.2 | async-start | bytes 2097152 | tf_op jit(solution)/shard_map/all_to_all | solution.py:183
  177.2 7.3 %copy-start.1 = (bf16[4,32,4,1024]{3,2,1,0:T(4,128)(2,1)}, bf16[4,32,4,1024]{3,2,1,0:T(4,128)(2,1)S(1)}, u32[]{:S(2)}) copy-start(bf16[4,32,4,1024]{3,2,1,0:T(4,128)(2,1)S(1)} %all-to-all-done.2) | copy-start | bytes 3145732
  177.2 18.3 %all-to-all-start.5 = ((bf16[4,32,4,1024]{3,2,1,0:T(4,128)(2,1)}), bf16[4,32,4,1024]{3,2,1,0:T(4,128)(2,1)}, u32[]{:S(2)}, u32[]{:S(2)}) async-start(bf16[4,32,4,1024]{3,2,1,0:T(4,128)(2,1)} %reshape.451), calls=%async_computation.5 | async-start | bytes 2097152 | tf_op jit(solution)/shard_map/all_to_all | solution.py:183
  195.5 16.6 %all-to-all-start.3 = ((bf16[32,4,1024]{2,1,0:T(4,128)(2,1)}), bf16[32,4,1024]{2,1,0:T(4,128)(2,1)S(1)}, u32[]{:S(2)}, u32[]{:S(2)}) async-start(bf16[32,4,1024]{2,1,0:T(4,128)(2,1)} %reduce_sum.96), calls=%async_computation.3 | async-start | bytes 524288 | tf_op jit(solution)/shard_map/all_to_all | solution.py:187
  212.1 15.6 %all-to-all-start.6 = ((bf16[32,4,1024]{2,1,0:T(4,128)(2,1)}), bf16[32,4,1024]{2,1,0:T(4,128)(2,1)S(1)}, u32[]{:S(2)}, u32[]{:S(2)}) async-start(bf16[32,4,1024]{2,1,0:T(4,128)(2,1)} %reduce_sum.98), calls=%async_computation.6 | async-start | bytes 524288 | tf_op jit(solution)/shard_map/all_to_all | solution.py:187
  (6 other events, 12.6 us)
Sparse Core Ops, SparseCore 0:
  9.9 30.7 all-gather.5
  71.7 33.6 all-gather.7
  107.8 21.2 all-gather.9

commit v5 on v3

--- a/solution.py
+++ b/solution.py
@@ -115,6 +115,15 @@
     new_keys, new_values = to_positions(grown_keys, grown_values)
     chosen_keys = jnp.take(prefix_keys, group_ids, axis=0)
     chosen_values = jnp.take(prefix_values, group_ids, axis=0)
+    groups = lax.axis_size(("head", "blk"))
+    full_weight = lax.all_to_all(
+        jnp.broadcast_to(out_weight[None], (groups,) + out_weight.shape),
+        ("head", "blk"),
+        split_axis=0,
+        concat_axis=0,
+        tiled=True,
+    ).reshape(groups * out_weight.shape[0], out_weight.shape[1])
+    full_weight, query = lax.optimization_barrier((full_weight, query))
     attended = attend_request(
         (
             query[0],
@@ -130,7 +139,6 @@
     requests_here = x_tokens.shape[0]
     rows_here = x_tokens.shape[1]
     width = x_tokens.shape[2]
-    full_weight = lax.all_gather(out_weight, ("head", "blk"), axis=0, tiled=True)
     by_token = lax.all_to_all(attended, ("head", "blk"), split_axis=1, concat_axis=2, tiled=True)
     projected = jnp.einsum(
         "rqf,fd->rqd", by_token, full_weight, preferred_element_type=jnp.float32
@@ -166,7 +174,14 @@
     step = slots_here // holders
     outgoing = buffer.reshape(experts * holders, step, width)
     arrived = lax.all_to_all(outgoing, "req", split_axis=0, concat_axis=0, tiled=True)
-    gathered = lax.all_gather(arrived, "head", axis=0, tiled=False)
+    peers = lax.axis_size("head")
+    gathered = lax.all_to_all(
+        jnp.broadcast_to(arrived[None], (peers,) + arrived.shape),
+        "head",
+        split_axis=0,
+        concat_axis=0,
+        tiled=True,
+    )
     flat_rows = gathered.reshape(-1, width)
     gate_val = jnp.einsum("nd,sdf->snf", flat_rows, both_gate, preferred_element_type=jnp.float32)
     up_val = jnp.einsum("nd,sdf->snf", flat_rows, both_up, preferred_element_type=jnp.float32)

time: 215 us -> 210 us (0.977)
  blocking collectives: 28.2 us -> 0 us
  starting transfers between devices: 23.3 us -> 47.3 us
  between operations: 16 us -> 2.52 us
  waiting for transfers between devices: 76.8 us -> 83.8 us
  local copies, waits for them, and re-layouts: 21.5 us -> 27.2 us
    all_to_all x1 -> x0, blocking collectives: 28.2 us -> none  [layer(): lax.all_to_all(outgoing, 'req', split_axis=0, concat_axis=0, tiled=True)]
    all_to_all x0 -> x3, waiting for transfers between devices: none -> 25.4 us  [the longest x1 16 us: layer(): lax.all_to_all(jnp.broadcast_to(out_weight[None], (groups,) + out_weight....]
    all_to_all x0 -> x3, starting transfers between devices: none -> 19.8 us  [the longest x1 11.6 us: layer(): lax.all_to_all(outgoing, 'req', split_axis=0, concat_axis=0, tiled=True)]
    ppermute x7, waiting for transfers between devices: 24.1 us -> 38 us  [to_positions(): blocks.append(lax.ppermute(block, ('head', 'blk'), perm))]
    all_gather x2 -> x0, waiting for transfers between devices: 12.6 us -> none  [the longest x1 12.6 us: layer(): gathered = lax.all_gather(arrived, 'head', axis=0, tiled=False)]
    ppermute x1, waiting for transfers between devices: 11 us -> 0.01 us  [layer(): other_down = lax.ppermute(expert_down, 'req', pair)]
    ppermute x1, waiting for transfers between devices: 8.96 us -> 0.01 us  [layer(): other_gate = lax.ppermute(expert_gate, 'req', pair)]
    broadcast_in_dim x0 -> x2, local copies, waits for them, and re-layouts: none -> 4.15 us  [the longest x1 2.55 us: layer(): jnp.broadcast_to(out_weight[None], (groups,) + out_weight.shape)]
  transfers between devices with their start and end apart: 15 -> 16, of which waited for: 7 -> 7; matrix products, arithmetic and copies ran while one was open for 28% -> 21% of each run, Pallas kernels for 0% -> 0%
where the time goes in v5:
time: 210 us; the launch traced here: 207 us
  waiting for transfers between devices  83.8 us (40%)
  starting transfers between devices  47.3 us (23%)
  matrix products  29.7 us (14%)
  local copies, waits for them, and re-layouts  27.2 us (13%)
  other arithmetic  16.6 us (8%)
  between operations  2.52 us (1%)
    ppermute x7, waiting for transfers between devices, to_positions(): blocks.append(lax.ppermute(block, ('head', 'blk'), perm))  38 us
    all_to_all x1, waiting for transfers between devices, layer(): lax.all_to_all(jnp.broadcast_to(out_weight[None], (groups,) + out_weight....  16 us
    all_to_all x1, waiting for transfers between devices, layer(): lax.all_to_all(full_sum, 'req', split_axis=0, concat_axis=0, tiled=True)  14.4 us
    unnamed x56, local copies, waits for them, and re-layouts  12.2 us
    all_to_all x1, starting transfers between devices, layer(): lax.all_to_all(outgoing, 'req', split_axis=0, concat_axis=0, tiled=True)  11.6 us
    sub x1, matrix products, attend_request(): weights = jnp.where(visible[None], jnp.exp(scores - highest), 0.0)  10.7 us
    ppermute x7, starting transfers between devices, to_positions(): blocks.append(lax.ppermute(block, ('head', 'blk'), perm))  9.82 us
    dot_general x1, matrix products, layer(): jnp.einsum('snf,sfd->snd', hidden, both_down, preferred_element_type=jnp....  8.72 us
  transfers between devices with their start and end apart: 16, of which 7 were waited for; matrix products, arithmetic and copies ran while one was open for 21% of the time, Pallas kernels for 0%

profile of v5, /device:TPU:4, one launch (start us, length us, event | category | flops | bytes accessed | tf_op | source)
XLA Modules:
  0.0 207.1 jit_solution(6164763747944178579)
XLA Ops:
  0.6 2.6 %broadcast_in_dim.106 = bf16[8,128,1024]{2,1,0:T(8,128)(2,1)} broadcast(bf16[128,1024]{1,0:T(8,128)(2,1)} %param.30), dimensions={1,2} | broadcast | bytes 2359296 | tf_op jit(solution)/shard_map/broadcast_in_dim | solution.py:120
  3.2 4.6 %all-to-all-start = ((bf16[8,128,1024]{2,1,0:T(8,128)(2,1)}), bf16[8,128,1024]{2,1,0:T(8,128)(2,1)S(1)}, u32[]{:S(2)}, u32[]{:S(2)}) async-start(bf16[8,128,1024]{2,1,0:T(8,128)(2,1)} %broadcast_in_dim.106), calls=%async_computation | async-start | bytes 4194304 | tf_op jit(solution)/shard_map/all_to_all | solution.py:119
  16.6 2.5 %fusion.10 = pred[512,3072]{1,0:T(8,128)(4,1)} fusion(s32[3072]{0:T(1024)S(1)} %iota_add_fusion, pred[3072]{0:T(1024)(128)(4,1)S(1)} %get-tuple-element.57, pred[3072]{0:T(1024)(128)(4,1)S(1)} %get-tuple-element.58), kind=kLoop, calls=%fused_computation.15 | loop fusion | flops 4718592 | bytes 1591296 | tf_op jit(solution)/shard_map/or | solution.py:45
  19.0 16.0 %all-to-all-done = bf16[8,128,1024]{2,1,0:T(8,128)(2,1)S(1)} async-done(((bf16[8,128,1024]{2,1,0:T(8,128)(2,1)}), bf16[8,128,1024]{2,1,0:T(8,128)(2,1)S(1)}, u32[]{:S(2)}, u32[]{:S(2)}) %all-to-all-start) | async-done | bytes 2097184 | tf_op jit(solution)/shard_map/all_to_all | solution.py:119
  35.8 10.7 %fusion.91 = (f32[2,512]{1,0:T(2,128)S(1)}, bf16[2,512,3072]{2,1,0:T(8,128)(2,1)}) fusion(pred[512,3072]{1,0:T(8,128)(4,1)} %fusion.10, bf16[512,2,64]{0,2,1:T(8,128)(2,1)} %bitcast.156, bf16[512,2,64]{0,2,1:T(8,128)(2,1)S(1)} %bitcast.152, bf16[2048,2,64]{0,2,1:T(8,128)(2,1)S(1)} %bitcast.149, bf16[512,2,64]{0,2,1:T(8,128)(2,1)} %bitcast.155), kind=kOutput, calls=%fused_computation.151 | convolution fusion | flops 832048128 | bytes 8785920 | tf_op jit(solution)/shard_map/sub | solution.py:53
  46.5 4.9 %fusion.40 = bf16[512,2,64]{0,2,1:T(8,128)(2,1)S(1)} fusion(bf16[2,512,3072]{2,1,0:T(8,128)(2,1)} %get-tuple-element.54, bf16[512,2,64]{0,2,1:T(8,128)(2,1)S(1)} %bitcast.153, bf16[2048,2,64]{0,2,1:T(8,128)(2,1)S(1)} %bitcast.150, bf16[512,2,64]{0,2,1:T(8,128)(2,1)} %bitcast.154, f32[512,2]{0,1:T(2,128)S(1)} %bitcast.157), kind=kOutput, calls=%fused_computation.49 | convolution fusion | flops 405143552 | bytes 7213056 | tf_op jit(solution)/shard_map/hqk,khd->qhd/dot_general | solution.py:56
  52.1 1.4 reduce.4
  54.2 3.4 %all-to-all-start.1 = ((bf16[8,2,4096]{2,1,0:T(2,128)(2,1)}), bf16[8,2,4096]{2,1,0:T(2,128)(2,1)S(1)}, u32[]{:S(2)}, u32[]{:S(2)}) async-start(bf16[8,2,4096]{2,1,0:T(2,128)(2,1)} %reshape.579), calls=%async_computation.1 | async-start | bytes 262144 | tf_op jit(solution)/shard_map/all_to_all | solution.py:142
  57.6 6.0 %all-to-all-done.1 = bf16[8,2,4096]{2,1,0:T(2,128)(2,1)S(1)} async-done(((bf16[8,2,4096]{2,1,0:T(2,128)(2,1)}), bf16[8,2,4096]{2,1,0:T(2,128)(2,1)S(1)}, u32[]{:S(2)}, u32[]{:S(2)}) %all-to-all-start.1) | async-done | bytes 131104 | tf_op jit(solution)/shard_map/all_to_all | solution.py:142
  66.2 2.0 scatter_custom_fusion
  68.2 11.6 %all-to-all-start.2 = ((bf16[32,8,1024]{2,1,0:T(8,128)(2,1)}), bf16[32,8,1024]{2,1,0:T(8,128)(2,1)S(1)}, u32[]{:S(2)}, u32[]{:S(2)}) async-start(bf16[32,8,1024]{2,1,0:T(8,128)(2,1)} %bitcast.26), calls=%async_computation.2 | async-start | bytes 1048576 | tf_op jit(solution)/shard_map/all_to_all | solution.py:176
  79.8 1.4 collective-permute-start.2
  83.4 4.5 %fusion.54 = (bf16[1,2560,128]{2,1,0:T(8,128)(2,1)S(1)}, bf16[1,2560,128]{2,1,0:T(8,128)(2,1)S(1)}) fusion(s32[]{:T(128)} %bitcast.41, bf16[1,2048,128]{2,1,0:T(8,128)(2,1)S(1)} %broadcast.378, bf16[1,512,128]{2,1,0:T(8,128)(2,1)} %param.22, bf16[1,2048,128]{2,1,0:T(8,128)(2,1)S(1)} %copy-done.4, pred[2560]{0:T(1024)(128)(4,1)S(1)} %iota_compare_fusion.4, ...), kind=kLoop, calls=%fused_computation.60 | loop fusion | flops 4587520 | bytes 3148292 | tf_op jit(solution)/shard_map/vmap(jit(_where))/select_n | solution.py:72
  87.9 8.5 %all-to-all-done.2 = bf16[32,8,1024]{2,1,0:T(8,128)(2,1)S(1)} async-done(((bf16[32,8,1024]{2,1,0:T(8,128)(2,1)}), bf16[32,8,1024]{2,1,0:T(8,128)(2,1)S(1)}, u32[]{:S(2)}, u32[]{:S(2)}) %all-to-all-start.2) | async-done | bytes 524320 | tf_op jit(solution)/shard_map/all_to_all | solution.py:176
  96.4 1.6 broadcast_in_dim.112
  98.0 3.6 %all-to-all-start.3 = ((bf16[4,32,8,1024]{3,2,1,0:T(8,128)(2,1)}), bf16[4,32,8,1024]{3,2,1,0:T(8,128)(2,1)S(1)}, u32[]{:S(2)}, u32[]{:S(2)}) async-start(bf16[4,32,8,1024]{3,2,1,0:T(8,128)(2,1)} %broadcast_in_dim.112), calls=%async_computation.3 | async-start | bytes 4194304 | tf_op jit(solution)/shard_map/all_to_all | solution.py:178
  102.8 2.0 collective-permute-start.4
  105.4 20.3 %collective-permute-done.3 = bf16[2,320,128]{2,1,0:T(8,128)(2,1)} collective-permute-done((bf16[2,320,128]{2,1,0:T(8,128)(2,1)}, bf16[2,320,128]{2,1,0:T(8,128)(2,1)}, u32[]{:S(2)}, u32[]{:S(2)}) %collective-permute-start.3) | collective-permute-done | bytes 163872 | tf_op jit(solution)/shard_map/ppermute | solution.py:85
  126.7 1.8 collective-permute-start.6
  129.4 4.6 %fusion.23 = f32[2,352,1024]{2,1,0:T(8,128)} fusion(bf16[1024,1024,1]{1,0,2:T(8,128)(2,1)S(1)} %bitcast.142, bf16[1,1024,352]{1,2,0:T(8,128)(2,1)} %bitcast.22, bf16[1,1024,352]{1,2,0:T(8,128)(2,1)} %bitcast.21), kind=kOutput, calls=%fused_computation.29 | convolution fusion | flops 1477115904 | bytes 6422528 | tf_op jit(solution)/shard_map/nd,sdf->snf/dot_general | solution.py:186
  134.0 2.0 collective-permute-start.7
  136.0 2.3 %collective-permute-start.8 = (bf16[2,320,128]{2,1,0:T(8,128)(2,1)}, bf16[2,320,128]{2,1,0:T(8,128)(2,1)}, u32[]{:S(2)}, u32[]{:S(2)}) collective-permute-start(bf16[2,320,128]{2,1,0:T(8,128)(2,1)} %get-tuple-element.44), channel_id=1, source_target_pairs={{0,6},{1,7},{2,0},{3,1},{4,2},{5,3},{6,4},{7,5},{8,14},{9,15},{10,... | collective-permute-start | bytes 491528 | tf_op jit(solution)/shard_map/ppermute | solution.py:85
  138.3 8.7 %convert_reduce_fusion = bf16[1024,1024]{1,0:T(8,128)(2,1)} fusion(bf16[1,352,1024]{2,1,0:T(8,128)(2,1)} %bitcast.35, bf16[1,352,1024]{2,1,0:T(8,128)(2,1)} %bitcast.34, f32[2,352,1024]{2,1,0:T(8,128)} %fusion.23, bf16[1024,1024,1]{1,0,2:T(8,128)(2,1)S(1)} %bitcast.143, bf16[1,1024,352]{1,2,0:T(8,128)(2,1)} %bitcast.31, bf16[1,1024,352]{1,2,0:T(8,128)(2,1)} %bitcast.30), kind=kOutput, calls=%fused_computation.18 | convolution fusion | flops 2964586496 | bytes 9961472 | tf_op jit(solution)/shard_map/snf,sfd->snd/dot_general | solution.py:189
  147.0 3.6 %all-to-all-start.4 = ((bf16[4,32,8,1024]{3,2,1,0:T(8,128)(2,1)}), bf16[4,32,8,1024]{3,2,1,0:T(8,128)(2,1)S(1)}, u32[]{:S(2)}, u32[]{:S(2)}) async-start(bf16[4,32,8,1024]{3,2,1,0:T(8,128)(2,1)} %bitcast.144), calls=%async_computation.4 | async-start | bytes 4194304 | tf_op jit(solution)/shard_map/all_to_all | solution.py:193
  150.7 1.8 collective-permute-start.9
  157.2 17.7 %collective-permute-done.9 = bf16[2,320,128]{2,1,0:T(8,128)(2,1)S(1)} collective-permute-done((bf16[2,320,128]{2,1,0:T(8,128)(2,1)}, bf16[2,320,128]{2,1,0:T(8,128)(2,1)S(1)}, u32[]{:S(2)}, u32[]{:S(2)}) %collective-permute-start.9) | collective-permute-done | bytes 163872 | tf_op jit(solution)/shard_map/ppermute | solution.py:85
  174.9 1.8 gather_fusion.1
  176.7 1.5 select_bitcast_fusion
  178.2 1.3 reduce_sum.72
  179.5 7.3 %all-to-all-start.5 = ((bf16[32,8,1024]{2,1,0:T(8,128)(2,1)}), bf16[32,8,1024]{2,1,0:T(8,128)(2,1)S(1)}, u32[]{:S(2)}, u32[]{:S(2)}) async-start(bf16[32,8,1024]{2,1,0:T(8,128)(2,1)} %reduce_sum.72), calls=%async_computation.5 | async-start | bytes 1048576 | tf_op jit(solution)/shard_map/all_to_all | solution.py:197
  188.3 1.3 gather_fusion.2
  190.0 14.4 %all-to-all-done.5 = bf16[32,8,1024]{2,1,0:T(8,128)(2,1)S(1)} async-done(((bf16[32,8,1024]{2,1,0:T(8,128)(2,1)}), bf16[32,8,1024]{2,1,0:T(8,128)(2,1)S(1)}, u32[]{:S(2)}, u32[]{:S(2)}) %all-to-all-start.5) | async-done | bytes 524320 | tf_op jit(solution)/shard_map/all_to_all | solution.py:197
  (123 shorter events, 27.0 us)
Async XLA Ops:
  0.6 187.5 %copy-start = (bf16[1024,16]{0,1:T(8,128)(2,1)S(1)}, bf16[1024,16]{0,1:T(8,128)(2,1)}, u32[]{:S(2)}) copy-start(bf16[1024,16]{0,1:T(8,128)(2,1)} %param.32) | copy-start | bytes 98308
  3.2 5.3 %copy-start.9 = (bf16[1,512,128]{2,1,0:T(8,128)(2,1)S(1)}, bf16[1,512,128]{2,1,0:T(8,128)(2,1)}, u32[]{:S(2)}) copy-start(bf16[1,512,128]{2,1,0:T(8,128)(2,1)} %param.22) | copy-start | bytes 393220
  3.2 6.1 %copy-start.3 = (bf16[1,2048,128]{2,1,0:T(8,128)(2,1)S(1)}, bf16[1,2048,128]{2,1,0:T(8,128)(2,1)}, u32[]{:S(2)}) copy-start(bf16[1,2048,128]{2,1,0:T(8,128)(2,1)} %param.24) | copy-start | bytes 1572868
  3.2 31.8 %all-to-all-start = ((bf16[8,128,1024]{2,1,0:T(8,128)(2,1)}), bf16[8,128,1024]{2,1,0:T(8,128)(2,1)S(1)}, u32[]{:S(2)}, u32[]{:S(2)}) async-start(bf16[8,128,1024]{2,1,0:T(8,128)(2,1)} %broadcast_in_dim.106), calls=%async_computation | async-start | bytes 4194304 | tf_op jit(solution)/shard_map/all_to_all | solution.py:119
  7.8 4.9 %copy-start.10 = (bf16[1,512,128]{2,1,0:T(8,128)(2,1)S(1)}, bf16[1,512,128]{2,1,0:T(8,128)(2,1)}, u32[]{:S(2)}) copy-start(bf16[1,512,128]{2,1,0:T(8,128)(2,1)} %param.23) | copy-start | bytes 393220
  7.8 5.7 %copy-start.5 = (bf16[1,2048,128]{2,1,0:T(8,128)(2,1)S(1)}, bf16[1,2048,128]{2,1,0:T(8,128)(2,1)}, u32[]{:S(2)}) copy-start(bf16[1,2048,128]{2,1,0:T(8,128)(2,1)} %param.25) | copy-start | bytes 1572868
  9.3 6.0 %copy-start.17 = (s32[1,64,2]{1,2,0:T(2,128)S(1)}, s32[1,64,2]{1,2,0:T(2,128)}, u32[]{:S(2)}) copy-start(s32[1,64,2]{1,2,0:T(2,128)} %param.36) | copy-start | bytes 1540
  9.3 6.5 %copy-start.19 = (s32[1,64,2]{1,2,0:T(2,128)S(1)}, s32[1,64,2]{1,2,0:T(2,128)}, u32[]{:S(2)}) copy-start(s32[1,64,2]{1,2,0:T(2,128)} %param.37) | copy-start | bytes 1540
  13.5 21.5 %copy-start.14 = (bf16[1,512,128]{2,1,0:T(8,128)(2,1)S(1)}, bf16[1,512,128]{2,1,0:T(8,128)(2,1)}, u32[]{:S(2)}) copy-start(bf16[1,512,128]{2,1,0:T(8,128)(2,1)} %param.21) | copy-start | bytes 393220
  13.5 22.2 %copy-start.11 = (bf16[1,2048,128]{1,2,0:T(8,128)(2,1)S(1)}, bf16[1,2048,128]{1,2,0:T(8,128)(2,1)}, u32[]{:S(2)}) copy-start(bf16[1,2048,128]{1,2,0:T(8,128)(2,1)} %copy.96) | copy-start | bytes 1572868
  15.3 20.4 %copy-start.15 = (bf16[1,512,128]{1,2,0:T(8,128)(2,1)S(1)}, bf16[1,512,128]{1,2,0:T(8,128)(2,1)}, u32[]{:S(2)}) copy-start(bf16[1,512,128]{1,2,0:T(8,128)(2,1)} %copy.97) | copy-start | bytes 393220
  35.8 10.7 %copy-start.12 = (bf16[1,2048,128]{1,2,0:T(8,128)(2,1)S(1)}, bf16[1,2048,128]{1,2,0:T(8,128)(2,1)}, u32[]{:S(2)}) copy-start(bf16[1,2048,128]{1,2,0:T(8,128)(2,1)} %copy.92) | copy-start | bytes 1572868
  35.8 10.7 %copy-start.16 = (bf16[1,512,128]{1,2,0:T(8,128)(2,1)S(1)}, bf16[1,512,128]{1,2,0:T(8,128)(2,1)}, u32[]{:S(2)}) copy-start(bf16[1,512,128]{1,2,0:T(8,128)(2,1)} %copy.93) | copy-start | bytes 393220
  51.4 12.5 %copy-start.13 = (bf16[1,64,1024]{2,1,0:T(8,128)(2,1)S(1)}, bf16[1,64,1024]{2,1,0:T(8,128)(2,1)}, u32[]{:S(2)}) copy-start(bf16[1,64,1024]{2,1,0:T(8,128)(2,1)} %param.20) | copy-start | bytes 393220
  54.2 9.4 %all-to-all-start.1 = ((bf16[8,2,4096]{2,1,0:T(2,128)(2,1)}), bf16[8,2,4096]{2,1,0:T(2,128)(2,1)S(1)}, u32[]{:S(2)}, u32[]{:S(2)}) async-start(bf16[8,2,4096]{2,1,0:T(2,128)(2,1)} %reshape.579), calls=%async_computation.1 | async-start | bytes 262144 | tf_op jit(solution)/shard_map/all_to_all | solution.py:142
  63.7 1.5 copy-start.18
  66.1 17.3 %copy-start.4 = (bf16[1,2048,128]{2,1,0:T(8,128)(2,1)S(1)}, bf16[1,2048,128]{2,1,0:T(8,128)(2,1)}, u32[]{:S(2)}) copy-start(bf16[1,2048,128]{2,1,0:T(8,128)(2,1)} %param.24) | copy-start | bytes 1572868
  66.1 17.3 %copy-start.6 = (bf16[1,2048,128]{2,1,0:T(8,128)(2,1)S(1)}, bf16[1,2048,128]{2,1,0:T(8,128)(2,1)}, u32[]{:S(2)}) copy-start(bf16[1,2048,128]{2,1,0:T(8,128)(2,1)} %param.25) | copy-start | bytes 1572868
  68.2 28.2 %all-to-all-start.2 = ((bf16[32,8,1024]{2,1,0:T(8,128)(2,1)}), bf16[32,8,1024]{2,1,0:T(8,128)(2,1)S(1)}, u32[]{:S(2)}, u32[]{:S(2)}) async-start(bf16[32,8,1024]{2,1,0:T(8,128)(2,1)} %bitcast.26), calls=%async_computation.2 | async-start | bytes 1048576 | tf_op jit(solution)/shard_map/all_to_all | solution.py:176
  79.8 54.2 %collective-permute-start.2 = (bf16[352,1024]{1,0:T(8,128)(2,1)}, bf16[352,1024]{1,0:T(8,128)(2,1)}, u32[]{:S(2)}, u32[]{:S(2)}) collective-permute-start(bf16[352,1024]{1,0:T(8,128)(2,1)} %param.35), channel_id=1, source_target_pairs={{0,8},{8,0},{16,24},{24,16},{32,40},{40,32},{48,56},{56,48},{64,72... | collective-permute-start | bytes 2162696 | tf_op jit(solution)/shard_map/ppermute | solution.py:170
  81.2 45.4 %collective-permute-start = (bf16[1024,352]{0,1:T(8,128)(2,1)}, bf16[1024,352]{0,1:T(8,128)(2,1)}, u32[]{:S(2)}, u32[]{:S(2)}) collective-permute-start(bf16[1024,352]{0,1:T(8,128)(2,1)} %param.33), channel_id=1, source_target_pairs={{0,8},{8,0},{16,24},{24,16},{32,40},{40,32},{48,56},{56,48},{64,72... | collective-permute-start | bytes 2162696 | tf_op jit(solution)/shard_map/ppermute | solution.py:168
  82.1 53.9 %collective-permute-start.1 = (bf16[1024,352]{0,1:T(8,128)(2,1)}, bf16[1024,352]{0,1:T(8,128)(2,1)}, u32[]{:S(2)}, u32[]{:S(2)}) collective-permute-start(bf16[1024,352]{0,1:T(8,128)(2,1)} %param.34), channel_id=1, source_target_pairs={{0,8},{8,0},{16,24},{24,16},{32,40},{40,32},{48,56},{56,48},{64,72... | collective-permute-start | bytes 2162696 | tf_op jit(solution)/shard_map/ppermute | solution.py:169
  98.0 31.4 %all-to-all-start.3 = ((bf16[4,32,8,1024]{3,2,1,0:T(8,128)(2,1)}), bf16[4,32,8,1024]{3,2,1,0:T(8,128)(2,1)S(1)}, u32[]{:S(2)}, u32[]{:S(2)}) async-start(bf16[4,32,8,1024]{3,2,1,0:T(8,128)(2,1)} %broadcast_in_dim.112), calls=%async_computation.3 | async-start | bytes 4194304 | tf_op jit(solution)/shard_map/all_to_all | solution.py:178
  102.8 22.9 %collective-permute-start.3 = (bf16[2,320,128]{2,1,0:T(8,128)(2,1)}, bf16[2,320,128]{2,1,0:T(8,128)(2,1)}, u32[]{:S(2)}, u32[]{:S(2)}) collective-permute-start(bf16[2,320,128]{2,1,0:T(8,128)(2,1)} %get-tuple-element.49), channel_id=1, source_target_pairs={{0,1},{1,2},{2,3},{3,4},{4,5},{5,6},{6,7},{7,0},{8,9},{9,10},{10,1... | collective-permute-start | bytes 491528 | tf_op jit(solution)/shard_map/ppermute | solution.py:85
  102.8 47.9 %collective-permute-start.4 = (bf16[2,320,128]{2,1,0:T(8,128)(2,1)}, bf16[2,320,128]{2,1,0:T(8,128)(2,1)}, u32[]{:S(2)}, u32[]{:S(2)}) collective-permute-start(bf16[2,320,128]{2,1,0:T(8,128)(2,1)} %get-tuple-element.48), channel_id=1, source_target_pairs={{0,2},{1,3},{2,4},{3,5},{4,6},{5,7},{6,0},{7,1},{8,10},{9,11},{10,... | collective-permute-start | bytes 491528 | tf_op jit(solution)/shard_map/ppermute | solution.py:85
  125.7 27.6 %collective-permute-start.5 = (bf16[2,320,128]{2,1,0:T(8,128)(2,1)}, bf16[2,320,128]{2,1,0:T(8,128)(2,1)}, u32[]{:S(2)}, u32[]{:S(2)}) collective-permute-start(bf16[2,320,128]{2,1,0:T(8,128)(2,1)} %get-tuple-element.47), channel_id=1, source_target_pairs={{0,3},{1,4},{2,5},{3,6},{4,7},{5,0},{6,1},{7,2},{8,11},{9,12},{10,... | collective-permute-start | bytes 491528 | tf_op jit(solution)/shard_map/ppermute | solution.py:85
  126.7 27.6 %collective-permute-start.6 = (bf16[2,320,128]{2,1,0:T(8,128)(2,1)}, bf16[2,320,128]{2,1,0:T(8,128)(2,1)}, u32[]{:S(2)}, u32[]{:S(2)}) collective-permute-start(bf16[2,320,128]{2,1,0:T(8,128)(2,1)} %get-tuple-element.46), channel_id=1, source_target_pairs={{0,4},{1,5},{2,6},{3,7},{4,0},{5,1},{6,2},{7,3},{8,12},{9,13},{10,... | collective-permute-start | bytes 491528 | tf_op jit(solution)/shard_map/ppermute | solution.py:85
  134.0 21.3 %collective-permute-start.7 = (bf16[2,320,128]{2,1,0:T(8,128)(2,1)}, bf16[2,320,128]{2,1,0:T(8,128)(2,1)}, u32[]{:S(2)}, u32[]{:S(2)}) collective-permute-start(bf16[2,320,128]{2,1,0:T(8,128)(2,1)} %get-tuple-element.45), channel_id=1, source_target_pairs={{0,5},{1,6},{2,7},{3,0},{4,1},{5,2},{6,3},{7,4},{8,13},{9,14},{10,... | collective-permute-start | bytes 491528 | tf_op jit(solution)/shard_map/ppermute | solution.py:85
  136.0 20.2 %collective-permute-start.8 = (bf16[2,320,128]{2,1,0:T(8,128)(2,1)}, bf16[2,320,128]{2,1,0:T(8,128)(2,1)}, u32[]{:S(2)}, u32[]{:S(2)}) collective-permute-start(bf16[2,320,128]{2,1,0:T(8,128)(2,1)} %get-tuple-element.44), channel_id=1, source_target_pairs={{0,6},{1,7},{2,0},{3,1},{4,2},{5,3},{6,4},{7,5},{8,14},{9,15},{10,... | collective-permute-start | bytes 491528 | tf_op jit(solution)/shard_map/ppermute | solution.py:85
  147.0 31.1 %all-to-all-start.4 = ((bf16[4,32,8,1024]{3,2,1,0:T(8,128)(2,1)}), bf16[4,32,8,1024]{3,2,1,0:T(8,128)(2,1)S(1)}, u32[]{:S(2)}, u32[]{:S(2)}) async-start(bf16[4,32,8,1024]{3,2,1,0:T(8,128)(2,1)} %bitcast.144), calls=%async_computation.4 | async-start | bytes 4194304 | tf_op jit(solution)/shard_map/all_to_all | solution.py:193
  150.7 24.2 %collective-permute-start.9 = (bf16[2,320,128]{2,1,0:T(8,128)(2,1)}, bf16[2,320,128]{2,1,0:T(8,128)(2,1)S(1)}, u32[]{:S(2)}, u32[]{:S(2)}) collective-permute-start(bf16[2,320,128]{2,1,0:T(8,128)(2,1)} %get-tuple-element.43), channel_id=1, source_target_pairs={{0,7},{1,0},{2,1},{3,2},{4,3},{5,4},{6,5},{7,6},{8,15},{9,8},{10,9... | collective-permute-start | bytes 491528 | tf_op jit(solution)/shard_map/ppermute | solution.py:85
  179.5 24.8 %all-to-all-start.5 = ((bf16[32,8,1024]{2,1,0:T(8,128)(2,1)}), bf16[32,8,1024]{2,1,0:T(8,128)(2,1)S(1)}, u32[]{:S(2)}, u32[]{:S(2)}) async-start(bf16[32,8,1024]{2,1,0:T(8,128)(2,1)} %reduce_sum.72), calls=%async_computation.5 | async-start | bytes 1048576 | tf_op jit(solution)/shard_map/all_to_all | solution.py:197
  (4 other events, 3.8 us)

commit v6 on v2

--- a/solution.py
+++ b/solution.py
@@ -72,12 +72,13 @@
     return jnp.where((span < length)[:, None], padded_cache, shifted)
 
 
-def to_positions(grown):
+def to_positions(grown_keys, grown_values):
     groups = lax.axis_size(("head", "blk"))
-    lead, rows, width = grown.shape
-    parts = grown.reshape(lead, groups, rows // groups, width)
+    lead, rows, width = grown_keys.shape
+    parts = jnp.stack([grown_keys, grown_values]).reshape(2 * lead, groups, rows // groups, width)
     got = lax.all_to_all(parts, ("head", "blk"), split_axis=1, concat_axis=1, tiled=True)
-    return jnp.transpose(got, (0, 2, 1, 3)).reshape(lead, rows // groups, groups * width)
+    joined = jnp.transpose(got, (0, 2, 1, 3)).reshape(2, lead, rows // groups, groups * width)
+    return joined[0], joined[1]
 
 
 def layer(
@@ -102,8 +103,8 @@
 ):
     grown_keys = jax.vmap(extend)(cache_keys, key_new, history_len)
     grown_values = jax.vmap(extend)(cache_values, value_new, history_len)
-    new_keys = to_positions(grown_keys)
-    new_values = to_positions(grown_values)
+    new_keys, new_values = to_positions(grown_keys, grown_values)
+    new_keys, new_values, query = lax.optimization_barrier((new_keys, new_values, query))
     chosen_keys = jnp.take(prefix_keys, group_ids, axis=0)
     chosen_values = jnp.take(prefix_values, group_ids, axis=0)
     attended = attend_request(

time: 212 us -> 215 us (1.014)
  waiting for transfers between devices: 56.9 us -> 67.3 us
  starting transfers between devices: 22.3 us -> 18.8 us
  local copies, waits for them, and re-layouts: 14.5 us -> 11.8 us
    ppermute x1, waiting for transfers between devices: 5.94 us -> 15.9 us  [layer(): other_gate = lax.ppermute(expert_gate, 'req', pair)]
    all_gather x1, waiting for transfers between devices: 16.2 us -> 9.16 us  [layer(): gathered = lax.all_gather(arrived, 'head', axis=0, tiled=False)]
    ppermute x1, waiting for transfers between devices: 6.72 us -> 12.9 us  [layer(): other_down = lax.ppermute(expert_down, 'req', pair)]
    all_to_all x2 -> x1, starting transfers between devices: 7.08 us -> 4.6 us  [to_positions(): lax.all_to_all(parts, ('head', 'blk'), split_axis=1, concat_axis=1, tiled...]
    unnamed x42 -> x44, local copies, waits for them, and re-layouts: 6.62 us -> 4.41 us
    all_to_all x2 -> x1, waiting for transfers between devices: 9.72 us -> 9.39 us  [to_positions(): lax.all_to_all(parts, ('head', 'blk'), split_axis=1, concat_axis=1, tiled...]
  transfers between devices with their start and end apart: 9 -> 8, of which waited for: 6 -> 7; matrix products, arithmetic and copies ran while one was open for 25% -> 16% of each run, Pallas kernels for 0% -> 0%
where the time goes in v6:
time: 215 us
  waiting for transfers between devices  67.3 us (31%)
  blocking collectives  56.1 us (26%)
  matrix products  29.8 us (14%)
  starting transfers between devices  18.8 us (9%)
  between operations  15.9 us (7%)
  other arithmetic  15 us (7%)
  local copies, waits for them, and re-layouts  11.8 us (5%)
    all_to_all x1, blocking collectives, layer(): lax.all_to_all(outgoing, 'req', split_axis=0, concat_axis=0, tiled=True)  28.2 us
    all_to_all x1, blocking collectives, layer(): lax.all_to_all(pair_sum.reshape(gathered.shape), 'head', split_axis=0, co...  27.9 us
    ppermute x1, waiting for transfers between devices, layer(): other_gate = lax.ppermute(expert_gate, 'req', pair)  15.9 us
    ppermute x1, waiting for transfers between devices, layer(): other_down = lax.ppermute(expert_down, 'req', pair)  12.9 us
    all_to_all x1, waiting for transfers between devices, layer(): lax.all_to_all(full_sum, 'req', split_axis=0, concat_axis=0, tiled=True)  12.4 us
    all_to_all x1, waiting for transfers between devices, to_positions(): lax.all_to_all(parts, ('head', 'blk'), split_axis=1, concat_axis=1, tiled...  9.39 us
    all_gather x1, waiting for transfers between devices, layer(): gathered = lax.all_gather(arrived, 'head', axis=0, tiled=False)  9.16 us
    dot_general x1, matrix products, layer(): jnp.einsum('snf,sfd->snd', hidden, both_down, preferred_element_type=jnp....  8.72 us
  transfers between devices with their start and end apart: 8, of which 7 were waited for; matrix products, arithmetic and copies ran while one was open for 16% of the time, Pallas kernels for 0%

profile of v6, /device:TPU:4, one launch (start us, length us, event | category | flops | bytes accessed | tf_op | source)
XLA Modules:
  0.0 214.7 jit_solution(11611319066609451851)
XLA Ops:
  7.9 5.2 %fusion.67 = (bf16[1,2560,128]{2,1,0:T(8,128)(2,1)S(1)}, bf16[1,2560,128]{2,1,0:T(8,128)(2,1)S(1)}) fusion(s32[]{:T(128)} %bitcast.6, bf16[1,2048,128]{2,1,0:T(8,128)(2,1)S(1)} %broadcast.267, bf16[1,512,128]{2,1,0:T(8,128)(2,1)} %param.22, bf16[1,2048,128]{2,1,0:T(8,128)(2,1)} %param.24, pred[2560]{0:T(1024)(128)(4,1)S(1)} %iota_compare_fusion.4, ...), kind=kLoop, calls=%fused_computation.65 | loop fusion | flops 4587520 | bytes 3148292 | tf_op jit(solution)/shard_map/vmap(jit(_where))/select_n | solution.py:72
  13.1 1.2 pad_maximum_fusion
  14.4 4.6 %all-to-all-start = ((bf16[2,8,320,128]{3,2,0,1:T(8,128)(2,1)}), bf16[2,8,320,128]{3,2,0,1:T(8,128)(2,1)S(1)}, u32[]{:S(2)}, u32[]{:S(2)}) async-start(bf16[2,8,320,128]{3,2,0,1:T(8,128)(2,1)} %pad_maximum_fusion), calls=%async_computation | async-start | bytes 2621440 | tf_op jit(solution)/shard_map/all_to_all | solution.py:79
  19.7 1.0 copy.100
  23.6 1.0 dynamic-slice_select_fusion
  27.0 1.3 fusion.10
  28.3 9.4 %all-to-all-done = bf16[2,8,320,128]{3,2,0,1:T(8,128)(2,1)S(1)} async-done(((bf16[2,8,320,128]{3,2,0,1:T(8,128)(2,1)}), bf16[2,8,320,128]{3,2,0,1:T(8,128)(2,1)S(1)}, u32[]{:S(2)}, u32[]{:S(2)}) %all-to-all-start) | async-done | bytes 1310752 | tf_op jit(solution)/shard_map/all_to_all | solution.py:79
  37.8 1.3 copy_bitcast_fusion
  39.3 8.7 %fusion.101 = (f32[2,512]{1,0:T(2,128)S(1)}, bf16[2,512,3072]{2,1,0:T(8,128)(2,1)}) fusion(pred[512,3072]{1,0:T(8,128)(4,1)S(1)} %fusion.10, bf16[512,2,64]{0,2,1:T(8,128)(2,1)S(1)} %bitcast.131, bf16[512,2,64]{0,2,1:T(8,128)(2,1)S(1)} %bitcast.128, bf16[2048,2,64]{0,2,1:T(8,128)(2,1)S(1)} %bitcast.125, bf16[512,2,64]{0,2,1:T(8,128)(2,1)S(1)} %bitcast.130), kind=kOutput, calls=%fused_computation.128 | convolution fusion | flops 832048128 | bytes 8785920 | tf_op jit(solution)/shard_map/sub | solution.py:53
  47.9 4.8 %fusion.55 = bf16[512,2,64]{0,2,1:T(8,128)(2,1)S(1)} fusion(bf16[2,512,3072]{2,1,0:T(8,128)(2,1)} %get-tuple-element.48, bf16[512,2,64]{0,2,1:T(8,128)(2,1)S(1)} %bitcast.127, bf16[2048,2,64]{0,2,1:T(8,128)(2,1)S(1)} %bitcast.124, bf16[512,2,64]{0,2,1:T(8,128)(2,1)S(1)} %bitcast.129, f32[512,2]{0,1:T(2,128)S(1)} %bitcast.133), kind=kOutput, calls=%fused_computation.54 | convolution fusion | flops 405143552 | bytes 7213056 | tf_op jit(solution)/shard_map/hqk,khd->qhd/dot_general | solution.py:56
  53.5 1.4 reduce.4
  55.6 3.4 %all-to-all-start.1 = ((bf16[8,2,4096]{2,1,0:T(2,128)(2,1)}), bf16[8,2,4096]{2,1,0:T(2,128)(2,1)S(1)}, u32[]{:S(2)}, u32[]{:S(2)}) async-start(bf16[8,2,4096]{2,1,0:T(2,128)(2,1)} %reshape.514), calls=%async_computation.1 | async-start | bytes 262144 | tf_op jit(solution)/shard_map/all_to_all | solution.py:126
  59.2 5.8 %all-to-all-done.1 = bf16[8,2,4096]{2,1,0:T(2,128)(2,1)S(1)} async-done(((bf16[8,2,4096]{2,1,0:T(2,128)(2,1)}), bf16[8,2,4096]{2,1,0:T(2,128)(2,1)S(1)}, u32[]{:S(2)}, u32[]{:S(2)}) %all-to-all-start.1) | async-done | bytes 131104 | tf_op jit(solution)/shard_map/all_to_all | solution.py:126
  65.3 2.2 %multiply_reduce_fusion.1 = (f32[64]{0:T(128)S(1)}, f32[1,64,1024]{2,1,0:T(8,128)S(1)}) fusion(bf16[1024,1024]{1,0:T(8,128)(2,1)} %all-gather.4.cloned.1.call-done, bf16[8,8,8,128]{3,2,1,0:T(8,128)(2,1)S(1)} %bitcast.122, bf16[1,64,1024]{2,1,0:T(8,128)(2,1)S(1)} %copy-done.6), kind=kOutput, calls=%fused_computation.79 | convolution fusion | flops 134479808 | bytes 2621696 | tf_op jit(solution)/shard_map/rqf,fd->rqd/dot_general | solution.py:127
  67.9 1.4 scatter_custom_fusion
  69.2 28.2 %all_to_all.35 = bf16[32,8,1024]{2,1,0:T(8,128)(2,1)} all-to-all(bf16[32,8,1024]{2,1,0:T(8,128)(2,1)S(1)} %bitcast.119), channel_id=1, replica_groups=mesh['req'=32,'head'=4,'blk'=2] {'req'}, dimensions={0} | all-to-all | bytes 1048576 | tf_op jit(solution)/shard_map/all_to_all | solution.py:160
  97.5 1.3 collective-permute-start
  98.7 0.9 collective-permute-start.1
  99.6 1.2 collective-permute-start.2
  100.8 15.9 %collective-permute-done = bf16[1024,352]{0,1:T(8,128)(2,1)} collective-permute-done((bf16[1024,352]{0,1:T(8,128)(2,1)S(1)}, bf16[1024,352]{0,1:T(8,128)(2,1)}, u32[]{:S(2)}, u32[]{:S(2)}) %collective-permute-start) | collective-permute-done | bytes 720928 | tf_op jit(solution)/shard_map/ppermute | solution.py:152
  116.7 9.2 %all-gather.6.cloned.1.call-done = bf16[128,8,1024]{2,1,0:T(8,128)(2,1)} async-done(((bf16[32,8,1024]{2,1,0:T(8,128)(2,1)}), bf16[128,8,1024]{2,1,0:T(8,128)(2,1)}) %all-gather.6.cloned.1.call-update) | async-done | bytes 2097168 | tf_op jit(solution)/shard_map/all_gather | solution.py:161
  125.8 5.3 %fusion.23 = f32[2,352,1024]{2,1,0:T(8,128)} fusion(bf16[128,8,1024]{2,1,0:T(8,128)(2,1)} %all-gather.6.cloned.1.call-done, bf16[1,1024,352]{1,2,0:T(8,128)(2,1)} %bitcast.25, bf16[1,1024,352]{1,2,0:T(8,128)(2,1)S(1)} %bitcast.132), kind=kOutput, calls=%fused_computation.29 | convolution fusion | flops 1477115904 | bytes 6422528 | tf_op jit(solution)/shard_map/nd,sdf->snf/dot_general | solution.py:163
  131.1 1.0 collective-permute-done.1
  132.1 12.9 %collective-permute-done.2 = bf16[352,1024]{1,0:T(8,128)(2,1)} collective-permute-done((bf16[352,1024]{1,0:T(8,128)(2,1)}, bf16[352,1024]{1,0:T(8,128)(2,1)}, u32[]{:S(2)}, u32[]{:S(2)}) %collective-permute-start.2) | collective-permute-done | bytes 720928 | tf_op jit(solution)/shard_map/ppermute | solution.py:154
  145.1 8.7 %convert_reduce_fusion = bf16[1024,1024]{1,0:T(8,128)(2,1)} fusion(f32[2,352,1024]{2,1,0:T(8,128)} %fusion.23, bf16[128,8,1024]{2,1,0:T(8,128)(2,1)S(1)} %copy-done.15, bf16[1,1024,352]{1,2,0:T(8,128)(2,1)} %bitcast.34, bf16[1,1024,352]{1,2,0:T(8,128)(2,1)} %bitcast.33, bf16[1,352,1024]{2,1,0:T(8,128)(2,1)} %bitcast.38, bf16[1,352,1024]{2,1,0:T(8,128)(2,1)} %bitcast.37), kind=kOutput, calls=%fused_computation.17 | convolution fusion | flops 2964586496 | bytes 9961472 | tf_op jit(solution)/shard_map/snf,sfd->snd/dot_general | solution.py:166
  153.8 27.9 %all_to_all.36 = bf16[4,32,8,1024]{3,2,1,0:T(8,128)(2,1)S(1)} all-to-all(bf16[4,32,8,1024]{3,2,1,0:T(8,128)(2,1)} %bitcast.118), channel_id=1, replica_groups=mesh['req'=32,'head'=4,'blk'=2] {'head'}, dimensions={0} | all-to-all | bytes 4194304 | tf_op jit(solution)/shard_map/all_to_all | solution.py:170
  181.7 1.3 reduce_sum.72
  183.0 7.3 %all-to-all-start.4 = ((bf16[32,8,1024]{2,1,0:T(8,128)(2,1)}), bf16[32,8,1024]{2,1,0:T(8,128)(2,1)S(1)}, u32[]{:S(2)}, u32[]{:S(2)}) async-start(bf16[32,8,1024]{2,1,0:T(8,128)(2,1)} %reduce_sum.72), calls=%async_computation.4 | async-start | bytes 1048576 | tf_op jit(solution)/shard_map/all_to_all | solution.py:174
  191.0 1.3 gather_fusion.1
  192.7 12.4 %all-to-all-done.4 = bf16[32,8,1024]{2,1,0:T(8,128)(2,1)S(1)} async-done(((bf16[32,8,1024]{2,1,0:T(8,128)(2,1)}), bf16[32,8,1024]{2,1,0:T(8,128)(2,1)S(1)}, u32[]{:S(2)}, u32[]{:S(2)}) %all-to-all-start.4) | async-done | bytes 524320 | tf_op jit(solution)/shard_map/all_to_all | solution.py:174
  205.2 0.8 gather_fusion
  206.4 0.8 multiply_reduce_fusion
  (90 shorter events, 9.9 us)
Async XLA Ops:
  7.2 183.7 %copy-start = (bf16[1024,16]{0,1:T(8,128)(2,1)S(1)}, bf16[1024,16]{0,1:T(8,128)(2,1)}, u32[]{:S(2)}) copy-start(bf16[1024,16]{0,1:T(8,128)(2,1)} %param.32) | copy-start | bytes 98308
  13.1 6.6 %copy-start.1 = (bf16[1,2048,128]{2,1,0:T(8,128)(2,1)S(1)}, bf16[1,2048,128]{2,1,0:T(8,128)(2,1)}, u32[]{:S(2)}) copy-start(bf16[1,2048,128]{2,1,0:T(8,128)(2,1)} %param.24) | copy-start | bytes 1572868
  14.4 6.4 %copy-start.3 = (bf16[1,512,128]{2,1,0:T(8,128)(2,1)S(1)}, bf16[1,512,128]{2,1,0:T(8,128)(2,1)}, u32[]{:S(2)}) copy-start(bf16[1,512,128]{2,1,0:T(8,128)(2,1)} %param.22) | copy-start | bytes 393220
  14.4 7.2 %copy-start.2 = (bf16[1,2048,128]{2,1,0:T(8,128)(2,1)S(1)}, bf16[1,2048,128]{2,1,0:T(8,128)(2,1)}, u32[]{:S(2)}) copy-start(bf16[1,2048,128]{2,1,0:T(8,128)(2,1)} %param.25) | copy-start | bytes 1572868
  14.4 7.4 %copy-start.4 = (bf16[1,512,128]{2,1,0:T(8,128)(2,1)S(1)}, bf16[1,512,128]{2,1,0:T(8,128)(2,1)}, u32[]{:S(2)}) copy-start(bf16[1,512,128]{2,1,0:T(8,128)(2,1)} %param.23) | copy-start | bytes 393220
  14.4 23.3 %all-to-all-start = ((bf16[2,8,320,128]{3,2,0,1:T(8,128)(2,1)}), bf16[2,8,320,128]{3,2,0,1:T(8,128)(2,1)S(1)}, u32[]{:S(2)}, u32[]{:S(2)}) async-start(bf16[2,8,320,128]{3,2,0,1:T(8,128)(2,1)} %pad_maximum_fusion), calls=%async_computation | async-start | bytes 2621440 | tf_op jit(solution)/shard_map/all_to_all | solution.py:79
  19.0 4.2 %copy-start.12 = (s32[1,64,2]{1,2,0:T(2,128)S(1)}, s32[1,64,2]{1,2,0:T(2,128)}, u32[]{:S(2)}) copy-start(s32[1,64,2]{1,2,0:T(2,128)} %param.36) | copy-start | bytes 1540
  19.0 7.4 %copy-start.14 = (s32[1,64,2]{1,2,0:T(2,128)S(1)}, s32[1,64,2]{1,2,0:T(2,128)}, u32[]{:S(2)}) copy-start(s32[1,64,2]{1,2,0:T(2,128)} %param.37) | copy-start | bytes 1540
  19.0 46.3 %all-gather.4.cloned.1.call-start = ((), (), s32[]{:S(2)}) async-start(), calls=%async_computation.5 | async-start | bytes 2359296 | tf_op jit(solution)/shard_map/all_gather | solution.py:125
  37.8 1.3 copy-start.7
  37.8 1.4 copy-start.5
  37.8 1.4 copy-start.9
  37.8 1.4 copy-start.11
  39.2 8.7 %copy-start.8 = (bf16[1,512,128]{1,2,0:T(8,128)(2,1)S(1)}, bf16[1,512,128]{1,2,0:T(8,128)(2,1)}, u32[]{:S(2)}) copy-start(bf16[1,512,128]{1,2,0:T(8,128)(2,1)} %copy.95) | copy-start | bytes 393220
  39.3 8.7 %copy-start.10 = (bf16[1,512,128]{1,2,0:T(8,128)(2,1)S(1)}, bf16[1,512,128]{1,2,0:T(8,128)(2,1)}, u32[]{:S(2)}) copy-start(bf16[1,512,128]{1,2,0:T(8,128)(2,1)} %copy.93) | copy-start | bytes 393220
  52.8 12.5 %copy-start.6 = (bf16[1,64,1024]{2,1,0:T(8,128)(2,1)S(1)}, bf16[1,64,1024]{2,1,0:T(8,128)(2,1)}, u32[]{:S(2)}) copy-start(bf16[1,64,1024]{2,1,0:T(8,128)(2,1)} %param.20) | copy-start | bytes 393220
  54.9 12.6 %copy-start.13 = (f32[1024]{0:T(1024)S(1)}, f32[1024]{0:T(1024)}, u32[]{:S(2)}) copy-start(f32[1024]{0:T(1024)} %param.31) | copy-start | bytes 12292
  55.6 9.4 %all-to-all-start.1 = ((bf16[8,2,4096]{2,1,0:T(2,128)(2,1)}), bf16[8,2,4096]{2,1,0:T(2,128)(2,1)S(1)}, u32[]{:S(2)}, u32[]{:S(2)}) async-start(bf16[8,2,4096]{2,1,0:T(2,128)(2,1)} %reshape.514), calls=%async_computation.1 | async-start | bytes 262144 | tf_op jit(solution)/shard_map/all_to_all | solution.py:126
  59.0 66.9 %all-gather.6.cloned.1.call-start = ((), (), s32[]{:S(2)}) async-start(), calls=%async_computation.6 | async-start | bytes 2621440 | tf_op jit(solution)/shard_map/all_gather | solution.py:161
  67.5 30.0 %copy-start.16 = (bf16[1024,352]{0,1:T(8,128)(2,1)S(1)}, bf16[1024,352]{0,1:T(8,128)(2,1)}, u32[]{:S(2)}) copy-start(bf16[1024,352]{0,1:T(8,128)(2,1)} %param.33) | copy-start | bytes 2162692
  97.5 19.2 %collective-permute-start = (bf16[1024,352]{0,1:T(8,128)(2,1)S(1)}, bf16[1024,352]{0,1:T(8,128)(2,1)}, u32[]{:S(2)}, u32[]{:S(2)}) collective-permute-start(bf16[1024,352]{0,1:T(8,128)(2,1)S(1)} %copy-done.16), channel_id=1, source_target_pairs={{0,8},{8,0},{16,24},{24,16},{32,40},{40,32},{48,56},{56,48},{64,72... | collective-permute-start | bytes 2162696 | tf_op jit(solution)/shard_map/ppermute | solution.py:152
  98.7 33.4 %collective-permute-start.1 = (bf16[1024,352]{0,1:T(8,128)(2,1)}, bf16[1024,352]{0,1:T(8,128)(2,1)}, u32[]{:S(2)}, u32[]{:S(2)}) collective-permute-start(bf16[1024,352]{0,1:T(8,128)(2,1)} %param.34), channel_id=1, source_target_pairs={{0,8},{8,0},{16,24},{24,16},{32,40},{40,32},{48,56},{56,48},{64,72... | collective-permute-start | bytes 2162696 | tf_op jit(solution)/shard_map/ppermute | solution.py:153
  99.6 45.5 %collective-permute-start.2 = (bf16[352,1024]{1,0:T(8,128)(2,1)}, bf16[352,1024]{1,0:T(8,128)(2,1)}, u32[]{:S(2)}, u32[]{:S(2)}) collective-permute-start(bf16[352,1024]{1,0:T(8,128)(2,1)} %param.35), channel_id=1, source_target_pairs={{0,8},{8,0},{16,24},{24,16},{32,40},{40,32},{48,56},{56,48},{64,72... | collective-permute-start | bytes 2162696 | tf_op jit(solution)/shard_map/ppermute | solution.py:154
  125.8 19.2 %copy-start.15 = (bf16[128,8,1024]{2,1,0:T(8,128)(2,1)S(1)}, bf16[128,8,1024]{2,1,0:T(8,128)(2,1)}, u32[]{:S(2)}) copy-start(bf16[128,8,1024]{2,1,0:T(8,128)(2,1)} %all-gather.6.cloned.1.call-done) | copy-start | bytes 6291460
  183.0 22.1 %all-to-all-start.4 = ((bf16[32,8,1024]{2,1,0:T(8,128)(2,1)}), bf16[32,8,1024]{2,1,0:T(8,128)(2,1)S(1)}, u32[]{:S(2)}, u32[]{:S(2)}) async-start(bf16[32,8,1024]{2,1,0:T(8,128)(2,1)} %reduce_sum.72), calls=%async_computation.4 | async-start | bytes 1048576 | tf_op jit(solution)/shard_map/all_to_all | solution.py:174
Sparse Core Ops, SparseCore 0:
  21.7 31.1 all-gather.3
  97.6 28.2 all-gather.5

commit v7 on v6

--- a/solution.py
+++ b/solution.py
@@ -73,11 +73,28 @@
 
 
 def to_positions(grown_keys, grown_values):
-    groups = lax.axis_size(("head", "blk"))
+    heads = lax.axis_size("head")
+    cores = lax.axis_size("blk")
+    me_h = lax.axis_index("head")
+    me_b = lax.axis_index("blk")
     lead, rows, width = grown_keys.shape
-    parts = jnp.stack([grown_keys, grown_values]).reshape(2 * lead, groups, rows // groups, width)
-    got = lax.all_to_all(parts, ("head", "blk"), split_axis=1, concat_axis=1, tiled=True)
-    joined = jnp.transpose(got, (0, 2, 1, 3)).reshape(2, lead, rows // groups, groups * width)
+    span = rows // (heads * cores)
+    parts = jnp.stack([grown_keys[0], grown_values[0]]).reshape(2, heads, cores, span, width)
+    keep = lax.dynamic_index_in_dim(parts, me_b, axis=2, keepdims=False)
+    sent = lax.dynamic_index_in_dim(parts, 1 - me_b, axis=2, keepdims=False)
+    got = lax.ppermute(sent, "blk", [(0, 1), (1, 0)])
+    first = jnp.where(me_b == 0, keep, got)
+    second = jnp.where(me_b == 0, got, keep)
+    mine = jnp.concatenate([first, second], axis=-1)
+    blocks = [lax.dynamic_index_in_dim(mine, me_h, axis=1, keepdims=False)]
+    for k in range(1, heads):
+        block = lax.dynamic_index_in_dim(mine, (me_h + k) % heads, axis=1, keepdims=False)
+        perm = [(i, (i + k) % heads) for i in range(heads)]
+        blocks.append(lax.ppermute(block, "head", perm))
+    stacked = jnp.stack(blocks, axis=1)
+    order = (me_h - jnp.arange(heads)) % heads
+    by_source = jnp.take(stacked, order, axis=1)
+    joined = jnp.transpose(by_source, (0, 2, 1, 3)).reshape(2, lead, span, heads * cores * width)
     return joined[0], joined[1]
 
 
@@ -104,7 +121,6 @@
     grown_keys = jax.vmap(extend)(cache_keys, key_new, history_len)
     grown_values = jax.vmap(extend)(cache_values, value_new, history_len)
     new_keys, new_values = to_positions(grown_keys, grown_values)
-    new_keys, new_values, query = lax.optimization_barrier((new_keys, new_values, query))
     chosen_keys = jnp.take(prefix_keys, group_ids, axis=0)
     chosen_values = jnp.take(prefix_values, group_ids, axis=0)
     attended = attend_request(

time: 215 us -> 211 us (0.981)
  blocking collectives: 56.1 us -> 28.2 us
  waiting for transfers between devices: 67.3 us -> 78.7 us
  starting transfers between devices: 18.8 us -> 24.9 us
  local copies, waits for them, and re-layouts: 11.8 us -> 15.4 us
  other arithmetic: 15 us -> 17.8 us
    ppermute x0 -> x4, waiting for transfers between devices: none -> 29.3 us  [the longest x3 27.5 us: to_positions(): blocks.append(lax.ppermute(block, 'head', perm))]
    all_to_all x1 -> x0, blocking collectives: 27.9 us -> none  [layer(): lax.all_to_all(pair_sum.reshape(gathered.shape), 'head', split_axis=0, co...]
    all_to_all x1, waiting for transfers between devices: 9.39 us -> 0.01 us  [layer(): lax.all_to_all(pair_sum.reshape(gathered.shape), 'head', split_axis=0, co...]
    ppermute x0 -> x4, starting transfers between devices: none -> 6.19 us  [the longest x3 6.19 us: to_positions(): blocks.append(lax.ppermute(block, 'head', perm))]
    ppermute x1, waiting for transfers between devices: 15.9 us -> 10.1 us  [layer(): other_gate = lax.ppermute(expert_gate, 'req', pair)]
    unnamed x44 -> x43, local copies, waits for them, and re-layouts: 4.41 us -> 6.2 us
  transfers between devices with their start and end apart: 8 -> 12, of which waited for: 7 -> 9; matrix products, arithmetic and copies ran while one was open for 16% -> 21% of each run, Pallas kernels for 0% -> 0%
where the time goes in v7:
time: 211 us; the launch traced here: 210 us
  waiting for transfers between devices  78.7 us (37%)
  matrix products  29.4 us (14%)
  blocking collectives  28.2 us (13%)
  starting transfers between devices  24.9 us (12%)
  other arithmetic  17.8 us (8%)
  between operations  15.9 us (8%)
  local copies, waits for them, and re-layouts  15.4 us (7%)
    all_to_all x1, blocking collectives, layer(): lax.all_to_all(outgoing, 'req', split_axis=0, concat_axis=0, tiled=True)  28.2 us
    ppermute x3, waiting for transfers between devices, to_positions(): blocks.append(lax.ppermute(block, 'head', perm))  27.5 us
    ppermute x1, waiting for transfers between devices, layer(): other_down = lax.ppermute(expert_down, 'req', pair)  12.9 us
    all_to_all x1, waiting for transfers between devices, layer(): lax.all_to_all(full_sum, 'req', split_axis=0, concat_axis=0, tiled=True)  10.9 us
    ppermute x1, waiting for transfers between devices, layer(): other_gate = lax.ppermute(expert_gate, 'req', pair)  10.1 us
    all_gather x1, waiting for transfers between devices, layer(): gathered = lax.all_gather(arrived, 'head', axis=0, tiled=False)  8.97 us
    sub x1, matrix products, attend_request(): weights = jnp.where(visible[None], jnp.exp(scores - highest), 0.0)  8.94 us
    dot_general x1, matrix products, layer(): jnp.einsum('snf,sfd->snd', hidden, both_down, preferred_element_type=jnp....  8.73 us
  transfers between devices with their start and end apart: 12, of which 9 were waited for; matrix products, arithmetic and copies ran while one was open for 21% of the time, Pallas kernels for 0%

profile of v7, /device:TPU:4, one launch (start us, length us, event | category | flops | bytes accessed | tf_op | source)
XLA Modules:
  0.0 210.3 jit_solution(15279838628208335793)
XLA Ops:
  10.4 2.0 copy.108
  13.8 2.8 %fusion.10 = pred[512,3072]{0,1:T(8,128)(4,1)S(1)} fusion(s32[3072]{0:T(1024)S(1)} %iota_add_fusion, pred[3072]{0:T(1024)(128)(4,1)S(1)} %get-tuple-element.51, pred[3072]{0:T(1024)(128)(4,1)S(1)} %get-tuple-element.52), kind=kLoop, calls=%fused_computation.17 | loop fusion | flops 4718592 | bytes 1591296 | tf_op jit(solution)/shard_map/or | solution.py:45
  16.6 8.9 %fusion.111 = (f32[2,512]{1,0:T(2,128)S(1)}, bf16[2,512,3072]{1,2,0:T(8,128)(2,1)}) fusion(pred[512,3072]{0,1:T(8,128)(4,1)S(1)} %fusion.10, bf16[512,2,64]{0,2,1:T(8,128)(2,1)} %bitcast.167, bf16[512,2,64]{0,2,1:T(8,128)(2,1)S(1)} %bitcast.166, bf16[2048,2,64]{0,2,1:T(8,128)(2,1)} %bitcast.158, bf16[512,2,64]{0,2,1:T(8,128)(2,1)S(1)} %bitcast.164), kind=kOutput, calls=%fused_computation.162 | convolution fusion | flops 832048128 | bytes 8785920 | tf_op jit(solution)/shard_map/sub | solution.py:53
  25.6 4.0 %fusion.55 = bf16[512,2,64]{0,2,1:T(8,128)(2,1)S(1)} fusion(bf16[2,512,3072]{1,2,0:T(8,128)(2,1)} %get-tuple-element.48, bf16[512,2,64]{0,2,1:T(8,128)(2,1)S(1)} %bitcast.165, bf16[2048,2,64]{0,2,1:T(8,128)(2,1)S(1)} %bitcast.157, bf16[512,2,64]{0,2,1:T(8,128)(2,1)S(1)} %bitcast.163, f32[512,2]{0,1:T(2,128)S(1)} %bitcast.168), kind=kOutput, calls=%fused_computation.67 | convolution fusion | flops 405143552 | bytes 7213056 | tf_op jit(solution)/shard_map/hqk,khd->qhd/dot_general | solution.py:56
  30.3 1.4 reduce.4
  32.4 4.5 %all-to-all-start = ((bf16[8,2,4096]{2,1,0:T(2,128)(2,1)}), bf16[8,2,4096]{2,1,0:T(2,128)(2,1)S(1)}, u32[]{:S(2)}, u32[]{:S(2)}) async-start(bf16[8,2,4096]{2,1,0:T(2,128)(2,1)} %reshape.575), calls=%async_computation | async-start | bytes 262144 | tf_op jit(solution)/shard_map/all_to_all | solution.py:142
  38.1 4.8 %all-to-all-done = bf16[8,2,4096]{2,1,0:T(2,128)(2,1)S(1)} async-done(((bf16[8,2,4096]{2,1,0:T(2,128)(2,1)}), bf16[8,2,4096]{2,1,0:T(2,128)(2,1)S(1)}, u32[]{:S(2)}, u32[]{:S(2)}) %all-to-all-start) | async-done | bytes 131104 | tf_op jit(solution)/shard_map/all_to_all | solution.py:142
  43.3 2.2 %multiply_reduce_fusion.1 = (f32[64]{0:T(128)S(1)}, f32[1,64,1024]{2,1,0:T(8,128)S(1)}) fusion(bf16[1024,1024]{1,0:T(8,128)(2,1)} %all-gather.4.cloned.1.call-done, bf16[8,8,8,128]{3,2,1,0:T(8,128)(2,1)S(1)} %bitcast.155, bf16[1,64,1024]{2,1,0:T(8,128)(2,1)S(1)} %copy-done.10), kind=kOutput, calls=%fused_computation.100 | convolution fusion | flops 134479808 | bytes 2621696 | tf_op jit(solution)/shard_map/rqf,fd->rqd/dot_general | solution.py:143
  47.2 1.4 scatter_custom_fusion
  48.6 28.2 %all_to_all.30 = bf16[32,8,1024]{2,1,0:T(8,128)(2,1)} all-to-all(bf16[32,8,1024]{2,1,0:T(8,128)(2,1)S(1)} %bitcast.150), channel_id=1, replica_groups=mesh['req'=32,'head'=4,'blk'=2] {'req'}, dimensions={0} | all-to-all | bytes 1048576 | tf_op jit(solution)/shard_map/all_to_all | solution.py:176
  76.8 1.3 collective-permute-start
  78.9 1.2 collective-permute-start.2
  80.2 5.8 %fusion.67 = (bf16[1,2560,128]{2,1,0:T(8,128)(2,1)S(1)}, bf16[1,2560,128]{2,1,0:T(8,128)(2,1)S(1)}) fusion(s32[]{:T(128)} %bitcast.41, bf16[1,2048,128]{2,1,0:T(8,128)(2,1)S(1)} %broadcast.374, bf16[1,512,128]{2,1,0:T(8,128)(2,1)S(1)} %copy-done.8, bf16[1,2048,128]{2,1,0:T(8,128)(2,1)S(1)} %copy-done.4, pred[2560]{0:T(1024)(128)(4,1)S(1)} %iota_compare_fusion.4, ...), kind=kLoop, calls=%fused_computation.78 | loop fusion | flops 4587520 | bytes 3148292 | tf_op jit(solution)/shard_map/vmap(jit(_where))/select_n | solution.py:72
  86.1 10.1 %collective-permute-done = bf16[1024,352]{0,1:T(8,128)(2,1)} collective-permute-done((bf16[1024,352]{0,1:T(8,128)(2,1)}, bf16[1024,352]{0,1:T(8,128)(2,1)}, u32[]{:S(2)}, u32[]{:S(2)}) %collective-permute-start) | collective-permute-done | bytes 720928 | tf_op jit(solution)/shard_map/ppermute | solution.py:168
  96.2 9.0 %all-gather.6.cloned.1.call-done = bf16[128,8,1024]{2,1,0:T(8,128)(2,1)} async-done(((bf16[32,8,1024]{2,1,0:T(8,128)(2,1)}), bf16[128,8,1024]{2,1,0:T(8,128)(2,1)}) %all-gather.6.cloned.1.call-update) | async-done | bytes 2097168 | tf_op jit(solution)/shard_map/all_gather | solution.py:177
  105.2 5.5 %fusion.23 = f32[2,352,1024]{2,1,0:T(8,128)} fusion(bf16[128,8,1024]{2,1,0:T(8,128)(2,1)} %all-gather.6.cloned.1.call-done, bf16[1,1024,352]{1,2,0:T(8,128)(2,1)} %bitcast.22, bf16[1,1024,352]{1,2,0:T(8,128)(2,1)} %bitcast.21), kind=kOutput, calls=%fused_computation.32 | convolution fusion | flops 1477115904 | bytes 6422528 | tf_op jit(solution)/shard_map/nd,sdf->snf/dot_general | solution.py:179
  110.6 1.0 collective-permute-done.1
  111.6 12.9 %collective-permute-done.2 = bf16[352,1024]{1,0:T(8,128)(2,1)} collective-permute-done((bf16[352,1024]{1,0:T(8,128)(2,1)}, bf16[352,1024]{1,0:T(8,128)(2,1)}, u32[]{:S(2)}, u32[]{:S(2)}) %collective-permute-start.2) | collective-permute-done | bytes 720928 | tf_op jit(solution)/shard_map/ppermute | solution.py:170
  124.6 8.7 %convert_reduce_fusion = bf16[1024,1024]{1,0:T(8,128)(2,1)} fusion(f32[2,352,1024]{2,1,0:T(8,128)} %fusion.23, bf16[128,8,1024]{2,1,0:T(8,128)(2,1)S(1)} %copy-done.15, bf16[1,1024,352]{1,2,0:T(8,128)(2,1)} %bitcast.31, bf16[1,1024,352]{1,2,0:T(8,128)(2,1)} %bitcast.30, bf16[1,352,1024]{2,1,0:T(8,128)(2,1)} %bitcast.35, bf16[1,352,1024]{2,1,0:T(8,128)(2,1)} %bitcast.34), kind=kOutput, calls=%fused_computation.20 | convolution fusion | flops 2964586496 | bytes 9961472 | tf_op jit(solution)/shard_map/snf,sfd->snd/dot_general | solution.py:182
  133.3 3.6 %all-to-all-start.2 = ((bf16[4,32,8,1024]{3,2,1,0:T(8,128)(2,1)}), bf16[4,32,8,1024]{3,2,1,0:T(8,128)(2,1)S(1)}, u32[]{:S(2)}, u32[]{:S(2)}) async-start(bf16[4,32,8,1024]{3,2,1,0:T(8,128)(2,1)} %bitcast.149), calls=%async_computation.2 | async-start | bytes 4194304 | tf_op jit(solution)/shard_map/all_to_all | solution.py:186
  138.4 1.8 collective-permute-done.3
  140.2 1.2 bitcast_select_fusion.4
  141.6 2.1 collective-permute-start.4
  143.6 2.7 %collective-permute-start.5 = (bf16[2,320,256]{2,1,0:T(8,128)(2,1)S(1)}, bf16[2,320,256]{2,1,0:T(8,128)(2,1)S(1)}, u32[]{:S(2)}, u32[]{:S(2)}) collective-permute-start(bf16[2,320,256]{2,1,0:T(8,128)(2,1)S(1)} %get-tuple-element.43), channel_id=1, source_target_pairs={{0,4},{2,6},{4,0},{6,2},{1,5},{3,7},{5,1},{7,3},{8,12},{10,14},{12... | collective-permute-start | bytes 983048 | tf_op jit(solution)/shard_map/ppermute | solution.py:93
  146.3 1.5 collective-permute-start.6
  147.8 23.2 %collective-permute-done.4 = bf16[2,320,256]{2,1,0:T(8,128)(2,1)S(1)} collective-permute-done((bf16[2,320,256]{2,1,0:T(8,128)(2,1)S(1)}, bf16[2,320,256]{2,1,0:T(8,128)(2,1)S(1)}, u32[]{:S(2)}, u32[]{:S(2)}) %collective-permute-start.4) | collective-permute-done | bytes 327712 | tf_op jit(solution)/shard_map/ppermute | solution.py:93
  171.0 4.3 %collective-permute-done.5 = bf16[2,320,256]{2,1,0:T(8,128)(2,1)S(1)} collective-permute-done((bf16[2,320,256]{2,1,0:T(8,128)(2,1)S(1)}, bf16[2,320,256]{2,1,0:T(8,128)(2,1)S(1)}, u32[]{:S(2)}, u32[]{:S(2)}) %collective-permute-start.5) | collective-permute-done | bytes 327712 | tf_op jit(solution)/shard_map/ppermute | solution.py:93
  175.5 1.7 gather_fusion.1
  177.2 1.3 reduce_sum.72
  178.5 7.3 %all-to-all-start.3 = ((bf16[32,8,1024]{2,1,0:T(8,128)(2,1)}), bf16[32,8,1024]{2,1,0:T(8,128)(2,1)S(1)}, u32[]{:S(2)}, u32[]{:S(2)}) async-start(bf16[32,8,1024]{2,1,0:T(8,128)(2,1)} %reduce_sum.72), calls=%async_computation.3 | async-start | bytes 1048576 | tf_op jit(solution)/shard_map/all_to_all | solution.py:190
  188.1 1.3 gather_fusion.2
  189.8 10.9 %all-to-all-done.3 = bf16[32,8,1024]{2,1,0:T(8,128)(2,1)S(1)} async-done(((bf16[32,8,1024]{2,1,0:T(8,128)(2,1)}), bf16[32,8,1024]{2,1,0:T(8,128)(2,1)S(1)}, u32[]{:S(2)}, u32[]{:S(2)}) %all-to-all-start.3) | async-done | bytes 524320 | tf_op jit(solution)/shard_map/all_to_all | solution.py:190
  (105 shorter events, 16.0 us)
Async XLA Ops:
  7.2 180.8 %copy-start = (bf16[1024,16]{0,1:T(8,128)(2,1)S(1)}, bf16[1024,16]{0,1:T(8,128)(2,1)}, u32[]{:S(2)}) copy-start(bf16[1024,16]{0,1:T(8,128)(2,1)} %param.32) | copy-start | bytes 98308
  7.2 5.2 %copy-start.8 = (bf16[1,512,128]{2,1,0:T(8,128)(2,1)S(1)}, bf16[1,512,128]{2,1,0:T(8,128)(2,1)}, u32[]{:S(2)}) copy-start(bf16[1,512,128]{2,1,0:T(8,128)(2,1)} %param.22) | copy-start | bytes 393220
  7.2 5.4 %copy-start.11 = (bf16[1,512,128]{2,1,0:T(8,128)(2,1)S(1)}, bf16[1,512,128]{2,1,0:T(8,128)(2,1)}, u32[]{:S(2)}) copy-start(bf16[1,512,128]{2,1,0:T(8,128)(2,1)} %param.21) | copy-start | bytes 393220
  7.2 6.2 %copy-start.5 = (bf16[1,2048,128]{2,1,0:T(8,128)(2,1)S(1)}, bf16[1,2048,128]{2,1,0:T(8,128)(2,1)}, u32[]{:S(2)}) copy-start(bf16[1,2048,128]{2,1,0:T(8,128)(2,1)} %param.25) | copy-start | bytes 1572868
  7.2 36.0 %all-gather.4.cloned.1.call-start = ((), (), s32[]{:S(2)}) async-start(), calls=%async_computation.4 | async-start | bytes 2359296 | tf_op jit(solution)/shard_map/all_gather | solution.py:141
  10.2 3.4 %copy-start.9 = (bf16[1,512,128]{2,1,0:T(8,128)(2,1)S(1)}, bf16[1,512,128]{2,1,0:T(8,128)(2,1)}, u32[]{:S(2)}) copy-start(bf16[1,512,128]{2,1,0:T(8,128)(2,1)} %param.23) | copy-start | bytes 393220
  25.6 11.3 %copy-start.12 = (s32[1,64,2]{1,2,0:T(2,128)S(1)}, s32[1,64,2]{1,2,0:T(2,128)}, u32[]{:S(2)}) copy-start(s32[1,64,2]{1,2,0:T(2,128)} %param.36) | copy-start | bytes 1540
  25.6 11.8 %copy-start.14 = (s32[1,64,2]{1,2,0:T(2,128)S(1)}, s32[1,64,2]{1,2,0:T(2,128)}, u32[]{:S(2)}) copy-start(s32[1,64,2]{1,2,0:T(2,128)} %param.37) | copy-start | bytes 1540
  29.6 13.7 %copy-start.10 = (bf16[1,64,1024]{2,1,0:T(8,128)(2,1)S(1)}, bf16[1,64,1024]{2,1,0:T(8,128)(2,1)}, u32[]{:S(2)}) copy-start(bf16[1,64,1024]{2,1,0:T(8,128)(2,1)} %param.20) | copy-start | bytes 393220
  32.4 10.6 %all-to-all-start = ((bf16[8,2,4096]{2,1,0:T(2,128)(2,1)}), bf16[8,2,4096]{2,1,0:T(2,128)(2,1)S(1)}, u32[]{:S(2)}, u32[]{:S(2)}) async-start(bf16[8,2,4096]{2,1,0:T(2,128)(2,1)} %reshape.575), calls=%async_computation | async-start | bytes 262144 | tf_op jit(solution)/shard_map/all_to_all | solution.py:142
  36.9 68.3 %all-gather.6.cloned.1.call-start = ((), (), s32[]{:S(2)}) async-start(), calls=%async_computation.5 | async-start | bytes 2621440 | tf_op jit(solution)/shard_map/all_gather | solution.py:177
  43.1 3.1 %copy-start.13 = (f32[1024]{0:T(1024)S(1)}, f32[1024]{0:T(1024)}, u32[]{:S(2)}) copy-start(f32[1024]{0:T(1024)} %param.31) | copy-start | bytes 12292
  45.4 0.7 copy-start.2
  46.3 0.7 copy-start.6
  47.2 33.0 %copy-start.4 = (bf16[1,2048,128]{2,1,0:T(8,128)(2,1)S(1)}, bf16[1,2048,128]{2,1,0:T(8,128)(2,1)}, u32[]{:S(2)}) copy-start(bf16[1,2048,128]{2,1,0:T(8,128)(2,1)} %param.24) | copy-start | bytes 1572868
  76.8 19.4 %collective-permute-start = (bf16[1024,352]{0,1:T(8,128)(2,1)}, bf16[1024,352]{0,1:T(8,128)(2,1)}, u32[]{:S(2)}, u32[]{:S(2)}) collective-permute-start(bf16[1024,352]{0,1:T(8,128)(2,1)} %param.33), channel_id=1, source_target_pairs={{0,8},{8,0},{16,24},{24,16},{32,40},{40,32},{48,56},{56,48},{64,72... | collective-permute-start | bytes 2162696 | tf_op jit(solution)/shard_map/ppermute | solution.py:168
  78.0 33.6 %collective-permute-start.1 = (bf16[1024,352]{0,1:T(8,128)(2,1)}, bf16[1024,352]{0,1:T(8,128)(2,1)}, u32[]{:S(2)}, u32[]{:S(2)}) collective-permute-start(bf16[1024,352]{0,1:T(8,128)(2,1)} %param.34), channel_id=1, source_target_pairs={{0,8},{8,0},{16,24},{24,16},{32,40},{40,32},{48,56},{56,48},{64,72... | collective-permute-start | bytes 2162696 | tf_op jit(solution)/shard_map/ppermute | solution.py:169
  78.9 45.7 %collective-permute-start.2 = (bf16[352,1024]{1,0:T(8,128)(2,1)}, bf16[352,1024]{1,0:T(8,128)(2,1)}, u32[]{:S(2)}, u32[]{:S(2)}) collective-permute-start(bf16[352,1024]{1,0:T(8,128)(2,1)} %param.35), channel_id=1, source_target_pairs={{0,8},{8,0},{16,24},{24,16},{32,40},{40,32},{48,56},{56,48},{64,72... | collective-permute-start | bytes 2162696 | tf_op jit(solution)/shard_map/ppermute | solution.py:170
  105.2 19.4 %copy-start.15 = (bf16[128,8,1024]{2,1,0:T(8,128)(2,1)S(1)}, bf16[128,8,1024]{2,1,0:T(8,128)(2,1)}, u32[]{:S(2)}) copy-start(bf16[128,8,1024]{2,1,0:T(8,128)(2,1)} %all-gather.6.cloned.1.call-done) | copy-start | bytes 6291460
  133.3 43.9 %all-to-all-start.2 = ((bf16[4,32,8,1024]{3,2,1,0:T(8,128)(2,1)}), bf16[4,32,8,1024]{3,2,1,0:T(8,128)(2,1)S(1)}, u32[]{:S(2)}, u32[]{:S(2)}) async-start(bf16[4,32,8,1024]{3,2,1,0:T(8,128)(2,1)} %bitcast.149), calls=%async_computation.2 | async-start | bytes 4194304 | tf_op jit(solution)/shard_map/all_to_all | solution.py:186
  137.8 2.4 %collective-permute-start.3 = (bf16[2,4,320,128]{3,2,1,0:T(8,128)(2,1)}, bf16[2,4,320,128]{3,2,1,0:T(8,128)(2,1)}, u32[]{:S(2)}, u32[]{:S(2)}) collective-permute-start(bf16[2,4,320,128]{3,2,1,0:T(8,128)(2,1)} %dynamic-slice_bitcast_fusion), channel_id=1, source_target_pairs={{0,1},{1,0},{2,3},{3,2},{4,5},{5,4},{6,7},{7,6},{8,9},{9,8},{10,11... | collective-permute-start | bytes 1966088 | tf_op jit(solution)/shard_map/ppermute | solution.py:85
  141.6 29.4 %collective-permute-start.4 = (bf16[2,320,256]{2,1,0:T(8,128)(2,1)S(1)}, bf16[2,320,256]{2,1,0:T(8,128)(2,1)S(1)}, u32[]{:S(2)}, u32[]{:S(2)}) collective-permute-start(bf16[2,320,256]{2,1,0:T(8,128)(2,1)S(1)} %get-tuple-element.42), channel_id=1, source_target_pairs={{0,2},{2,4},{4,6},{6,0},{1,3},{3,5},{5,7},{7,1},{8,10},{10,12},{12... | collective-permute-start | bytes 983048 | tf_op jit(solution)/shard_map/ppermute | solution.py:93
  143.6 31.7 %collective-permute-start.5 = (bf16[2,320,256]{2,1,0:T(8,128)(2,1)S(1)}, bf16[2,320,256]{2,1,0:T(8,128)(2,1)S(1)}, u32[]{:S(2)}, u32[]{:S(2)}) collective-permute-start(bf16[2,320,256]{2,1,0:T(8,128)(2,1)S(1)} %get-tuple-element.43), channel_id=1, source_target_pairs={{0,4},{2,6},{4,0},{6,2},{1,5},{3,7},{5,1},{7,3},{8,12},{10,14},{12... | collective-permute-start | bytes 983048 | tf_op jit(solution)/shard_map/ppermute | solution.py:93
  146.3 29.0 %collective-permute-start.6 = (bf16[2,320,256]{2,1,0:T(8,128)(2,1)S(1)}, bf16[2,320,256]{2,1,0:T(8,128)(2,1)S(1)}, u32[]{:S(2)}, u32[]{:S(2)}) collective-permute-start(bf16[2,320,256]{2,1,0:T(8,128)(2,1)S(1)} %get-tuple-element.44), channel_id=1, source_target_pairs={{0,6},{2,0},{4,2},{6,4},{1,7},{3,1},{5,3},{7,5},{8,14},{10,8},{12,... | collective-permute-start | bytes 983048 | tf_op jit(solution)/shard_map/ppermute | solution.py:93
  177.2 8.6 %copy-start.1 = (bf16[4,2,320,256]{3,2,1,0:T(8,128)(2,1)S(1)}, bf16[4,2,320,256]{3,2,1,0:T(8,128)(2,1)}, u32[]{:S(2)}) copy-start(bf16[4,2,320,256]{3,2,1,0:T(8,128)(2,1)} %gather_fusion.1) | copy-start | bytes 3932164
  178.5 22.1 %all-to-all-start.3 = ((bf16[32,8,1024]{2,1,0:T(8,128)(2,1)}), bf16[32,8,1024]{2,1,0:T(8,128)(2,1)S(1)}, u32[]{:S(2)}, u32[]{:S(2)}) async-start(bf16[32,8,1024]{2,1,0:T(8,128)(2,1)} %reduce_sum.72), calls=%async_computation.3 | async-start | bytes 1048576 | tf_op jit(solution)/shard_map/all_to_all | solution.py:190
  186.1 1.9 copy-start.7
  201.6 1.2 copy-start.3
Sparse Core Ops, SparseCore 0:
  9.9 30.7 all-gather.3
  76.9 28.2 all-gather.5

commit v8 on v3

--- a/solution.py
+++ b/solution.py
@@ -160,21 +160,21 @@
     other_gate = lax.ppermute(expert_gate, "req", pair)
     other_up = lax.ppermute(expert_up, "req", pair)
     other_down = lax.ppermute(expert_down, "req", pair)
-    both_gate = jnp.stack([expert_gate, other_gate])
-    both_up = jnp.stack([expert_up, other_up])
-    both_down = jnp.stack([expert_down, other_down])
     step = slots_here // holders
     outgoing = buffer.reshape(experts * holders, step, width)
     arrived = lax.all_to_all(outgoing, "req", split_axis=0, concat_axis=0, tiled=True)
     gathered = lax.all_gather(arrived, "head", axis=0, tiled=False)
     flat_rows = gathered.reshape(-1, width)
-    gate_val = jnp.einsum("nd,sdf->snf", flat_rows, both_gate, preferred_element_type=jnp.float32)
-    up_val = jnp.einsum("nd,sdf->snf", flat_rows, both_up, preferred_element_type=jnp.float32)
-    hidden = (jax.nn.gelu(gate_val, approximate=True) * up_val).astype(jnp.bfloat16)
-    blocks_out = jnp.einsum(
-        "snf,sfd->snd", hidden, both_down, preferred_element_type=jnp.float32
-    ).astype(jnp.bfloat16)
-    pair_sum = jnp.sum(blocks_out.astype(jnp.float32), axis=0).astype(jnp.bfloat16)
+
+    def serve(w_gate, w_up, w_down):
+        gate_val = jnp.dot(flat_rows, w_gate, preferred_element_type=jnp.float32)
+        up_val = jnp.dot(flat_rows, w_up, preferred_element_type=jnp.float32)
+        hidden = (jax.nn.gelu(gate_val, approximate=True) * up_val).astype(jnp.bfloat16)
+        return jnp.dot(hidden, w_down, preferred_element_type=jnp.float32).astype(jnp.bfloat16)
+
+    own_out = serve(expert_gate, expert_up, expert_down)
+    other_out = serve(other_gate, other_up, other_down)
+    pair_sum = (own_out.astype(jnp.float32) + other_out.astype(jnp.float32)).astype(jnp.bfloat16)
     shard_parts = lax.all_to_all(
         pair_sum.reshape(gathered.shape), "head", split_axis=0, concat_axis=0, tiled=True
     )

time: 215 us -> 216 us (level)
  waiting for transfers between devices: 76.8 us -> 71.9 us
  matrix products: 29.5 us -> 33.9 us
    all_gather x1, waiting for transfers between devices: 12.6 us -> 21.7 us  [layer(): gathered = lax.all_gather(arrived, 'head', axis=0, tiled=False)]
    ppermute x1, waiting for transfers between devices: 8.96 us -> 0.01 us  [layer(): other_gate = lax.ppermute(expert_gate, 'req', pair)]
    dot_general x2 -> x4, matrix products: 14.2 us -> 18.6 us  [the longest x2 11.5 us: serve(): jnp.dot(hidden, w_down, preferred_element_type=jnp.float32)]
    ppermute x1, waiting for transfers between devices: 11 us -> 8.49 us  [layer(): other_down = lax.ppermute(expert_down, 'req', pair)]
    ppermute x7, waiting for transfers between devices: 24.1 us -> 21.8 us  [to_positions(): blocks.append(lax.ppermute(block, ('head', 'blk'), perm))]
    unnamed x51 -> x47, local copies, waits for them, and re-layouts: 11.4 us -> 11.4 us
  transfers between devices with their start and end apart: 15 -> 15, of which waited for: 7 -> 6; matrix products, arithmetic and copies ran while one was open for 28% -> 30% of each run, Pallas kernels for 0% -> 0%
where the time goes in v8:
time: 216 us; the launch traced here: 213 us
  waiting for transfers between devices  71.9 us (33%)
  matrix products  33.9 us (16%)
  blocking collectives  28.2 us (13%)
  starting transfers between devices  24.1 us (11%)
  local copies, waits for them, and re-layouts  21.5 us (10%)
  other arithmetic  17.6 us (8%)
  between operations  16 us (7%)
    all_to_all x1, blocking collectives, layer(): lax.all_to_all(outgoing, 'req', split_axis=0, concat_axis=0, tiled=True)  28.2 us
    ppermute x7, waiting for transfers between devices, to_positions(): blocks.append(lax.ppermute(block, ('head', 'blk'), perm))  21.8 us
    all_gather x1, waiting for transfers between devices, layer(): gathered = lax.all_gather(arrived, 'head', axis=0, tiled=False)  21.7 us
    all_to_all x1, waiting for transfers between devices, layer(): lax.all_to_all(full_sum, 'req', split_axis=0, concat_axis=0, tiled=True)  14.4 us
    dot_general x2, matrix products, serve(): jnp.dot(hidden, w_down, preferred_element_type=jnp.float32)  11.5 us
    unnamed x47, local copies, waits for them, and re-layouts  11.4 us
    sub x1, matrix products, attend_request(): weights = jnp.where(visible[None], jnp.exp(scores - highest), 0.0)  8.82 us
    ppermute x1, waiting for transfers between devices, layer(): other_down = lax.ppermute(expert_down, 'req', pair)  8.49 us
  transfers between devices with their start and end apart: 15, of which 6 were waited for; matrix products, arithmetic and copies ran while one was open for 30% of the time, Pallas kernels for 0%

profile of v8, /device:TPU:4, one launch (start us, length us, event | category | flops | bytes accessed | tf_op | source)
XLA Modules:
  0.0 213.1 jit_solution(710488349695852495)
XLA Ops:
  11.0 1.3 copy.79
  15.6 2.8 %fusion.10 = pred[512,3072]{0,1:T(8,128)(4,1)S(1)} fusion(s32[3072]{0:T(1024)S(1)} %iota_add_fusion, pred[3072]{0:T(1024)(128)(4,1)S(1)} %get-tuple-element.53, pred[3072]{0:T(1024)(128)(4,1)S(1)} %get-tuple-element.54), kind=kLoop, calls=%fused_computation.17 | loop fusion | flops 4718592 | bytes 1591296 | tf_op jit(solution)/shard_map/or | solution.py:45
  18.4 8.8 %fusion.117 = (f32[2,512]{1,0:T(2,128)S(1)}, bf16[2,512,3072]{1,2,0:T(8,128)(2,1)}) fusion(pred[512,3072]{0,1:T(8,128)(4,1)S(1)} %fusion.10, bf16[512,2,64]{0,2,1:T(8,128)(2,1)} %bitcast.173, bf16[512,2,64]{0,2,1:T(8,128)(2,1)} %bitcast.172, bf16[2048,2,64]{0,2,1:T(8,128)(2,1)S(1)} %bitcast.167, bf16[512,2,64]{0,2,1:T(8,128)(2,1)} %bitcast.170), kind=kOutput, calls=%fused_computation.172 | convolution fusion | flops 832048128 | bytes 8785920 | tf_op jit(solution)/shard_map/sub | solution.py:53
  27.3 4.1 %fusion.54 = bf16[512,2,64]{0,2,1:T(8,128)(2,1)S(1)} fusion(bf16[2,512,3072]{1,2,0:T(8,128)(2,1)} %get-tuple-element.50, bf16[512,2,64]{0,2,1:T(8,128)(2,1)} %bitcast.171, bf16[2048,2,64]{0,2,1:T(8,128)(2,1)S(1)} %bitcast.166, bf16[512,2,64]{0,2,1:T(8,128)(2,1)} %bitcast.169, f32[512,2]{0,1:T(2,128)S(1)} %bitcast.174), kind=kOutput, calls=%fused_computation.60 | convolution fusion | flops 405143552 | bytes 7213056 | tf_op jit(solution)/shard_map/hqk,khd->qhd/dot_general | solution.py:56
  32.1 1.4 reduce.3
  34.2 4.6 %all-to-all-start = ((bf16[8,2,4096]{2,1,0:T(2,128)(2,1)}), bf16[8,2,4096]{2,1,0:T(2,128)(2,1)S(1)}, u32[]{:S(2)}, u32[]{:S(2)}) async-start(bf16[8,2,4096]{2,1,0:T(2,128)(2,1)} %reshape.574), calls=%async_computation | async-start | bytes 262144 | tf_op jit(solution)/shard_map/all_to_all | solution.py:134
  40.1 4.8 %all-to-all-done = bf16[8,2,4096]{2,1,0:T(2,128)(2,1)S(1)} async-done(((bf16[8,2,4096]{2,1,0:T(2,128)(2,1)}), bf16[8,2,4096]{2,1,0:T(2,128)(2,1)S(1)}, u32[]{:S(2)}, u32[]{:S(2)}) %all-to-all-start) | async-done | bytes 131104 | tf_op jit(solution)/shard_map/all_to_all | solution.py:134
  45.2 2.2 %multiply_reduce_fusion.1 = (f32[64]{0:T(128)S(1)}, f32[1,64,1024]{2,1,0:T(8,128)S(1)}) fusion(bf16[1024,1024]{1,0:T(8,128)(2,1)} %all-gather.4.cloned.1.call-done, bf16[8,8,8,128]{3,2,1,0:T(8,128)(2,1)S(1)} %bitcast.164, bf16[1,64,1024]{2,1,0:T(8,128)(2,1)S(1)} %copy-done.9), kind=kOutput, calls=%fused_computation.93 | convolution fusion | flops 134479808 | bytes 2621696 | tf_op jit(solution)/shard_map/rqf,fd->rqd/dot_general | solution.py:135
  49.1 1.4 scatter_custom_fusion
  50.5 28.2 %all_to_all.30 = bf16[32,8,1024]{2,1,0:T(8,128)(2,1)} all-to-all(bf16[32,8,1024]{2,1,0:T(8,128)(2,1)S(1)} %bitcast.161), channel_id=1, replica_groups=mesh['req'=32,'head'=4,'blk'=2] {'req'}, dimensions={0} | all-to-all | bytes 1048576 | tf_op jit(solution)/shard_map/all_to_all | solution.py:165
  78.9 5.8 %fusion.79 = (bf16[1,2560,128]{2,1,0:T(8,128)(2,1)S(1)}, bf16[1,2560,128]{2,1,0:T(8,128)(2,1)S(1)}) fusion(s32[]{:T(128)} %bitcast.31, bf16[1,2048,128]{2,1,0:T(8,128)(2,1)S(1)} %broadcast.394, bf16[1,512,128]{2,1,0:T(8,128)(2,1)S(1)} %copy-done.7, bf16[1,2048,128]{2,1,0:T(8,128)(2,1)S(1)} %copy-done.3, pred[2560]{0:T(1024)(128)(4,1)S(1)} %iota_compare_fusion.4, ...), kind=kLoop, calls=%fused_computation.79 | loop fusion | flops 4587520 | bytes 3148292 | tf_op jit(solution)/shard_map/vmap(jit(_where))/select_n | solution.py:72
  86.5 1.4 collective-permute-start.5
  87.9 2.7 %collective-permute-start.6 = (bf16[2,320,128]{2,1,0:T(8,128)(2,1)}, bf16[2,320,128]{2,1,0:T(8,128)(2,1)}, u32[]{:S(2)}, u32[]{:S(2)}) collective-permute-start(bf16[2,320,128]{2,1,0:T(8,128)(2,1)} %get-tuple-element.42), channel_id=1, source_target_pairs={{0,4},{1,5},{2,6},{3,7},{4,0},{5,1},{6,2},{7,3},{8,12},{9,13},{10,... | collective-permute-start | bytes 491528 | tf_op jit(solution)/shard_map/ppermute | solution.py:85
  90.5 1.2 collective-permute-start.1
  92.4 4.1 %collective-permute-done.3 = bf16[2,320,128]{2,1,0:T(8,128)(2,1)S(1)} collective-permute-done((bf16[2,320,128]{2,1,0:T(8,128)(2,1)S(1)}, bf16[2,320,128]{2,1,0:T(8,128)(2,1)S(1)}, u32[]{:S(2)}, u32[]{:S(2)}) %collective-permute-start.3) | collective-permute-done | bytes 163872 | tf_op jit(solution)/shard_map/ppermute | solution.py:85
  97.7 21.7 %all-gather.6.cloned.1.call-done = bf16[128,8,1024]{2,1,0:T(8,128)(2,1)} async-done(((bf16[32,8,1024]{2,1,0:T(8,128)(2,1)}), bf16[128,8,1024]{2,1,0:T(8,128)(2,1)}) %all-gather.6.cloned.1.call-update) | async-done | bytes 2097168 | tf_op jit(solution)/shard_map/all_gather | solution.py:166
  119.3 3.9 %fusion.18 = f32[1024,352]{0,1:T(8,128)} fusion(bf16[1024,352]{0,1:T(8,128)(2,1)} %param.33, bf16[128,8,1024]{2,1,0:T(8,128)(2,1)} %all-gather.6.cloned.1.call-done), kind=kOutput, calls=%fused_computation.28 | convolution fusion | flops 738197504 | bytes 4259840 | tf_op jit(solution)/shard_map/dot_general | solution.py:170
  123.3 1.2 collective-permute-start.2
  124.5 3.2 %fusion.12 = f32[1024,352]{0,1:T(8,128)} fusion(bf16[1024,352]{0,1:T(8,128)(2,1)} %collective-permute-done.1, bf16[128,8,1024]{2,1,0:T(8,128)(2,1)S(1)} %copy-done.14), kind=kOutput, calls=%fused_computation.22 | convolution fusion | flops 738197504 | bytes 4259840 | tf_op jit(solution)/shard_map/dot_general | solution.py:171
  127.7 5.4 %fusion.45 = bf16[1024,1024]{1,0:T(8,128)(2,1)} fusion(bf16[352,1024]{1,0:T(8,128)(2,1)} %param.35, bf16[1024,352]{0,1:T(8,128)(2,1)} %param.34, bf16[128,8,1024]{2,1,0:T(8,128)(2,1)S(1)} %copy-done.14, f32[1024,352]{0,1:T(8,128)} %fusion.18), kind=kOutput, calls=%fused_computation.49 | convolution fusion | flops 1479999488 | bytes 7077888 | tf_op jit(solution)/shard_map/dot_general | solution.py:173
  133.0 8.5 %collective-permute-done.2 = bf16[352,1024]{1,0:T(8,128)(2,1)} collective-permute-done((bf16[352,1024]{1,0:T(8,128)(2,1)}, bf16[352,1024]{1,0:T(8,128)(2,1)}, u32[]{:S(2)}, u32[]{:S(2)}) %collective-permute-start.2) | collective-permute-done | bytes 720928 | tf_op jit(solution)/shard_map/ppermute | solution.py:162
  141.8 6.1 %add_convert_fusion = bf16[1024,1024]{1,0:T(8,128)(2,1)} fusion(bf16[1024,1024]{1,0:T(8,128)(2,1)} %fusion.45, bf16[352,1024]{1,0:T(8,128)(2,1)} %collective-permute-done.2, f32[1024,352]{0,1:T(8,128)} %fusion.12, bf16[1024,352]{0,1:T(8,128)(2,1)} %collective-permute-done, bf16[128,8,1024]{2,1,0:T(8,128)(2,1)S(1)} %copy-done.14), kind=kOutput, calls=%fused_computation.19 | convolution fusion | flops 1485242368 | bytes 9175040 | tf_op jit(solution)/shard_map/dot_general | solution.py:173
  147.9 3.6 %all-to-all-start.2 = ((bf16[4,32,8,1024]{3,2,1,0:T(8,128)(2,1)}), bf16[4,32,8,1024]{3,2,1,0:T(8,128)(2,1)S(1)}, u32[]{:S(2)}, u32[]{:S(2)}) async-start(bf16[4,32,8,1024]{3,2,1,0:T(8,128)(2,1)} %bitcast.160), calls=%async_computation.2 | async-start | bytes 4194304 | tf_op jit(solution)/shard_map/all_to_all | solution.py:178
  151.6 1.4 collective-permute-start.9
  157.7 17.7 %collective-permute-done.9 = bf16[2,320,128]{2,1,0:T(8,128)(2,1)S(1)} collective-permute-done((bf16[2,320,128]{2,1,0:T(8,128)(2,1)}, bf16[2,320,128]{2,1,0:T(8,128)(2,1)S(1)}, u32[]{:S(2)}, u32[]{:S(2)}) %collective-permute-start.9) | collective-permute-done | bytes 163872 | tf_op jit(solution)/shard_map/ppermute | solution.py:85
  175.4 1.8 gather_fusion.1
  177.2 1.5 select_bitcast_fusion
  178.7 1.3 reduce_sum.59
  180.0 6.0 %all-to-all-start.3 = ((bf16[32,8,1024]{2,1,0:T(8,128)(2,1)}), bf16[32,8,1024]{2,1,0:T(8,128)(2,1)S(1)}, u32[]{:S(2)}, u32[]{:S(2)}) async-start(bf16[32,8,1024]{2,1,0:T(8,128)(2,1)} %reduce_sum.59), calls=%async_computation.3 | async-start | bytes 1048576 | tf_op jit(solution)/shard_map/all_to_all | solution.py:182
  186.1 1.3 copy_bitcast_fusion
  187.5 1.3 gather_fusion.2
  189.2 14.4 %all-to-all-done.3 = bf16[32,8,1024]{2,1,0:T(8,128)(2,1)S(1)} async-done(((bf16[32,8,1024]{2,1,0:T(8,128)(2,1)}), bf16[32,8,1024]{2,1,0:T(8,128)(2,1)S(1)}, u32[]{:S(2)}, u32[]{:S(2)}) %all-to-all-start.3) | async-done | bytes 524320 | tf_op jit(solution)/shard_map/all_to_all | solution.py:182
  (114 shorter events, 22.3 us)
Async XLA Ops:
  7.2 180.2 %copy-start = (bf16[1024,16]{0,1:T(8,128)(2,1)S(1)}, bf16[1024,16]{0,1:T(8,128)(2,1)}, u32[]{:S(2)}) copy-start(bf16[1024,16]{0,1:T(8,128)(2,1)} %param.32) | copy-start | bytes 98308
  7.2 5.1 %copy-start.7 = (bf16[1,512,128]{2,1,0:T(8,128)(2,1)S(1)}, bf16[1,512,128]{2,1,0:T(8,128)(2,1)}, u32[]{:S(2)}) copy-start(bf16[1,512,128]{2,1,0:T(8,128)(2,1)} %param.22) | copy-start | bytes 393220
  7.2 5.9 %copy-start.10 = (bf16[1,512,128]{2,1,0:T(8,128)(2,1)S(1)}, bf16[1,512,128]{2,1,0:T(8,128)(2,1)}, u32[]{:S(2)}) copy-start(bf16[1,512,128]{2,1,0:T(8,128)(2,1)} %param.21) | copy-start | bytes 393220
  7.2 7.4 %copy-start.4 = (bf16[1,2048,128]{2,1,0:T(8,128)(2,1)S(1)}, bf16[1,2048,128]{2,1,0:T(8,128)(2,1)}, u32[]{:S(2)}) copy-start(bf16[1,2048,128]{2,1,0:T(8,128)(2,1)} %param.25) | copy-start | bytes 1572868
  7.2 38.0 %all-gather.4.cloned.1.call-start = ((), (), s32[]{:S(2)}) async-start(), calls=%async_computation.4 | async-start | bytes 2359296 | tf_op jit(solution)/shard_map/all_gather | solution.py:133
  11.0 3.8 %copy-start.8 = (bf16[1,512,128]{2,1,0:T(8,128)(2,1)S(1)}, bf16[1,512,128]{2,1,0:T(8,128)(2,1)}, u32[]{:S(2)}) copy-start(bf16[1,512,128]{2,1,0:T(8,128)(2,1)} %param.23) | copy-start | bytes 393220
  27.3 11.6 %copy-start.11 = (s32[1,64,2]{1,2,0:T(2,128)S(1)}, s32[1,64,2]{1,2,0:T(2,128)}, u32[]{:S(2)}) copy-start(s32[1,64,2]{1,2,0:T(2,128)} %param.36) | copy-start | bytes 1540
  31.4 7.9 %copy-start.13 = (s32[1,64,2]{1,2,0:T(2,128)S(1)}, s32[1,64,2]{1,2,0:T(2,128)}, u32[]{:S(2)}) copy-start(s32[1,64,2]{1,2,0:T(2,128)} %param.37) | copy-start | bytes 1540
  31.4 13.8 %copy-start.9 = (bf16[1,64,1024]{2,1,0:T(8,128)(2,1)S(1)}, bf16[1,64,1024]{2,1,0:T(8,128)(2,1)}, u32[]{:S(2)}) copy-start(bf16[1,64,1024]{2,1,0:T(8,128)(2,1)} %param.20) | copy-start | bytes 393220
  34.2 10.7 %all-to-all-start = ((bf16[8,2,4096]{2,1,0:T(2,128)(2,1)}), bf16[8,2,4096]{2,1,0:T(2,128)(2,1)S(1)}, u32[]{:S(2)}, u32[]{:S(2)}) async-start(bf16[8,2,4096]{2,1,0:T(2,128)(2,1)} %reshape.574), calls=%async_computation | async-start | bytes 262144 | tf_op jit(solution)/shard_map/all_to_all | solution.py:134
  38.8 80.6 %all-gather.6.cloned.1.call-start = ((), (), s32[]{:S(2)}) async-start(), calls=%async_computation.5 | async-start | bytes 2621440 | tf_op jit(solution)/shard_map/all_gather | solution.py:166
  45.0 3.0 %copy-start.12 = (f32[1024]{0:T(1024)S(1)}, f32[1024]{0:T(1024)}, u32[]{:S(2)}) copy-start(f32[1024]{0:T(1024)} %param.31) | copy-start | bytes 12292
  47.4 0.7 copy-start.1
  48.2 0.7 copy-start.5
  49.1 29.8 %copy-start.3 = (bf16[1,2048,128]{2,1,0:T(8,128)(2,1)S(1)}, bf16[1,2048,128]{2,1,0:T(8,128)(2,1)}, u32[]{:S(2)}) copy-start(bf16[1,2048,128]{2,1,0:T(8,128)(2,1)} %param.24) | copy-start | bytes 1572868
  85.8 10.7 %collective-permute-start.3 = (bf16[2,320,128]{2,1,0:T(8,128)(2,1)S(1)}, bf16[2,320,128]{2,1,0:T(8,128)(2,1)S(1)}, u32[]{:S(2)}, u32[]{:S(2)}) collective-permute-start(bf16[2,320,128]{2,1,0:T(8,128)(2,1)S(1)} %get-tuple-element.45), channel_id=1, source_target_pairs={{0,1},{1,2},{2,3},{3,4},{4,5},{5,6},{6,7},{7,0},{8,9},{9,10},{10,1... | collective-permute-start | bytes 491528 | tf_op jit(solution)/shard_map/ppermute | solution.py:85
  85.8 65.7 %collective-permute-start.4 = (bf16[2,320,128]{2,1,0:T(8,128)(2,1)}, bf16[2,320,128]{2,1,0:T(8,128)(2,1)}, u32[]{:S(2)}, u32[]{:S(2)}) collective-permute-start(bf16[2,320,128]{2,1,0:T(8,128)(2,1)} %get-tuple-element.44), channel_id=1, source_target_pairs={{0,2},{1,3},{2,4},{3,5},{4,6},{5,7},{6,0},{7,1},{8,10},{9,11},{10,... | collective-permute-start | bytes 491528 | tf_op jit(solution)/shard_map/ppermute | solution.py:85
  86.5 67.4 %collective-permute-start.5 = (bf16[2,320,128]{2,1,0:T(8,128)(2,1)}, bf16[2,320,128]{2,1,0:T(8,128)(2,1)}, u32[]{:S(2)}, u32[]{:S(2)}) collective-permute-start(bf16[2,320,128]{2,1,0:T(8,128)(2,1)} %get-tuple-element.43), channel_id=1, source_target_pairs={{0,3},{1,4},{2,5},{3,6},{4,7},{5,0},{6,1},{7,2},{8,11},{9,12},{10,... | collective-permute-start | bytes 491528 | tf_op jit(solution)/shard_map/ppermute | solution.py:85
  87.9 67.0 %collective-permute-start.6 = (bf16[2,320,128]{2,1,0:T(8,128)(2,1)}, bf16[2,320,128]{2,1,0:T(8,128)(2,1)}, u32[]{:S(2)}, u32[]{:S(2)}) collective-permute-start(bf16[2,320,128]{2,1,0:T(8,128)(2,1)} %get-tuple-element.42), channel_id=1, source_target_pairs={{0,4},{1,5},{2,6},{3,7},{4,0},{5,1},{6,2},{7,3},{8,12},{9,13},{10,... | collective-permute-start | bytes 491528 | tf_op jit(solution)/shard_map/ppermute | solution.py:85
  90.5 32.8 %collective-permute-start.1 = (bf16[1024,352]{0,1:T(8,128)(2,1)}, bf16[1024,352]{0,1:T(8,128)(2,1)}, u32[]{:S(2)}, u32[]{:S(2)}) collective-permute-start(bf16[1024,352]{0,1:T(8,128)(2,1)} %param.34), channel_id=1, source_target_pairs={{0,8},{8,0},{16,24},{24,16},{32,40},{40,32},{48,56},{56,48},{64,72... | collective-permute-start | bytes 2162696 | tf_op jit(solution)/shard_map/ppermute | solution.py:161
  96.5 36.5 %collective-permute-start = (bf16[1024,352]{0,1:T(8,128)(2,1)}, bf16[1024,352]{0,1:T(8,128)(2,1)}, u32[]{:S(2)}, u32[]{:S(2)}) collective-permute-start(bf16[1024,352]{0,1:T(8,128)(2,1)} %param.33), channel_id=1, source_target_pairs={{0,8},{8,0},{16,24},{24,16},{32,40},{40,32},{48,56},{56,48},{64,72... | collective-permute-start | bytes 2162696 | tf_op jit(solution)/shard_map/ppermute | solution.py:160
  119.3 5.1 %copy-start.14 = (bf16[128,8,1024]{2,1,0:T(8,128)(2,1)S(1)}, bf16[128,8,1024]{2,1,0:T(8,128)(2,1)}, u32[]{:S(2)}) copy-start(bf16[128,8,1024]{2,1,0:T(8,128)(2,1)} %all-gather.6.cloned.1.call-done) | copy-start | bytes 6291460
  123.3 18.2 %collective-permute-start.2 = (bf16[352,1024]{1,0:T(8,128)(2,1)}, bf16[352,1024]{1,0:T(8,128)(2,1)}, u32[]{:S(2)}, u32[]{:S(2)}) collective-permute-start(bf16[352,1024]{1,0:T(8,128)(2,1)} %param.35), channel_id=1, source_target_pairs={{0,8},{8,0},{16,24},{24,16},{32,40},{40,32},{48,56},{56,48},{64,72... | collective-permute-start | bytes 2162696 | tf_op jit(solution)/shard_map/ppermute | solution.py:162
  133.0 22.8 %collective-permute-start.7 = (bf16[2,320,128]{2,1,0:T(8,128)(2,1)}, bf16[2,320,128]{2,1,0:T(8,128)(2,1)}, u32[]{:S(2)}, u32[]{:S(2)}) collective-permute-start(bf16[2,320,128]{2,1,0:T(8,128)(2,1)} %get-tuple-element.41), channel_id=1, source_target_pairs={{0,5},{1,6},{2,7},{3,0},{4,1},{5,2},{6,3},{7,4},{8,13},{9,14},{10,... | collective-permute-start | bytes 491528 | tf_op jit(solution)/shard_map/ppermute | solution.py:85
  141.5 15.2 %collective-permute-start.8 = (bf16[2,320,128]{2,1,0:T(8,128)(2,1)}, bf16[2,320,128]{2,1,0:T(8,128)(2,1)}, u32[]{:S(2)}, u32[]{:S(2)}) collective-permute-start(bf16[2,320,128]{2,1,0:T(8,128)(2,1)} %get-tuple-element.40), channel_id=1, source_target_pairs={{0,6},{1,7},{2,0},{3,1},{4,2},{5,3},{6,4},{7,5},{8,14},{9,15},{10,... | collective-permute-start | bytes 491528 | tf_op jit(solution)/shard_map/ppermute | solution.py:85
  147.9 30.7 %all-to-all-start.2 = ((bf16[4,32,8,1024]{3,2,1,0:T(8,128)(2,1)}), bf16[4,32,8,1024]{3,2,1,0:T(8,128)(2,1)S(1)}, u32[]{:S(2)}, u32[]{:S(2)}) async-start(bf16[4,32,8,1024]{3,2,1,0:T(8,128)(2,1)} %bitcast.160), calls=%async_computation.2 | async-start | bytes 4194304 | tf_op jit(solution)/shard_map/all_to_all | solution.py:178
  151.6 23.8 %collective-permute-start.9 = (bf16[2,320,128]{2,1,0:T(8,128)(2,1)}, bf16[2,320,128]{2,1,0:T(8,128)(2,1)S(1)}, u32[]{:S(2)}, u32[]{:S(2)}) collective-permute-start(bf16[2,320,128]{2,1,0:T(8,128)(2,1)} %get-tuple-element.39), channel_id=1, source_target_pairs={{0,7},{1,0},{2,1},{3,2},{4,3},{5,4},{6,5},{7,6},{8,15},{9,8},{10,9... | collective-permute-start | bytes 491528 | tf_op jit(solution)/shard_map/ppermute | solution.py:85
  180.0 23.5 %all-to-all-start.3 = ((bf16[32,8,1024]{2,1,0:T(8,128)(2,1)}), bf16[32,8,1024]{2,1,0:T(8,128)(2,1)S(1)}, u32[]{:S(2)}, u32[]{:S(2)}) async-start(bf16[32,8,1024]{2,1,0:T(8,128)(2,1)} %reduce_sum.59), calls=%async_computation.3 | async-start | bytes 1048576 | tf_op jit(solution)/shard_map/all_to_all | solution.py:182
  186.1 1.3 copy-start.6
  204.5 1.2 copy-start.2
Sparse Core Ops, SparseCore 0:
  9.9 30.8 all-gather.3
  78.8 40.5 all-gather.5
